TPU v7x, 1024 devices: a whole 4x4x32 slice. The times are simulated.
1024 devices in a mesh: seq: 64 (over z, core), tp: 16 (over x, y).
Axes of the slice: x: 4, y: 4, z: 32, core: 2. Of those that a mesh axis runs over, the one named last changes fastest.
Arguments:
- lin_query: bfloat16 [8192, 4096], P('seq', 'tp'), may hold values from -23 to 23
- lin_key: bfloat16 [8192, 4096], P('seq', 'tp'), may hold values from -0.5 to 0.5
- lin_value: bfloat16 [8192, 4096], P('seq', 'tp'), may hold values from -6 to 6
- decay_rate: float32 [32], P('tp'), may hold values from 0 to 1
- norm_gain: float32 [4096], P('tp'), may hold values from 0.1 to 1.9
- lin_grad: bfloat16 [8192, 4096], P('seq', 'tp'), may hold values from -6 to 6
- soft_query: bfloat16 [8192, 4096], P('seq', 'tp'), may hold values from -5 to 5
- soft_key: bfloat16 [8192, 4096], P('seq', 'tp'), may hold values from -5 to 5
- soft_value: bfloat16 [8192, 4096], P('seq', 'tp'), may hold values from -6 to 6
- soft_grad: bfloat16 [8192, 4096], P('seq', 'tp'), may hold values from -6 to 6
- segments: int32 [64], replicated, may hold values from 0 to 21, never falling along the last dimension, each value on 1 to 6 neighbouring positions
Outputs:
- lin_query_grad: bfloat16 [8192, 4096], P('seq', 'tp')
- lin_key_grad: bfloat16 [8192, 4096], P('seq', 'tp')
- lin_value_grad: bfloat16 [8192, 4096], P('seq', 'tp')
- soft_query_grad: bfloat16 [8192, 4096], P('seq', 'tp')
- soft_key_grad: bfloat16 [8192, 4096], P('seq', 'tp')
- soft_value_grad: bfloat16 [8192, 4096], P('seq', 'tp')
Inputs may be any that keep to these rules, and one draw needn't show every extreme that they name: `segments`: block labels never fall, start at 0, and one label covers at most 6 blocks.
All inputs are finite; a program needn't handle non-finite values.
Results may differ from a plain program's by a relative error of at most 0.013.
Values may be sent and summed in bfloat16 or wider, within the bound.
No kernel may reach another device: no remote copies, remote signals or barrier semaphores. Data moves between devices by JAX's collectives and lax.ppermute only.
A program may use at most 64 MiB of HBM per device.

v0:
```python
import math

import jax
import jax.numpy as jnp
from jax import lax
from jax.sharding import PartitionSpec as P

HD = 128
BLK = 128
REACH = 6


HIGH_PRECISION = lax.Precision.HIGHEST
NORM_EPS = 1e-06


def carried_in(shard, axis, combine, identity, reverse):
    count, here = (lax.axis_size(axis), lax.axis_index(axis))
    everything = jax.tree.map(
        lambda part, kind: lax.all_gather(part.astype(kind), axis),
        shard,
        (jnp.bfloat16, jnp.bfloat16),
    )
    start = jax.tree.map(
        lambda part, zero: jnp.broadcast_to(jnp.asarray(zero, part.dtype), part.shape),
        shard,
        identity,
    )

    def hop(k, before):
        at = count - 1 - k if reverse else k
        reached = at > here if reverse else at < here
        new = combine(
            before, jax.tree.map(lambda part, own: part[at].astype(own.dtype), everything, shard)
        )
        return jax.tree.map(lambda a, b: jnp.where(reached, a, b), new, before)

    return lax.fori_loop(0, count, hop, start)


def shifted(value, axis, steps):
    count = lax.axis_size(axis)
    first, last = (max(0, -steps), min(count, count - steps))
    return lax.ppermute(value, axis, [(source, source + steps) for source in range(first, last)])


def as_float(array):
    return array.astype(jnp.float32)


def decay_matrix(labels, decay_rate):
    place = jnp.arange(labels.shape[0], dtype=jnp.int32)
    distance = as_float(place[:, None] - place[None, :])
    visible = (labels[:, None] == labels[None, :]) & (distance >= 0)
    return jnp.where(
        visible[None], jnp.exp(-decay_rate[:, None, None] * jnp.maximum(distance, 0.0)[None]), 0.0
    )


def entry_weights(labels, decay_rate):
    place = as_float(jnp.arange(labels.shape[0], dtype=jnp.int32))
    return jnp.where(
        (labels == labels[0])[None, :], jnp.exp(-decay_rate[:, None] * place[None, :]), 0.0
    )


def exit_weights(labels, decay_rate):
    count = labels.shape[0]
    place = as_float(jnp.arange(count, dtype=jnp.int32))
    return jnp.where(
        (labels == labels[-1])[None, :],
        jnp.exp(-decay_rate[:, None] * (count - 1 - place)[None, :]),
        0.0,
    )


def forward_element(keys, values, labels, next_label, decay_rate):
    count = labels.shape[0]
    place = as_float(jnp.arange(count, dtype=jnp.int32))
    link = labels[-1] == next_label
    weight = jnp.where(
        (labels == labels[-1])[None, :] & link,
        jnp.exp(-decay_rate[:, None] * (count - place)[None, :]),
        0.0,
    )
    summary = jnp.einsum(
        "thd,the->hde",
        as_float(keys) * weight.T[:, :, None],
        as_float(values),
        precision=HIGH_PRECISION,
    )
    factor = jnp.where(labels[0] == next_label, jnp.exp(-decay_rate * count), 0.0)
    return (factor, summary)


def backward_element(queries, grads, labels, prev_label, decay_rate):
    count = labels.shape[0]
    place = as_float(jnp.arange(count, dtype=jnp.int32))
    link = labels[0] == prev_label
    weight = jnp.where(
        (labels == labels[0])[None, :] & link,
        jnp.exp(-decay_rate[:, None] * (place + 1.0)[None, :]),
        0.0,
    )
    summary = jnp.einsum(
        "thd,the->hde",
        as_float(queries) * weight.T[:, :, None],
        as_float(grads),
        precision=HIGH_PRECISION,
    )
    factor = jnp.where(link & (labels[0] == labels[-1]), jnp.exp(-decay_rate * count), 0.0)
    return (factor, summary)


def affine(earlier, later):
    return (earlier[0] * later[0], later[0][:, None, None] * earlier[1] + later[1])


def score_grads(probs, grads, value_part, delta):
    grad_probs = jnp.einsum("thd,uhd->htu", grads, value_part, preferred_element_type=jnp.float32)
    return (probs * (grad_probs - delta.T[:, :, None])).astype(jnp.bfloat16)


def body(
    lin_query,
    lin_key,
    lin_value,
    decay_rate,
    norm_gain,
    lin_grad,
    soft_query,
    soft_key,
    soft_value,
    soft_grad,
    segments,
):
    tokens = lin_query.shape[0]
    heads = lin_query.shape[1] // HD
    scale = 1.0 / math.sqrt(HD)
    device = lax.axis_index("seq")
    blocks_each = tokens // BLK
    pad_blocks = REACH * blocks_each
    padded = jnp.concatenate(
        [jnp.full((pad_blocks,), -1, jnp.int32), segments, jnp.full((pad_blocks,), -2, jnp.int32)]
    )
    window_blocks = lax.dynamic_slice_in_dim(
        padded, device * blocks_each, (2 * REACH + 1) * blocks_each
    )
    window_labels = jnp.repeat(window_blocks, BLK, total_repeat_length=(2 * REACH + 1) * tokens)
    own_labels = window_labels[REACH * tokens : (REACH + 1) * tokens]
    prev_label = window_labels[REACH * tokens - 1]
    next_label = window_labels[(REACH + 1) * tokens]
    key_labels = window_labels[tokens : (REACH + 1) * tokens]

    def split_heads(array):
        return array.reshape(tokens, heads, HD)

    queries = split_heads(lin_query)
    keys = split_heads(lin_key)
    values = split_heads(lin_value)
    soft_queries = split_heads(soft_query)
    soft_keys = split_heads(soft_key)
    soft_values = split_heads(soft_value)
    soft_grads = split_heads(soft_grad)
    factor, summary = forward_element(keys, values, own_labels, next_label, decay_rate)
    received = []
    state_in = carried_in(
        (factor, summary), "seq", affine, (jnp.ones_like(factor), jnp.zeros_like(summary)), False
    )[1]
    for back in range(1, REACH):
        received.append(shifted((soft_keys, soft_values), "seq", back))
    decay = decay_matrix(own_labels, decay_rate)
    scores = jnp.einsum("thd,shd->hts", queries, keys, preferred_element_type=jnp.float32)
    weights = (decay * scores).astype(jnp.bfloat16)
    entry = entry_weights(own_labels, decay_rate)
    leave = exit_weights(own_labels, decay_rate)
    inner = jnp.einsum("hts,shd->thd", weights, values, preferred_element_type=jnp.float32)
    carried = jnp.einsum("thd,hde->the", as_float(queries), state_in, precision=HIGH_PRECISION)
    lin_out = inner + carried * entry.T[:, :, None]
    flat = lin_out.reshape(tokens, heads * HD)
    scaled_grad = norm_gain[None, :] * as_float(lin_grad)
    sums = lax.psum((jnp.sum(flat * flat, axis=1), jnp.sum(flat * scaled_grad, axis=1)), "tp")
    width = lax.axis_size("tp") * heads * HD
    inverse = lax.rsqrt(sums[0] / width + NORM_EPS)
    cross = sums[1] / width
    norm_grad = (inverse[:, None] * scaled_grad - flat * (inverse**3 * cross)[:, None]).astype(
        jnp.bfloat16
    )
    grad_heads = split_heads(norm_grad)
    back_factor, back_summary = backward_element(
        queries, grad_heads, own_labels, prev_label, decay_rate
    )
    reverse_in = carried_in(
        (back_factor, back_summary),
        "seq",
        affine,
        (jnp.ones_like(back_factor), jnp.zeros_like(back_summary)),
        True,
    )[1]
    grad_scores_lin = jnp.einsum(
        "thd,shd->hts", grad_heads, values, preferred_element_type=jnp.float32
    )
    grad_weights = (decay * grad_scores_lin).astype(jnp.bfloat16)
    lin_query_grad = jnp.einsum(
        "hts,shd->thd", grad_weights, keys, preferred_element_type=jnp.float32
    )
    lin_query_grad = (
        lin_query_grad
        + jnp.einsum("the,hde->thd", as_float(grad_heads), state_in, precision=HIGH_PRECISION)
        * entry.T[:, :, None]
    )
    lin_key_grad = jnp.einsum(
        "hts,thd->shd", grad_weights, queries, preferred_element_type=jnp.float32
    )
    lin_key_grad = (
        lin_key_grad
        + jnp.einsum("she,hde->shd", as_float(values), reverse_in, precision=HIGH_PRECISION)
        * leave.T[:, :, None]
    )
    lin_value_grad = jnp.einsum(
        "hts,the->she", weights, grad_heads, preferred_element_type=jnp.float32
    )
    lin_value_grad = (
        lin_value_grad
        + jnp.einsum("shd,hde->she", as_float(keys), reverse_in, precision=HIGH_PRECISION)
        * leave.T[:, :, None]
    )
    key_window = jnp.concatenate(
        [received[back - 1][0] for back in range(REACH - 1, 0, -1)] + [soft_keys], 0
    )
    value_window = jnp.concatenate(
        [received[back - 1][1] for back in range(REACH - 1, 0, -1)] + [soft_values], 0
    )
    query_place = jnp.arange(tokens, dtype=jnp.int32)
    key_place = jnp.arange(REACH * tokens, dtype=jnp.int32) - (REACH - 1) * tokens
    visible = (key_labels[None, :] == own_labels[:, None]) & (
        key_place[None, :] <= query_place[:, None]
    )
    soft_scores = (
        jnp.einsum("thd,uhd->htu", soft_queries, key_window, preferred_element_type=jnp.float32)
        * scale
    )
    soft_scores = jnp.where(visible[None], soft_scores, -jnp.inf)
    top = jnp.max(soft_scores, axis=-1)
    expo = jnp.exp(soft_scores - top[..., None])
    total = jnp.sum(expo, axis=-1)
    probs = expo / total[..., None]
    probs_half = probs.astype(jnp.bfloat16)
    attended = jnp.einsum(
        "htu,uhd->thd", probs_half, value_window, preferred_element_type=jnp.float32
    )
    delta = jnp.sum(as_float(soft_grads) * attended, axis=-1)
    grad_scores = score_grads(probs, soft_grads, value_window, delta)
    soft_query_grad = (
        jnp.einsum("htu,uhd->thd", grad_scores, key_window, preferred_element_type=jnp.float32)
        * scale
    )
    key_terms = (
        jnp.einsum("htu,thd->uhd", grad_scores, soft_queries, preferred_element_type=jnp.float32)
        * scale
    )
    value_terms = jnp.einsum(
        "htu,thd->uhd", probs_half, soft_grads, preferred_element_type=jnp.float32
    )
    soft_key_grad = key_terms[(REACH - 1) * tokens :]
    soft_value_grad = value_terms[(REACH - 1) * tokens :]
    for back in range(1, REACH):
        lower = (REACH - 1 - back) * tokens
        got_key, got_value = (
            shifted(key_terms[lower : lower + tokens].astype(jnp.bfloat16), "seq", -back).astype(
                jnp.float32
            ),
            shifted(value_terms[lower : lower + tokens].astype(jnp.bfloat16), "seq", -back).astype(
                jnp.float32
            ),
        )
        soft_key_grad = soft_key_grad + got_key
        soft_value_grad = soft_value_grad + got_value

    def merge_heads(array):
        return array.reshape(tokens, heads * HD).astype(jnp.bfloat16)

    return (
        merge_heads(lin_query_grad),
        merge_heads(lin_key_grad),
        merge_heads(lin_value_grad),
        merge_heads(soft_query_grad),
        merge_heads(soft_key_grad),
        merge_heads(soft_value_grad),
    )


def solution(mesh):
    return jax.shard_map(
        body,
        mesh=mesh,
        in_specs=(
            P("seq", "tp"),
            P("seq", "tp"),
            P("seq", "tp"),
            P("tp"),
            P("tp"),
            P("seq", "tp"),
            P("seq", "tp"),
            P("seq", "tp"),
            P("seq", "tp"),
            P("seq", "tp"),
            P(),
        ),
        out_specs=(
            P("seq", "tp"),
            P("seq", "tp"),
            P("seq", "tp"),
            P("seq", "tp"),
            P("seq", "tp"),
            P("seq", "tp"),
        ),
        check_vma=False,
    )
```

profile of v0, /device:TPU:1, one launch (start us, length us, event | category | flops | bytes accessed | tf_op | source)
XLA Modules:
  0.0 481.4 jit_solution(12729976653989056552)
XLA Ops:
  8.9 4.5 fusion.65
  13.5 3.8 select_select_fusion
  23.1 1.0 copy.200
  24.1 1.3 broadcast_and_fusion
  27.1 1.3 dynamic-slice.6
  29.5 106.4 %all-reduce.3 = (bf16[128]{0:T(256)(128)(2,1)S(1)}, bf16[128]{0:T(256)(128)(2,1)S(1)}) all-reduce(bf16[128]{0:T(256)(128)(2,1)S(1)} %dynamic-update-slice.3, bf16[128]{0:T(256)(128)(2,1)S(1)} %dynamic-update-slice.4), channel_id=2, replica_groups=mesh['seq'=64,'tp'=16] {'seq'}, use_global_device_ids=true, to_apply=%add | all-reduce | flops 256 | bytes 1024
  136.0 1.0 copy.167
  137.1 1.1 fusion.21
  138.2 37.0 %all-gather.7.cloned.1.call-done = bf16[128,128,128]{2,1,0:T(8,128)(2,1)} async-done(((bf16[2,128,128]{2,1,0:T(8,128)(2,1)}), bf16[128,128,128]{2,1,0:T(8,128)(2,1)}) %all-gather.7.cloned.1.call-update) | async-done | bytes 4194320 | tf_op jit(solution)/shard_map/all_gather | solution.py:20
  175.2 62.4 %while.31 = (s32[]{:T(128)}, f32[2,128,128]{2,1,0:T(8,128)S(1)}, s32[]{:T(128)}, bf16[64,2]{1,0:T(8,128)(2,1)S(1)}, bf16[64,2,128,128]{3,2,1,0:T(8,128)(2,1)}, /*index=5*/s32[]{:T(128)}, s32[]{:T(128)}) while((s32[]{:T(128)}, f32[2,128,128]{2,1,0:T(8,128)S(1)}, s32[]{:T(128)}, bf16[64,2]{1,0:T(8,128)(2,1)S(1)}, ...), condition=%wide.region_1.2_spmd.clone, body=%wide.region_0.1_spmd.clone.sunk | while | flops 163846 | bytes 327813 | solution.py:38
  176.2 0.9 fusion.120
  177.2 0.9 fusion.120
  178.1 0.9 fusion.120
  179.1 0.9 fusion.120
  180.1 0.9 fusion.120
  181.1 0.9 fusion.120
  182.1 0.9 fusion.120
  183.0 0.9 fusion.120
  238.3 1.0 multiply_reduce_fusion
  239.3 33.2 %all-reduce.2 = (f32[128]{0:T(128)S(1)}, f32[128]{0:T(128)S(1)}) all-reduce(f32[128]{0:T(128)S(1)} %multiply_reduce_fusion, f32[128]{0:T(128)S(1)} %get-tuple-element.374), channel_id=1, replica_groups=mesh['seq'=64,'tp'=16] {'tp'}, use_global_device_ids=true, to_apply=%region_5.6 | all-reduce | flops 256 | bytes 2048 | tf_op jit(solution)/shard_map/psum | solution.py:182
  273.9 10.5 %collective-permute-start = (bf16[128,2,128]{2,0,1:T(8,128)(2,1)S(1)}, bf16[128,2,128]{2,0,1:T(8,128)(2,1)S(1)}, u32[]{:S(2)}, u32[]{:S(2)}) collective-permute-start(bf16[128,2,128]{2,0,1:T(8,128)(2,1)S(1)} %copy.126), channel_id=1, source_target_pairs={{0,80},{16,96},{32,112},{48,128},{64,144},{80,160},{96,176},{112,1... | collective-permute-start | bytes 196616 | tf_op jit(solution)/shard_map/ppermute | solution.py:44
  284.4 3.4 collective-permute-start.1
  287.8 2.0 collective-permute-start.2
  289.7 3.0 collective-permute-start.3
  292.7 4.9 %collective-permute-start.4 = (bf16[128,2,128]{2,0,1:T(8,128)(2,1)S(1)}, bf16[128,2,128]{2,0,1:T(8,128)(2,1)S(1)}, u32[]{:S(2)}, u32[]{:S(2)}) collective-permute-start(bf16[128,2,128]{2,0,1:T(8,128)(2,1)S(1)} %copy.126), channel_id=1, source_target_pairs={{0,16},{16,32},{32,48},{48,64},{64,80},{80,96},{96,112},{112,128},... | collective-permute-start | bytes 196616 | tf_op jit(solution)/shard_map/ppermute | solution.py:44
  298.7 2.9 collective-permute-start.5
  301.6 3.3 collective-permute-start.6
  304.9 4.4 collective-permute-start.7
  309.4 2.9 collective-permute-start.8
  312.3 1.9 collective-permute-start.9
  314.4 1.2 collective-permute-done.9
  317.3 1.3 collective-permute-start.14
  318.6 1.3 collective-permute-start.13
  319.9 1.3 collective-permute-start.12
  321.2 1.3 collective-permute-start.11
  322.5 1.9 collective-permute-start.10
  324.8 1.5 fusion.81
  327.1 1.3 collective-permute-start.19
  329.3 1.3 collective-permute-start.18
  330.6 2.7 collective-permute-done.12
  333.3 1.3 collective-permute-start.17
  334.6 1.3 collective-permute-start.16
  335.9 1.9 collective-permute-start.15
  339.3 3.3 collective-permute-done.18
  342.6 3.1 collective-permute-done.17
  345.7 1.0 fusion.33
  348.8 60.6 %all-gather.9.cloned.1.call-done = bf16[128,128,128]{2,1,0:T(8,128)(2,1)} async-done(((bf16[2,128,128]{2,1,0:T(8,128)(2,1)}), bf16[128,128,128]{2,1,0:T(8,128)(2,1)}) %all-gather.9.cloned.1.call-update) | async-done | bytes 4194320 | tf_op jit(solution)/shard_map/all_gather | solution.py:20
  409.3 62.9 %while.32 = (s32[]{:T(128)}, f32[2,128,128]{2,1,0:T(8,128)S(1)}, s32[]{:T(128)}, bf16[64,2]{1,0:T(8,128)(2,1)S(1)}, bf16[64,2,128,128]{3,2,1,0:T(8,128)(2,1)}, /*index=5*/s32[]{:T(128)}, s32[]{:T(128)}, s32[]{:T(128)}, s32[]{:T(128)}) while((s32[]{:T(128)}, f32[2,128,128]{2,1,0:T(8,128)S(1)}, s32[]{:T(128)}, ...), condition=%wide.region_7.8_spmd.clone, body=%wide.region_6.7_spmd.clone.sunk | while | flops 163850 | bytes 327875 | solution.py:38
  (359 shorter events, 130.5 us)
Async XLA Ops:
  7.2 18.9 %copy-start = (bf16[128,256]{1,0:T(8,128)(2,1)S(1)}, bf16[128,256]{1,0:T(8,128)(2,1)}, u32[]{:S(2)}) copy-start(bf16[128,256]{1,0:T(8,128)(2,1)} %param.19) | copy-start | bytes 196612
  7.2 265.3 %copy-start.2 = (bf16[128,256]{1,0:T(8,128)(2,1)S(1)}, bf16[128,256]{1,0:T(8,128)(2,1)}, u32[]{:S(2)}) copy-start(bf16[128,256]{1,0:T(8,128)(2,1)} %param.22) | copy-start | bytes 196612
  7.2 265.3 %copy-start.7 = (f32[256]{0:T(256)S(1)}, f32[256]{0:T(256)}, u32[]{:S(2)}) copy-start(f32[256]{0:T(256)} %param.21) | copy-start | bytes 3076
  7.2 266.4 %copy-start.3 = (bf16[128,256]{1,0:T(8,128)(2,1)S(1)}, bf16[128,256]{1,0:T(8,128)(2,1)}, u32[]{:S(2)}) copy-start(bf16[128,256]{1,0:T(8,128)(2,1)} %param.24) | copy-start | bytes 196612
  7.2 290.9 %copy-start.4 = (bf16[128,256]{1,0:T(8,128)(2,1)S(1)}, bf16[128,256]{1,0:T(8,128)(2,1)}, u32[]{:S(2)}) copy-start(bf16[128,256]{1,0:T(8,128)(2,1)} %param.25) | copy-start | bytes 196612
  7.2 291.2 %copy-start.5 = (bf16[128,256]{1,0:T(8,128)(2,1)S(1)}, bf16[128,256]{1,0:T(8,128)(2,1)}, u32[]{:S(2)}) copy-start(bf16[128,256]{1,0:T(8,128)(2,1)} %param.26) | copy-start | bytes 196612
  7.2 291.3 %copy-start.6 = (bf16[128,256]{1,0:T(8,128)(2,1)S(1)}, bf16[128,256]{1,0:T(8,128)(2,1)}, u32[]{:S(2)}) copy-start(bf16[128,256]{1,0:T(8,128)(2,1)} %param.23) | copy-start | bytes 196612
  7.2 168.0 %all-gather.7.cloned.1.call-start = ((), (), s32[]{:S(2)}) async-start(), calls=%async_computation | async-start | bytes 4259840 | tf_op jit(solution)/shard_map/all_gather | solution.py:20
  27.0 382.4 %all-gather.9.cloned.1.call-start = ((), (), s32[]{:S(2)}) async-start(), calls=%async_computation.1 | async-start | bytes 4259840 | tf_op jit(solution)/shard_map/all_gather | solution.py:20
  273.9 24.8 %collective-permute-start = (bf16[128,2,128]{2,0,1:T(8,128)(2,1)S(1)}, bf16[128,2,128]{2,0,1:T(8,128)(2,1)S(1)}, u32[]{:S(2)}, u32[]{:S(2)}) collective-permute-start(bf16[128,2,128]{2,0,1:T(8,128)(2,1)S(1)} %copy.126), channel_id=1, source_target_pairs={{0,80},{16,96},{32,112},{48,128},{64,144},{80,160},{96,176},{112,1... | collective-permute-start | bytes 196616 | tf_op jit(solution)/shard_map/ppermute | solution.py:44
  284.4 17.2 %collective-permute-start.1 = (bf16[128,2,128]{2,0,1:T(8,128)(2,1)S(1)}, bf16[128,2,128]{2,0,1:T(8,128)(2,1)S(1)}, u32[]{:S(2)}, u32[]{:S(2)}) collective-permute-start(bf16[128,2,128]{2,0,1:T(8,128)(2,1)S(1)} %copy.126), channel_id=1, source_target_pairs={{0,64},{16,80},{32,96},{48,112},{64,128},{80,144},{96,160},{112,17... | collective-permute-start | bytes 196616 | tf_op jit(solution)/shard_map/ppermute | solution.py:44
  287.8 17.2 %collective-permute-start.2 = (bf16[128,2,128]{2,0,1:T(8,128)(2,1)S(1)}, bf16[128,2,128]{2,0,1:T(8,128)(2,1)S(1)}, u32[]{:S(2)}, u32[]{:S(2)}) collective-permute-start(bf16[128,2,128]{2,0,1:T(8,128)(2,1)S(1)} %copy.126), channel_id=1, source_target_pairs={{0,48},{16,64},{32,80},{48,96},{64,112},{80,128},{96,144},{112,160... | collective-permute-start | bytes 196616 | tf_op jit(solution)/shard_map/ppermute | solution.py:44
  289.7 19.6 %collective-permute-start.3 = (bf16[128,2,128]{2,0,1:T(8,128)(2,1)S(1)}, bf16[128,2,128]{2,0,1:T(8,128)(2,1)S(1)}, u32[]{:S(2)}, u32[]{:S(2)}) collective-permute-start(bf16[128,2,128]{2,0,1:T(8,128)(2,1)S(1)} %copy.126), channel_id=1, source_target_pairs={{0,32},{16,48},{32,64},{48,80},{64,96},{80,112},{96,128},{112,144}... | collective-permute-start | bytes 196616 | tf_op jit(solution)/shard_map/ppermute | solution.py:44
  292.7 19.6 %collective-permute-start.4 = (bf16[128,2,128]{2,0,1:T(8,128)(2,1)S(1)}, bf16[128,2,128]{2,0,1:T(8,128)(2,1)S(1)}, u32[]{:S(2)}, u32[]{:S(2)}) collective-permute-start(bf16[128,2,128]{2,0,1:T(8,128)(2,1)S(1)} %copy.126), channel_id=1, source_target_pairs={{0,16},{16,32},{32,48},{48,64},{64,80},{80,96},{96,112},{112,128},... | collective-permute-start | bytes 196616 | tf_op jit(solution)/shard_map/ppermute | solution.py:44
  298.7 15.6 %collective-permute-start.5 = (bf16[128,2,128]{2,0,1:T(8,128)(2,1)S(1)}, bf16[128,2,128]{2,0,1:T(8,128)(2,1)S(1)}, u32[]{:S(2)}, u32[]{:S(2)}) collective-permute-start(bf16[128,2,128]{2,0,1:T(8,128)(2,1)S(1)} %copy.134), channel_id=1, source_target_pairs={{0,80},{16,96},{32,112},{48,128},{64,144},{80,160},{96,176},{112,1... | collective-permute-start | bytes 196616 | tf_op jit(solution)/shard_map/ppermute | solution.py:44
  301.6 12.7 %collective-permute-start.6 = (bf16[128,2,128]{2,0,1:T(8,128)(2,1)S(1)}, bf16[128,2,128]{2,0,1:T(8,128)(2,1)S(1)}, u32[]{:S(2)}, u32[]{:S(2)}) collective-permute-start(bf16[128,2,128]{2,0,1:T(8,128)(2,1)S(1)} %copy.134), channel_id=1, source_target_pairs={{0,64},{16,80},{32,96},{48,112},{64,128},{80,144},{96,160},{112,17... | collective-permute-start | bytes 196616 | tf_op jit(solution)/shard_map/ppermute | solution.py:44
  304.9 9.4 %collective-permute-start.7 = (bf16[128,2,128]{2,0,1:T(8,128)(2,1)S(1)}, bf16[128,2,128]{2,0,1:T(8,128)(2,1)S(1)}, u32[]{:S(2)}, u32[]{:S(2)}) collective-permute-start(bf16[128,2,128]{2,0,1:T(8,128)(2,1)S(1)} %copy.134), channel_id=1, source_target_pairs={{0,48},{16,64},{32,80},{48,96},{64,112},{80,128},{96,144},{112,160... | collective-permute-start | bytes 196616 | tf_op jit(solution)/shard_map/ppermute | solution.py:44
  309.4 5.0 %collective-permute-start.8 = (bf16[128,2,128]{2,0,1:T(8,128)(2,1)S(1)}, bf16[128,2,128]{2,0,1:T(8,128)(2,1)S(1)}, u32[]{:S(2)}, u32[]{:S(2)}) collective-permute-start(bf16[128,2,128]{2,0,1:T(8,128)(2,1)S(1)} %copy.134), channel_id=1, source_target_pairs={{0,32},{16,48},{32,64},{48,80},{64,96},{80,112},{96,128},{112,144}... | collective-permute-start | bytes 196616 | tf_op jit(solution)/shard_map/ppermute | solution.py:44
  312.3 3.3 collective-permute-start.9
  317.3 9.8 %collective-permute-start.14 = (bf16[128,2,128]{2,0,1:T(8,128)(2,1)S(1)}, bf16[128,2,128]{2,0,1:T(8,128)(2,1)S(1)}, u32[]{:S(2)}, u32[]{:S(2)}) collective-permute-start(bf16[128,2,128]{2,0,1:T(8,128)(2,1)S(1)} %get-tuple-element.342), channel_id=1, source_target_pairs={{80,0},{96,16},{112,32},{128,48},{144,64},{160,80},{176,96},{192,1... | collective-permute-start | bytes 196616 | tf_op jit(solution)/shard_map/ppermute | solution.py:44
  318.6 10.7 %collective-permute-start.13 = (bf16[128,2,128]{2,0,1:T(8,128)(2,1)S(1)}, bf16[128,2,128]{2,0,1:T(8,128)(2,1)S(1)}, u32[]{:S(2)}, u32[]{:S(2)}) collective-permute-start(bf16[128,2,128]{2,0,1:T(8,128)(2,1)S(1)} %get-tuple-element.343), channel_id=1, source_target_pairs={{64,0},{80,16},{96,32},{112,48},{128,64},{144,80},{160,96},{176,11... | collective-permute-start | bytes 196616 | tf_op jit(solution)/shard_map/ppermute | solution.py:44
  319.9 13.4 %collective-permute-start.12 = (bf16[128,2,128]{2,0,1:T(8,128)(2,1)S(1)}, bf16[128,2,128]{2,0,1:T(8,128)(2,1)S(1)}, u32[]{:S(2)}, u32[]{:S(2)}) collective-permute-start(bf16[128,2,128]{2,0,1:T(8,128)(2,1)S(1)} %get-tuple-element.344), channel_id=1, source_target_pairs={{48,0},{64,16},{80,32},{96,48},{112,64},{128,80},{144,96},{160,112... | collective-permute-start | bytes 196616 | tf_op jit(solution)/shard_map/ppermute | solution.py:44
  321.2 13.4 %collective-permute-start.11 = (bf16[128,2,128]{2,0,1:T(8,128)(2,1)S(1)}, bf16[128,2,128]{2,0,1:T(8,128)(2,1)S(1)}, u32[]{:S(2)}, u32[]{:S(2)}) collective-permute-start(bf16[128,2,128]{2,0,1:T(8,128)(2,1)S(1)} %get-tuple-element.345), channel_id=1, source_target_pairs={{32,0},{48,16},{64,32},{80,48},{96,64},{112,80},{128,96},{144,112}... | collective-permute-start | bytes 196616 | tf_op jit(solution)/shard_map/ppermute | solution.py:44
  322.5 13.4 %collective-permute-start.10 = (bf16[128,2,128]{2,0,1:T(8,128)(2,1)S(1)}, bf16[128,2,128]{2,0,1:T(8,128)(2,1)S(1)}, u32[]{:S(2)}, u32[]{:S(2)}) collective-permute-start(bf16[128,2,128]{2,0,1:T(8,128)(2,1)S(1)} %get-tuple-element.341), channel_id=1, source_target_pairs={{16,0},{32,16},{48,32},{64,48},{80,64},{96,80},{112,96},{128,112},... | collective-permute-start | bytes 196616 | tf_op jit(solution)/shard_map/ppermute | solution.py:44
  324.8 147.7 %copy-start.1 = (bf16[128,256]{1,0:T(8,128)(2,1)S(1)}, bf16[128,256]{1,0:T(8,128)(2,1)}, u32[]{:S(2)}) copy-start(bf16[128,256]{1,0:T(8,128)(2,1)} %param.18) | copy-start | bytes 196612
  327.1 12.2 %collective-permute-start.19 = (bf16[128,2,128]{0,2,1:T(8,128)(2,1)S(1)}, bf16[128,2,128]{0,2,1:T(8,128)(2,1)S(1)}, u32[]{:S(2)}, u32[]{:S(2)}) collective-permute-start(bf16[128,2,128]{0,2,1:T(8,128)(2,1)S(1)} %get-tuple-element.337), channel_id=1, source_target_pairs={{80,0},{96,16},{112,32},{128,48},{144,64},{160,80},{176,96},{192,1... | collective-permute-start | bytes 196616 | tf_op jit(solution)/shard_map/ppermute | solution.py:44
  329.3 13.4 %collective-permute-start.18 = (bf16[128,2,128]{0,2,1:T(8,128)(2,1)S(1)}, bf16[128,2,128]{0,2,1:T(8,128)(2,1)S(1)}, u32[]{:S(2)}, u32[]{:S(2)}) collective-permute-start(bf16[128,2,128]{0,2,1:T(8,128)(2,1)S(1)} %get-tuple-element.338), channel_id=1, source_target_pairs={{64,0},{80,16},{96,32},{112,48},{128,64},{144,80},{160,96},{176,11... | collective-permute-start | bytes 196616 | tf_op jit(solution)/shard_map/ppermute | solution.py:44
  333.3 12.4 %collective-permute-start.17 = (bf16[128,2,128]{0,2,1:T(8,128)(2,1)S(1)}, bf16[128,2,128]{0,2,1:T(8,128)(2,1)S(1)}, u32[]{:S(2)}, u32[]{:S(2)}) collective-permute-start(bf16[128,2,128]{0,2,1:T(8,128)(2,1)S(1)} %get-tuple-element.339), channel_id=1, source_target_pairs={{48,0},{64,16},{80,32},{96,48},{112,64},{128,80},{144,96},{160,112... | collective-permute-start | bytes 196616 | tf_op jit(solution)/shard_map/ppermute | solution.py:44
  334.6 11.1 %collective-permute-start.16 = (bf16[128,2,128]{0,2,1:T(8,128)(2,1)S(1)}, bf16[128,2,128]{0,2,1:T(8,128)(2,1)S(1)}, u32[]{:S(2)}, u32[]{:S(2)}) collective-permute-start(bf16[128,2,128]{0,2,1:T(8,128)(2,1)S(1)} %get-tuple-element.340), channel_id=1, source_target_pairs={{32,0},{48,16},{64,32},{80,48},{96,64},{112,80},{128,96},{144,112}... | collective-permute-start | bytes 196616 | tf_op jit(solution)/shard_map/ppermute | solution.py:44
  335.9 9.8 %collective-permute-start.15 = (bf16[128,2,128]{0,2,1:T(8,128)(2,1)S(1)}, bf16[128,2,128]{0,2,1:T(8,128)(2,1)S(1)}, u32[]{:S(2)}, u32[]{:S(2)}) collective-permute-start(bf16[128,2,128]{0,2,1:T(8,128)(2,1)S(1)} %get-tuple-element.336), channel_id=1, source_target_pairs={{16,0},{32,16},{48,32},{64,48},{80,64},{96,80},{112,96},{128,112},... | collective-permute-start | bytes 196616 | tf_op jit(solution)/shard_map/ppermute | solution.py:44
Sparse Core Ops, SparseCore 0:
  27.1 148.0 all-gather.6
  273.8 135.5 all-gather.8
where the time goes:
time: 488 us; the launch traced here: 481 us
  blocking collectives  140 us (29%)
  other arithmetic  134 us (27%)
  waiting for transfers between devices  109 us (22%)
  starting transfers between devices  53.4 us (11%)
  between operations  20.6 us (4%)
  local copies, waits for them, and re-layouts  11.1 us (2%)
  matrix products  8.23 us (2%)
    select_n x128, other arithmetic, hop(): return jax.tree.map(lambda a, b: jnp.where(reached, a, b), new, before)  119 us
    unnamed x1, blocking collectives  106 us
    all_gather x2, waiting for transfers between devices, carried_in(): lax.all_gather(part.astype(kind), axis)  97.6 us
    ppermute x20, starting transfers between devices, shifted(): lax.ppermute(value, axis, [(source, source + steps) for source in range(f...  53.3 us
    psum x1, blocking collectives, body(): lax.psum((jnp.sum(flat * flat, axis=1), jnp.sum(flat * scaled_grad, axis=...  33.2 us
    ppermute x20, waiting for transfers between devices, shifted(): lax.ppermute(value, axis, [(source, source + steps) for source in range(f...  11.8 us
  transfers between devices with their start and end apart: 22, of which 8 were waited for; matrix products, arithmetic and copies ran while one was open for 3% of the time, Pallas kernels for 0%

commit v1 on v0

--- a/solution.py
+++ b/solution.py
@@ -14,34 +14,34 @@
 NORM_EPS = 1e-06
 
 
-def carried_in(shard, axis, combine, identity, reverse):
-    count, here = (lax.axis_size(axis), lax.axis_index(axis))
-    everything = jax.tree.map(
-        lambda part, kind: lax.all_gather(part.astype(kind), axis),
-        shard,
-        (jnp.bfloat16, jnp.bfloat16),
-    )
-    start = jax.tree.map(
-        lambda part, zero: jnp.broadcast_to(jnp.asarray(zero, part.dtype), part.shape),
-        shard,
-        identity,
-    )
-
-    def hop(k, before):
-        at = count - 1 - k if reverse else k
-        reached = at > here if reverse else at < here
-        new = combine(
-            before, jax.tree.map(lambda part, own: part[at].astype(own.dtype), everything, shard)
-        )
-        return jax.tree.map(lambda a, b: jnp.where(reached, a, b), new, before)
-
-    return lax.fori_loop(0, count, hop, start)
-
-
 def shifted(value, axis, steps):
     count = lax.axis_size(axis)
     first, last = (max(0, -steps), min(count, count - steps))
     return lax.ppermute(value, axis, [(source, source + steps) for source in range(first, last)])
+
+
+def tp_sum(value, axis):
+    count = lax.axis_size(axis)
+    if count & (count - 1):
+        return lax.psum(value, axis)
+    step = 1
+    while step < count:
+        value = value + lax.ppermute(value, axis, [(i, i ^ step) for i in range(count)])
+        step *= 2
+    return value
+
+
+def packed(*parts):
+    return jnp.concatenate([part.reshape(-1) for part in parts])
+
+
+def unpacked(flat, shapes):
+    out, at = [], 0
+    for shape in shapes:
+        size = math.prod(shape)
+        out.append(flat[at : at + size].reshape(shape))
+        at += size
+    return out
 
 
 def as_float(array):
@@ -110,10 +110,6 @@
     )
     factor = jnp.where(link & (labels[0] == labels[-1]), jnp.exp(-decay_rate * count), 0.0)
     return (factor, summary)
-
-
-def affine(earlier, later):
-    return (earlier[0] * later[0], later[0][:, None, None] * earlier[1] + later[1])
 
 
 def score_grads(probs, grads, value_part, delta):
@@ -162,13 +158,31 @@
     soft_keys = split_heads(soft_key)
     soft_values = split_heads(soft_value)
     soft_grads = split_heads(soft_grad)
-    factor, summary = forward_element(keys, values, own_labels, next_label, decay_rate)
+    _, summary = forward_element(keys, values, own_labels, next_label, decay_rate)
+    span = 2 * REACH + 1
+    firsts = window_blocks[::blocks_each]
+    lasts = window_blocks[blocks_each - 1 :: blocks_each]
+    full_decay = jnp.exp(-decay_rate * tokens)
+    ahead = [
+        jnp.where(firsts[at] == firsts[at + 1], full_decay, 0.0) for at in range(span - 1)
+    ]
+    behind = [None] + [
+        jnp.where((firsts[at] == lasts[at - 1]) & (firsts[at] == lasts[at]), full_decay, 0.0)
+        for at in range(1, span)
+    ]
+    kv_shape = soft_keys.shape
+    state_shape = summary.shape
+    forward_pack = packed(soft_keys, soft_values, summary.astype(jnp.bfloat16))
     received = []
-    state_in = carried_in(
-        (factor, summary), "seq", affine, (jnp.ones_like(factor), jnp.zeros_like(summary)), False
-    )[1]
+    state_in = jnp.zeros_like(summary)
+    chain = jnp.ones_like(decay_rate)
     for back in range(1, REACH):
-        received.append(shifted((soft_keys, soft_values), "seq", back))
+        got_key, got_value, got_state = unpacked(
+            shifted(forward_pack, "seq", back), (kv_shape, kv_shape, state_shape)
+        )
+        received.append((got_key, got_value))
+        state_in = state_in + chain[:, None, None] * as_float(got_state)
+        chain = chain * ahead[REACH - back]
     decay = decay_matrix(own_labels, decay_rate)
     scores = jnp.einsum("thd,shd->hts", queries, keys, preferred_element_type=jnp.float32)
     weights = (decay * scores).astype(jnp.bfloat16)
@@ -179,7 +193,7 @@
     lin_out = inner + carried * entry.T[:, :, None]
     flat = lin_out.reshape(tokens, heads * HD)
     scaled_grad = norm_gain[None, :] * as_float(lin_grad)
-    sums = lax.psum((jnp.sum(flat * flat, axis=1), jnp.sum(flat * scaled_grad, axis=1)), "tp")
+    sums = tp_sum(jnp.stack([jnp.sum(flat * flat, axis=1), jnp.sum(flat * scaled_grad, axis=1)]), "tp")
     width = lax.axis_size("tp") * heads * HD
     inverse = lax.rsqrt(sums[0] / width + NORM_EPS)
     cross = sums[1] / width
@@ -187,16 +201,8 @@
         jnp.bfloat16
     )
     grad_heads = split_heads(norm_grad)
-    back_factor, back_summary = backward_element(
-        queries, grad_heads, own_labels, prev_label, decay_rate
-    )
-    reverse_in = carried_in(
-        (back_factor, back_summary),
-        "seq",
-        affine,
-        (jnp.ones_like(back_factor), jnp.zeros_like(back_summary)),
-        True,
-    )[1]
+    _, back_summary = backward_element(queries, grad_heads, own_labels, prev_label, decay_rate)
+    back_state = back_summary.astype(jnp.bfloat16)
     grad_scores_lin = jnp.einsum(
         "thd,shd->hts", grad_heads, values, preferred_element_type=jnp.float32
     )
@@ -212,19 +218,11 @@
     lin_key_grad = jnp.einsum(
         "hts,thd->shd", grad_weights, queries, preferred_element_type=jnp.float32
     )
-    lin_key_grad = (
-        lin_key_grad
-        + jnp.einsum("she,hde->shd", as_float(values), reverse_in, precision=HIGH_PRECISION)
-        * leave.T[:, :, None]
-    )
+
     lin_value_grad = jnp.einsum(
         "hts,the->she", weights, grad_heads, preferred_element_type=jnp.float32
     )
-    lin_value_grad = (
-        lin_value_grad
-        + jnp.einsum("shd,hde->she", as_float(keys), reverse_in, precision=HIGH_PRECISION)
-        * leave.T[:, :, None]
-    )
+
     key_window = jnp.concatenate(
         [received[back - 1][0] for back in range(REACH - 1, 0, -1)] + [soft_keys], 0
     )
@@ -264,18 +262,30 @@
     )
     soft_key_grad = key_terms[(REACH - 1) * tokens :]
     soft_value_grad = value_terms[(REACH - 1) * tokens :]
+    reverse_in = jnp.zeros_like(back_summary)
+    chain = jnp.ones_like(decay_rate)
     for back in range(1, REACH):
         lower = (REACH - 1 - back) * tokens
-        got_key, got_value = (
-            shifted(key_terms[lower : lower + tokens].astype(jnp.bfloat16), "seq", -back).astype(
-                jnp.float32
-            ),
-            shifted(value_terms[lower : lower + tokens].astype(jnp.bfloat16), "seq", -back).astype(
-                jnp.float32
-            ),
+        backward_pack = packed(
+            key_terms[lower : lower + tokens].astype(jnp.bfloat16),
+            value_terms[lower : lower + tokens].astype(jnp.bfloat16),
+            back_state,
         )
-        soft_key_grad = soft_key_grad + got_key
-        soft_value_grad = soft_value_grad + got_value
+        got_key, got_value, got_state = unpacked(
+            shifted(backward_pack, "seq", -back), (kv_shape, kv_shape, state_shape)
+        )
+        soft_key_grad = soft_key_grad + as_float(got_key)
+        soft_value_grad = soft_value_grad + as_float(got_value)
+        reverse_in = reverse_in + chain[:, None, None] * as_float(got_state)
+        chain = chain * behind[REACH + back]
+    lin_key_grad = lin_key_grad + (
+        jnp.einsum("she,hde->shd", as_float(values), reverse_in, precision=HIGH_PRECISION)
+        * leave.T[:, :, None]
+    )
+    lin_value_grad = lin_value_grad + (
+        jnp.einsum("shd,hde->she", as_float(keys), reverse_in, precision=HIGH_PRECISION)
+        * leave.T[:, :, None]
+    )
 
     def merge_heads(array):
         return array.reshape(tokens, heads * HD).astype(jnp.bfloat16)

time: 488 us -> 147 us (0.30)
  the two profiles are of different devices: /device:TPU:1 before, /device:TPU:327 now
where the time goes in v1:
time: 147 us; the launch traced here: 145 us
  starting transfers between devices  51.5 us (35%)
  waiting for transfers between devices  44.8 us (30%)
  local copies, waits for them, and re-layouts  14.8 us (10%)
  between operations  14.1 us (10%)
  other arithmetic  12.1 us (8%)
  matrix products  8.09 us (6%)
    ppermute x10, waiting for transfers between devices, shifted(): lax.ppermute(value, axis, [(source, source + steps) for source in range(f...  40.9 us
    ppermute x10, starting transfers between devices, shifted(): lax.ppermute(value, axis, [(source, source + steps) for source in range(f...  38.2 us
    ppermute x4, starting transfers between devices, tp_sum(): lax.ppermute(value, axis, [(i, i ^ step) for i in range(count)])  13.2 us
    unnamed x43, local copies, waits for them, and re-layouts  10.8 us
    gather x2, other arithmetic, body(): jnp.repeat(window_blocks, BLK, total_repeat_length=(2 * REACH + 1) * tokens)  4.66 us
    ppermute x4, waiting for transfers between devices, tp_sum(): lax.ppermute(value, axis, [(i, i ^ step) for i in range(count)])  3.99 us
    select_n x1, other arithmetic, body(): jnp.repeat(window_blocks, BLK, total_repeat_length=(2 * REACH + 1) * tokens)  3.75 us
  transfers between devices with their start and end apart: 14, of which 10 were waited for; matrix products, arithmetic and copies ran while one was open for 7% of the time, Pallas kernels for 0%

profile of v1, /device:TPU:327, one launch (start us, length us, event | category | flops | bytes accessed | tf_op | source)
XLA Modules:
  0.0 145.4 jit_solution(16505923639360739244)
XLA Ops:
  0.7 0.6 copy-done.10
  1.5 0.7 fusion.102
  12.3 4.5 %fusion.71 = (s32[1664]{0:T(1024)S(1)}, s32[1664,1]{0,1:T(1,128)S(1)}) fusion(s32[]{:T(128)} %bitcast.8, s32[]{:T(128)} %bitcast.9, s32[]{:T(128)} %bitcast.10, s32[]{:T(128)} %bitcast.11, s32[]{:T(128)} %bitcast.12, s32[]{:T(128)} %bitcast.14, s32[]{:T(128)} %bitcast.13, s32[1,1,13,128]{3,2,1,0:T(8,128)S(1)} %get-tuple-element.132, ...), kind=kLoop, calls=%fused_computation.143 | loop fusion | flops 23296 | bytes 26652 | tf_op jit(solution)/shard_map/jit(_take)/gather | solution.py:145
  16.9 3.7 %select_select_fusion = s32[1664]{0:T(1024)S(1)} fusion(pred[1664]{0:T(1024)(128)(4,1)S(1)} %get-tuple-element.35, pred[1664]{0:T(1024)(128)(4,1)S(1)} %get-tuple-element.34, pred[1664]{0:T(1024)(128)(4,1)S(1)} %get-tuple-element.33, pred[1664]{0:T(1024)(128)(4,1)S(1)} %get-tuple-element.32, pred[1664]{0:T(1024)(128)(4,1)S(1)} %get-tuple-element.31, ...), kind=kLoop, calls=%fused_computation.134 | loop fusion | flops 24960 | bytes 23320 | tf_op jit(solution)/shard_map/jit(_take)/select_n | solution.py:145
  20.7 0.6 fusion.101
  21.3 0.8 copy-done.2
  22.2 0.8 copy-done.1
  25.7 1.3 broadcast_and_fusion
  27.0 0.6 copy-done.9
  28.0 8.0 %collective-permute-start.4 = (bf16[98304]{0:T(1024)(128)(2,1)S(1)}, bf16[98304]{0:T(1024)(128)(2,1)S(1)}, u32[]{:S(2)}, u32[]{:S(2)}) collective-permute-start(bf16[98304]{0:T(1024)(128)(2,1)S(1)} %pad_maximum_fusion.5), channel_id=1, source_target_pairs={{0,80},{16,96},{32,112},{48,128},{64,144},{80,160},{96,176},{112,1... | collective-permute-start | bytes 589832 | tf_op jit(solution)/shard_map/ppermute | solution.py:20
  36.0 4.9 %collective-permute-start.3 = (bf16[98304]{0:T(1024)(128)(2,1)S(1)}, bf16[98304]{0:T(1024)(128)(2,1)S(1)}, u32[]{:S(2)}, u32[]{:S(2)}) collective-permute-start(bf16[98304]{0:T(1024)(128)(2,1)S(1)} %pad_maximum_fusion.5), channel_id=1, source_target_pairs={{0,64},{16,80},{32,96},{48,112},{64,128},{80,144},{96,160},{112,17... | collective-permute-start | bytes 589832 | tf_op jit(solution)/shard_map/ppermute | solution.py:20
  40.9 4.8 %collective-permute-start.2 = (bf16[98304]{0:T(1024)(128)(2,1)S(1)}, bf16[98304]{0:T(1024)(128)(2,1)S(1)}, u32[]{:S(2)}, u32[]{:S(2)}) collective-permute-start(bf16[98304]{0:T(1024)(128)(2,1)S(1)} %pad_maximum_fusion.5), channel_id=1, source_target_pairs={{0,48},{16,64},{32,80},{48,96},{64,112},{80,128},{96,144},{112,160... | collective-permute-start | bytes 589832 | tf_op jit(solution)/shard_map/ppermute | solution.py:20
  45.7 2.6 %collective-permute-start.1 = (bf16[98304]{0:T(1024)(128)(2,1)S(1)}, bf16[98304]{0:T(1024)(128)(2,1)S(1)}, u32[]{:S(2)}, u32[]{:S(2)}) collective-permute-start(bf16[98304]{0:T(1024)(128)(2,1)S(1)} %pad_maximum_fusion.5), channel_id=1, source_target_pairs={{0,32},{16,48},{32,64},{48,80},{64,96},{80,112},{96,128},{112,144}... | collective-permute-start | bytes 589832 | tf_op jit(solution)/shard_map/ppermute | solution.py:20
  48.3 3.2 %collective-permute-start = (bf16[98304]{0:T(1024)(128)(2,1)S(1)}, bf16[98304]{0:T(1024)(128)(2,1)S(1)}, u32[]{:S(2)}, u32[]{:S(2)}) collective-permute-start(bf16[98304]{0:T(1024)(128)(2,1)S(1)} %pad_maximum_fusion.5), channel_id=1, source_target_pairs={{0,16},{16,32},{32,48},{48,64},{64,80},{80,96},{96,112},{112,128},... | collective-permute-start | bytes 589832 | tf_op jit(solution)/shard_map/ppermute | solution.py:20
  51.9 0.6 copy-done.5
  52.7 0.7 copy-done.6
  53.5 0.7 copy-done.7
  55.2 4.8 %collective-permute-done.2 = bf16[98304]{0:T(1024)(128)(2,1)S(1)} collective-permute-done((bf16[98304]{0:T(1024)(128)(2,1)S(1)}, bf16[98304]{0:T(1024)(128)(2,1)S(1)}, u32[]{:S(2)}, u32[]{:S(2)}) %collective-permute-start.2) | collective-permute-done | bytes 196640 | tf_op jit(solution)/shard_map/ppermute | solution.py:20
  60.0 3.8 %collective-permute-done.1 = bf16[98304]{0:T(1024)(128)(2,1)S(1)} collective-permute-done((bf16[98304]{0:T(1024)(128)(2,1)S(1)}, bf16[98304]{0:T(1024)(128)(2,1)S(1)}, u32[]{:S(2)}, u32[]{:S(2)}) %collective-permute-start.1) | collective-permute-done | bytes 196640 | tf_op jit(solution)/shard_map/ppermute | solution.py:20
  63.8 2.1 %collective-permute-done = bf16[98304]{0:T(1024)(128)(2,1)S(1)} collective-permute-done((bf16[98304]{0:T(1024)(128)(2,1)S(1)}, bf16[98304]{0:T(1024)(128)(2,1)S(1)}, u32[]{:S(2)}, u32[]{:S(2)}) %collective-permute-start) | collective-permute-done | bytes 196640 | tf_op jit(solution)/shard_map/ppermute | solution.py:20
  66.7 0.7 copy-done.4
  67.6 3.2 %collective-permute-start.5 = (f32[2,128]{1,0:T(2,128)S(1)}, f32[2,128]{1,0:T(2,128)S(1)}, u32[]{:S(2)}, u32[]{:S(2)}) collective-permute-start(f32[2,128]{1,0:T(2,128)S(1)} %pad_maximum_fusion.6), channel_id=1, source_target_pairs={{0,1},{1,0},{2,3},{3,2},{4,5},{5,4},{6,7},{7,6},{8,9},{9,8},{10,11... | collective-permute-start | bytes 3080 | tf_op jit(solution)/shard_map/ppermute | solution.py:29
  71.1 1.3 fusion.103
  72.3 1.5 %fusion.104 = (bf16[768,2,128]{0,2,1:T(8,128)(2,1)S(1)}, f32[768,2,128]{0,2,1:T(8,128)}) fusion(bf16[128,2,128]{0,2,1:T(8,128)(2,1)S(1)} %bitcast.363, f32[2,128]{1,0:T(2,128)S(1)} %get-tuple-element.125, bf16[768,2,128]{2,0,1:T(8,128)(2,1)S(1)} %constant_dynamic-update-slice_fusion, bf16[128,2,128]{0,2,1:T(8,128)(2,1)S(1)} %bitcast.306, ...), kind=kOutput, calls=%fused_computation.196 | convolution fusion | flops 101843968 | bytes 1803264 | tf_op jit(solution)/shard_map/htu,thd->uhd/dot_general | solution.py:260
  73.8 0.7 fusion.24
  74.5 1.4 fusion.8
  76.5 4.5 %collective-permute-start.6 = (f32[2,128]{1,0:T(2,128)S(1)}, f32[2,128]{1,0:T(2,128)S(1)}, u32[]{:S(2)}, u32[]{:S(2)}) collective-permute-start(f32[2,128]{1,0:T(2,128)S(1)} %fusion.82), channel_id=1, source_target_pairs={{0,2},{1,3},{2,0},{3,1},{4,6},{5,7},{6,4},{7,5},{8,10},{9,11},{10,... | collective-permute-start | bytes 3080 | tf_op jit(solution)/shard_map/ppermute | solution.py:29
  81.1 1.2 collective-permute-done.6
  82.3 2.5 %collective-permute-start.7 = (f32[2,128]{1,0:T(2,128)S(1)}, f32[2,128]{1,0:T(2,128)S(1)}, u32[]{:S(2)}, u32[]{:S(2)}) collective-permute-start(f32[2,128]{1,0:T(2,128)S(1)} %fusion.136), channel_id=1, source_target_pairs={{0,4},{1,5},{2,6},{3,7},{4,0},{5,1},{6,2},{7,3},{8,12},{9,13},{10,... | collective-permute-start | bytes 3080 | tf_op jit(solution)/shard_map/ppermute | solution.py:29
  84.8 0.7 copy.122
  85.6 1.1 collective-permute-done.7
  86.7 3.0 %collective-permute-start.8 = (f32[2,128]{1,0:T(2,128)S(1)}, f32[2,128]{1,0:T(2,128)S(1)}, u32[]{:S(2)}, u32[]{:S(2)}) collective-permute-start(f32[2,128]{1,0:T(2,128)S(1)} %add.171), channel_id=1, source_target_pairs={{0,8},{1,9},{2,10},{3,11},{4,12},{5,13},{6,14},{7,15},{8,0},{9,1},... | collective-permute-start | bytes 3080 | tf_op jit(solution)/shard_map/ppermute | solution.py:29
  90.7 1.7 %collective-permute-done.8 = f32[2,128]{1,0:T(2,128)S(1)} collective-permute-done((f32[2,128]{1,0:T(2,128)S(1)}, f32[2,128]{1,0:T(2,128)S(1)}, u32[]{:S(2)}, u32[]{:S(2)}) %collective-permute-start.8) | collective-permute-done | bytes 1056 | tf_op jit(solution)/shard_map/ppermute | solution.py:29
  93.5 5.8 %collective-permute-start.9 = (bf16[98304]{0:T(1024)(128)(2,1)S(1)}, bf16[98304]{0:T(1024)(128)(2,1)S(1)}, u32[]{:S(2)}, u32[]{:S(2)}) collective-permute-start(bf16[98304]{0:T(1024)(128)(2,1)S(1)} %get-tuple-element.88), channel_id=1, source_target_pairs={{16,0},{32,16},{48,32},{64,48},{80,64},{96,80},{112,96},{128,112},... | collective-permute-start | bytes 589832 | tf_op jit(solution)/shard_map/ppermute | solution.py:20
  99.5 0.7 copy.119
  100.2 2.2 %collective-permute-start.10 = (bf16[98304]{0:T(1024)(128)(2,1)S(1)}, bf16[98304]{0:T(1024)(128)(2,1)S(1)}, u32[]{:S(2)}, u32[]{:S(2)}) collective-permute-start(bf16[98304]{0:T(1024)(128)(2,1)S(1)} %get-tuple-element.89), channel_id=1, source_target_pairs={{32,0},{48,16},{64,32},{80,48},{96,64},{112,80},{128,96},{144,112}... | collective-permute-start | bytes 589832 | tf_op jit(solution)/shard_map/ppermute | solution.py:20
  102.4 2.9 %collective-permute-start.11 = (bf16[98304]{0:T(1024)(128)(2,1)S(1)}, bf16[98304]{0:T(1024)(128)(2,1)S(1)}, u32[]{:S(2)}, u32[]{:S(2)}) collective-permute-start(bf16[98304]{0:T(1024)(128)(2,1)S(1)} %get-tuple-element.90), channel_id=1, source_target_pairs={{48,0},{64,16},{80,32},{96,48},{112,64},{128,80},{144,96},{160,112... | collective-permute-start | bytes 589832 | tf_op jit(solution)/shard_map/ppermute | solution.py:20
  105.3 1.9 %collective-permute-start.12 = (bf16[98304]{0:T(1024)(128)(2,1)S(1)}, bf16[98304]{0:T(1024)(128)(2,1)S(1)}, u32[]{:S(2)}, u32[]{:S(2)}) collective-permute-start(bf16[98304]{0:T(1024)(128)(2,1)S(1)} %get-tuple-element.91), channel_id=1, source_target_pairs={{64,0},{80,16},{96,32},{112,48},{128,64},{144,80},{160,96},{176,11... | collective-permute-start | bytes 589832 | tf_op jit(solution)/shard_map/ppermute | solution.py:20
  107.2 1.9 %collective-permute-start.13 = (bf16[98304]{0:T(1024)(128)(2,1)S(1)}, bf16[98304]{0:T(1024)(128)(2,1)S(1)}, u32[]{:S(2)}, u32[]{:S(2)}) collective-permute-start(bf16[98304]{0:T(1024)(128)(2,1)S(1)} %get-tuple-element.92), channel_id=1, source_target_pairs={{80,0},{96,16},{112,32},{128,48},{144,64},{160,80},{176,96},{192,1... | collective-permute-start | bytes 589832 | tf_op jit(solution)/shard_map/ppermute | solution.py:20
  109.2 0.6 collective-permute-done.10
  109.8 9.0 %collective-permute-done.11 = bf16[98304]{0:T(1024)(128)(2,1)S(1)} collective-permute-done((bf16[98304]{0:T(1024)(128)(2,1)S(1)}, bf16[98304]{0:T(1024)(128)(2,1)S(1)}, u32[]{:S(2)}, u32[]{:S(2)}) %collective-permute-start.11) | collective-permute-done | bytes 196640 | tf_op jit(solution)/shard_map/ppermute | solution.py:20
  118.8 7.3 %collective-permute-done.12 = bf16[98304]{0:T(1024)(128)(2,1)S(1)} collective-permute-done((bf16[98304]{0:T(1024)(128)(2,1)S(1)}, bf16[98304]{0:T(1024)(128)(2,1)S(1)}, u32[]{:S(2)}, u32[]{:S(2)}) %collective-permute-start.12) | collective-permute-done | bytes 196640 | tf_op jit(solution)/shard_map/ppermute | solution.py:20
  126.1 13.3 %collective-permute-done.13 = bf16[98304]{0:T(1024)(128)(2,1)S(1)} collective-permute-done((bf16[98304]{0:T(1024)(128)(2,1)S(1)}, bf16[98304]{0:T(1024)(128)(2,1)S(1)}, u32[]{:S(2)}, u32[]{:S(2)}) %collective-permute-start.13) | collective-permute-done | bytes 196640 | tf_op jit(solution)/shard_map/ppermute | solution.py:20
  141.0 0.7 copy.123
  141.9 0.9 fusion.31
  142.9 0.7 copy.124
  143.9 0.7 copy.120
  144.7 0.7 copy.121
  (120 shorter events, 8.3 us)
Async XLA Ops:
  0.6 27.1 %copy-start = (bf16[128,256]{1,0:T(8,128)(2,1)S(1)}, bf16[128,256]{1,0:T(8,128)(2,1)}, u32[]{:S(2)}) copy-start(bf16[128,256]{1,0:T(8,128)(2,1)} %param.15) | copy-start | bytes 196612
  0.7 0.7 copy-start.10
  12.2 9.0 %copy-start.3 = (bf16[128,256]{1,0:T(8,128)(2,1)S(1)}, bf16[128,256]{1,0:T(8,128)(2,1)}, u32[]{:S(2)}) copy-start(bf16[128,256]{1,0:T(8,128)(2,1)} %param.21) | copy-start | bytes 196612
  21.3 0.8 copy-start.2
  22.1 0.8 copy-start.1
  27.0 0.7 copy-start.9
  28.0 27.2 %collective-permute-start.4 = (bf16[98304]{0:T(1024)(128)(2,1)S(1)}, bf16[98304]{0:T(1024)(128)(2,1)S(1)}, u32[]{:S(2)}, u32[]{:S(2)}) collective-permute-start(bf16[98304]{0:T(1024)(128)(2,1)S(1)} %pad_maximum_fusion.5), channel_id=1, source_target_pairs={{0,80},{16,96},{32,112},{48,128},{64,144},{80,160},{96,176},{112,1... | collective-permute-start | bytes 589832 | tf_op jit(solution)/shard_map/ppermute | solution.py:20
  36.0 19.2 %collective-permute-start.3 = (bf16[98304]{0:T(1024)(128)(2,1)S(1)}, bf16[98304]{0:T(1024)(128)(2,1)S(1)}, u32[]{:S(2)}, u32[]{:S(2)}) collective-permute-start(bf16[98304]{0:T(1024)(128)(2,1)S(1)} %pad_maximum_fusion.5), channel_id=1, source_target_pairs={{0,64},{16,80},{32,96},{48,112},{64,128},{80,144},{96,160},{112,17... | collective-permute-start | bytes 589832 | tf_op jit(solution)/shard_map/ppermute | solution.py:20
  40.9 19.1 %collective-permute-start.2 = (bf16[98304]{0:T(1024)(128)(2,1)S(1)}, bf16[98304]{0:T(1024)(128)(2,1)S(1)}, u32[]{:S(2)}, u32[]{:S(2)}) collective-permute-start(bf16[98304]{0:T(1024)(128)(2,1)S(1)} %pad_maximum_fusion.5), channel_id=1, source_target_pairs={{0,48},{16,64},{32,80},{48,96},{64,112},{80,128},{96,144},{112,160... | collective-permute-start | bytes 589832 | tf_op jit(solution)/shard_map/ppermute | solution.py:20
  45.7 18.1 %collective-permute-start.1 = (bf16[98304]{0:T(1024)(128)(2,1)S(1)}, bf16[98304]{0:T(1024)(128)(2,1)S(1)}, u32[]{:S(2)}, u32[]{:S(2)}) collective-permute-start(bf16[98304]{0:T(1024)(128)(2,1)S(1)} %pad_maximum_fusion.5), channel_id=1, source_target_pairs={{0,32},{16,48},{32,64},{48,80},{64,96},{80,112},{96,128},{112,144}... | collective-permute-start | bytes 589832 | tf_op jit(solution)/shard_map/ppermute | solution.py:20
  48.3 17.6 %collective-permute-start = (bf16[98304]{0:T(1024)(128)(2,1)S(1)}, bf16[98304]{0:T(1024)(128)(2,1)S(1)}, u32[]{:S(2)}, u32[]{:S(2)}) collective-permute-start(bf16[98304]{0:T(1024)(128)(2,1)S(1)} %pad_maximum_fusion.5), channel_id=1, source_target_pairs={{0,16},{16,32},{32,48},{48,64},{64,80},{80,96},{96,112},{112,128},... | collective-permute-start | bytes 589832 | tf_op jit(solution)/shard_map/ppermute | solution.py:20
  51.7 0.8 copy-start.5
  52.5 0.8 copy-start.6
  53.4 0.8 copy-start.7
  66.6 0.8 copy-start.4
  66.6 0.8 copy-start.8
  67.6 8.9 %collective-permute-start.5 = (f32[2,128]{1,0:T(2,128)S(1)}, f32[2,128]{1,0:T(2,128)S(1)}, u32[]{:S(2)}, u32[]{:S(2)}) collective-permute-start(f32[2,128]{1,0:T(2,128)S(1)} %pad_maximum_fusion.6), channel_id=1, source_target_pairs={{0,1},{1,0},{2,3},{3,2},{4,5},{5,4},{6,7},{7,6},{8,9},{9,8},{10,11... | collective-permute-start | bytes 3080 | tf_op jit(solution)/shard_map/ppermute | solution.py:29
  76.5 5.8 %collective-permute-start.6 = (f32[2,128]{1,0:T(2,128)S(1)}, f32[2,128]{1,0:T(2,128)S(1)}, u32[]{:S(2)}, u32[]{:S(2)}) collective-permute-start(f32[2,128]{1,0:T(2,128)S(1)} %fusion.82), channel_id=1, source_target_pairs={{0,2},{1,3},{2,0},{3,1},{4,6},{5,7},{6,4},{7,5},{8,10},{9,11},{10,... | collective-permute-start | bytes 3080 | tf_op jit(solution)/shard_map/ppermute | solution.py:29
  82.3 4.3 %collective-permute-start.7 = (f32[2,128]{1,0:T(2,128)S(1)}, f32[2,128]{1,0:T(2,128)S(1)}, u32[]{:S(2)}, u32[]{:S(2)}) collective-permute-start(f32[2,128]{1,0:T(2,128)S(1)} %fusion.136), channel_id=1, source_target_pairs={{0,4},{1,5},{2,6},{3,7},{4,0},{5,1},{6,2},{7,3},{8,12},{9,13},{10,... | collective-permute-start | bytes 3080 | tf_op jit(solution)/shard_map/ppermute | solution.py:29
  86.7 5.8 %collective-permute-start.8 = (f32[2,128]{1,0:T(2,128)S(1)}, f32[2,128]{1,0:T(2,128)S(1)}, u32[]{:S(2)}, u32[]{:S(2)}) collective-permute-start(f32[2,128]{1,0:T(2,128)S(1)} %add.171), channel_id=1, source_target_pairs={{0,8},{1,9},{2,10},{3,11},{4,12},{5,13},{6,14},{7,15},{8,0},{9,1},... | collective-permute-start | bytes 3080 | tf_op jit(solution)/shard_map/ppermute | solution.py:29
  93.5 15.7 %collective-permute-start.9 = (bf16[98304]{0:T(1024)(128)(2,1)S(1)}, bf16[98304]{0:T(1024)(128)(2,1)S(1)}, u32[]{:S(2)}, u32[]{:S(2)}) collective-permute-start(bf16[98304]{0:T(1024)(128)(2,1)S(1)} %get-tuple-element.88), channel_id=1, source_target_pairs={{16,0},{32,16},{48,32},{64,48},{80,64},{96,80},{112,96},{128,112},... | collective-permute-start | bytes 589832 | tf_op jit(solution)/shard_map/ppermute | solution.py:20
  100.2 9.6 %collective-permute-start.10 = (bf16[98304]{0:T(1024)(128)(2,1)S(1)}, bf16[98304]{0:T(1024)(128)(2,1)S(1)}, u32[]{:S(2)}, u32[]{:S(2)}) collective-permute-start(bf16[98304]{0:T(1024)(128)(2,1)S(1)} %get-tuple-element.89), channel_id=1, source_target_pairs={{32,0},{48,16},{64,32},{80,48},{96,64},{112,80},{128,96},{144,112}... | collective-permute-start | bytes 589832 | tf_op jit(solution)/shard_map/ppermute | solution.py:20
  102.4 16.4 %collective-permute-start.11 = (bf16[98304]{0:T(1024)(128)(2,1)S(1)}, bf16[98304]{0:T(1024)(128)(2,1)S(1)}, u32[]{:S(2)}, u32[]{:S(2)}) collective-permute-start(bf16[98304]{0:T(1024)(128)(2,1)S(1)} %get-tuple-element.90), channel_id=1, source_target_pairs={{48,0},{64,16},{80,32},{96,48},{112,64},{128,80},{144,96},{160,112... | collective-permute-start | bytes 589832 | tf_op jit(solution)/shard_map/ppermute | solution.py:20
  105.3 20.8 %collective-permute-start.12 = (bf16[98304]{0:T(1024)(128)(2,1)S(1)}, bf16[98304]{0:T(1024)(128)(2,1)S(1)}, u32[]{:S(2)}, u32[]{:S(2)}) collective-permute-start(bf16[98304]{0:T(1024)(128)(2,1)S(1)} %get-tuple-element.91), channel_id=1, source_target_pairs={{64,0},{80,16},{96,32},{112,48},{128,64},{144,80},{160,96},{176,11... | collective-permute-start | bytes 589832 | tf_op jit(solution)/shard_map/ppermute | solution.py:20
  107.2 32.2 %collective-permute-start.13 = (bf16[98304]{0:T(1024)(128)(2,1)S(1)}, bf16[98304]{0:T(1024)(128)(2,1)S(1)}, u32[]{:S(2)}, u32[]{:S(2)}) collective-permute-start(bf16[98304]{0:T(1024)(128)(2,1)S(1)} %get-tuple-element.92), channel_id=1, source_target_pairs={{80,0},{96,16},{112,32},{128,48},{144,64},{160,80},{176,96},{192,1... | collective-permute-start | bytes 589832 | tf_op jit(solution)/shard_map/ppermute | solution.py:20

commit v2 on v1

--- a/solution.py
+++ b/solution.py
@@ -21,14 +21,7 @@
 
 
 def tp_sum(value, axis):
-    count = lax.axis_size(axis)
-    if count & (count - 1):
-        return lax.psum(value, axis)
-    step = 1
-    while step < count:
-        value = value + lax.ppermute(value, axis, [(i, i ^ step) for i in range(count)])
-        step *= 2
-    return value
+    return jnp.sum(lax.all_gather(value, axis), axis=0)
 
 
 def packed(*parts):
@@ -142,7 +135,7 @@
     window_blocks = lax.dynamic_slice_in_dim(
         padded, device * blocks_each, (2 * REACH + 1) * blocks_each
     )
-    window_labels = jnp.repeat(window_blocks, BLK, total_repeat_length=(2 * REACH + 1) * tokens)
+    window_labels = jnp.broadcast_to(window_blocks[:, None], (window_blocks.shape[0], BLK)).reshape(-1)
     own_labels = window_labels[REACH * tokens : (REACH + 1) * tokens]
     prev_label = window_labels[REACH * tokens - 1]
     next_label = window_labels[(REACH + 1) * tokens]

time: 147 us -> 137 us (0.932)
  the two profiles are of different devices: /device:TPU:327 before, /device:TPU:321 now
where the time goes in v2:
time: 137 us; the launch traced here: 136 us
  waiting for transfers between devices  40.2 us (29%)
  starting transfers between devices  40 us (29%)
  blocking collectives  18.1 us (13%)
  local copies, waits for them, and re-layouts  14.2 us (10%)
  between operations  14.1 us (10%)
  matrix products  6.13 us (4%)
  other arithmetic  3.65 us (3%)
    ppermute x10, waiting for transfers between devices, shifted(): lax.ppermute(value, axis, [(source, source + steps) for source in range(f...  40.2 us
    ppermute x10, starting transfers between devices, shifted(): lax.ppermute(value, axis, [(source, source + steps) for source in range(f...  40 us
    all_gather x1, blocking collectives, tp_sum(): return jnp.sum(lax.all_gather(value, axis), axis=0)  18.1 us
    unnamed x41, local copies, waits for them, and re-layouts  10 us
  transfers between devices with their start and end apart: 10, of which 7 were waited for; matrix products, arithmetic and copies ran while one was open for 2% of the time, Pallas kernels for 0%

profile of v2, /device:TPU:321, one launch (start us, length us, event | category | flops | bytes accessed | tf_op | source)
XLA Modules:
  0.0 136.4 jit_solution(14618084611496296654)
XLA Ops:
  0.7 0.7 pad_add_fusion
  1.5 0.7 fusion.92
  12.6 0.6 fusion.91
  15.7 0.8 copy-done.2
  16.6 0.8 copy-done.1
  17.5 0.5 copy-done.9
  18.3 8.0 %collective-permute-start.4 = (bf16[98304]{0:T(1024)(128)(2,1)S(1)}, bf16[98304]{0:T(1024)(128)(2,1)S(1)}, u32[]{:S(2)}, u32[]{:S(2)}) collective-permute-start(bf16[98304]{0:T(1024)(128)(2,1)S(1)} %pad_maximum_fusion.5), channel_id=1, source_target_pairs={{0,80},{16,96},{32,112},{48,128},{64,144},{80,160},{96,176},{112,1... | collective-permute-start | bytes 589832 | tf_op jit(solution)/shard_map/ppermute | solution.py:20
  26.4 4.9 %collective-permute-start.3 = (bf16[98304]{0:T(1024)(128)(2,1)S(1)}, bf16[98304]{0:T(1024)(128)(2,1)S(1)}, u32[]{:S(2)}, u32[]{:S(2)}) collective-permute-start(bf16[98304]{0:T(1024)(128)(2,1)S(1)} %pad_maximum_fusion.5), channel_id=1, source_target_pairs={{0,64},{16,80},{32,96},{48,112},{64,128},{80,144},{96,160},{112,17... | collective-permute-start | bytes 589832 | tf_op jit(solution)/shard_map/ppermute | solution.py:20
  31.3 4.8 %collective-permute-start.2 = (bf16[98304]{0:T(1024)(128)(2,1)S(1)}, bf16[98304]{0:T(1024)(128)(2,1)S(1)}, u32[]{:S(2)}, u32[]{:S(2)}) collective-permute-start(bf16[98304]{0:T(1024)(128)(2,1)S(1)} %pad_maximum_fusion.5), channel_id=1, source_target_pairs={{0,48},{16,64},{32,80},{48,96},{64,112},{80,128},{96,144},{112,160... | collective-permute-start | bytes 589832 | tf_op jit(solution)/shard_map/ppermute | solution.py:20
  36.0 2.6 %collective-permute-start.1 = (bf16[98304]{0:T(1024)(128)(2,1)S(1)}, bf16[98304]{0:T(1024)(128)(2,1)S(1)}, u32[]{:S(2)}, u32[]{:S(2)}) collective-permute-start(bf16[98304]{0:T(1024)(128)(2,1)S(1)} %pad_maximum_fusion.5), channel_id=1, source_target_pairs={{0,32},{16,48},{32,64},{48,80},{64,96},{80,112},{96,128},{112,144}... | collective-permute-start | bytes 589832 | tf_op jit(solution)/shard_map/ppermute | solution.py:20
  38.7 3.2 %collective-permute-start = (bf16[98304]{0:T(1024)(128)(2,1)S(1)}, bf16[98304]{0:T(1024)(128)(2,1)S(1)}, u32[]{:S(2)}, u32[]{:S(2)}) collective-permute-start(bf16[98304]{0:T(1024)(128)(2,1)S(1)} %pad_maximum_fusion.5), channel_id=1, source_target_pairs={{0,16},{16,32},{32,48},{48,64},{64,80},{80,96},{96,112},{112,128},... | collective-permute-start | bytes 589832 | tf_op jit(solution)/shard_map/ppermute | solution.py:20
  41.9 0.6 slice_compare_fusion
  42.9 0.6 copy-done.5
  43.7 0.7 copy-done.6
  44.5 0.7 copy-done.7
  45.8 0.3 fusion.25
  46.2 4.1 %collective-permute-done.2 = bf16[98304]{0:T(1024)(128)(2,1)S(1)} collective-permute-done((bf16[98304]{0:T(1024)(128)(2,1)S(1)}, bf16[98304]{0:T(1024)(128)(2,1)S(1)}, u32[]{:S(2)}, u32[]{:S(2)}) %collective-permute-start.2) | collective-permute-done | bytes 196640 | tf_op jit(solution)/shard_map/ppermute | solution.py:20
  50.3 3.8 %collective-permute-done.1 = bf16[98304]{0:T(1024)(128)(2,1)S(1)} collective-permute-done((bf16[98304]{0:T(1024)(128)(2,1)S(1)}, bf16[98304]{0:T(1024)(128)(2,1)S(1)}, u32[]{:S(2)}, u32[]{:S(2)}) %collective-permute-start.1) | collective-permute-done | bytes 196640 | tf_op jit(solution)/shard_map/ppermute | solution.py:20
  54.2 2.1 %collective-permute-done = bf16[98304]{0:T(1024)(128)(2,1)S(1)} collective-permute-done((bf16[98304]{0:T(1024)(128)(2,1)S(1)}, bf16[98304]{0:T(1024)(128)(2,1)S(1)}, u32[]{:S(2)}, u32[]{:S(2)}) %collective-permute-start) | collective-permute-done | bytes 196640 | tf_op jit(solution)/shard_map/ppermute | solution.py:20
  56.4 0.3 fusion.16
  56.7 0.2 multiply_reduce_fusion.1
  57.1 0.7 copy-done.4
  57.9 18.1 %all-gather.1 = f32[16,2,128]{2,1,0:T(2,128)S(1)} all-gather(f32[1,2,128]{2,1,0:T(2,128)S(1)} %maximum_bitcast_fusion), channel_id=2, replica_groups=mesh['seq'=64,'tp'=16] {'tp'}, dimensions={0}, use_global_device_ids=true | all-gather | bytes 17408 | tf_op jit(solution)/shard_map/all_gather | solution.py:24
  76.9 0.7 copy.191
  77.7 0.3 convolution_convert_fusion
  78.2 0.4 fusion.93
  78.7 1.5 %fusion.94 = (bf16[768,2,128]{0,2,1:T(8,128)(2,1)S(1)}, f32[768,2,128]{0,2,1:T(8,128)}) fusion(bf16[128,2,128]{0,2,1:T(8,128)(2,1)S(1)} %bitcast.317, f32[2,128]{1,0:T(2,128)S(1)} %get-tuple-element.99, bf16[768,2,128]{2,0,1:T(8,128)(2,1)S(1)} %constant_dynamic-update-slice_fusion, bf16[128,2,128]{0,2,1:T(8,128)(2,1)S(1)} %bitcast.260, ...), kind=kOutput, calls=%fused_computation.169 | convolution fusion | flops 101843968 | bytes 1803264 | tf_op jit(solution)/shard_map/htu,thd->uhd/dot_general | solution.py:253
  80.2 0.7 fusion.24
  81.6 0.3 fusion.8
  81.8 0.3 fusion.95
  82.6 7.6 %collective-permute-start.5 = (bf16[98304]{0:T(1024)(128)(2,1)S(1)}, bf16[98304]{0:T(1024)(128)(2,1)S(1)}, u32[]{:S(2)}, u32[]{:S(2)}) collective-permute-start(bf16[98304]{0:T(1024)(128)(2,1)S(1)} %get-tuple-element.70), channel_id=1, source_target_pairs={{16,0},{32,16},{48,32},{64,48},{80,64},{96,80},{112,96},{128,112},... | collective-permute-start | bytes 589832 | tf_op jit(solution)/shard_map/ppermute | solution.py:20
  90.2 0.3 fusion.18
  90.5 0.7 copy.194
  91.2 2.2 %collective-permute-start.6 = (bf16[98304]{0:T(1024)(128)(2,1)S(1)}, bf16[98304]{0:T(1024)(128)(2,1)S(1)}, u32[]{:S(2)}, u32[]{:S(2)}) collective-permute-start(bf16[98304]{0:T(1024)(128)(2,1)S(1)} %get-tuple-element.71), channel_id=1, source_target_pairs={{32,0},{48,16},{64,32},{80,48},{96,64},{112,80},{128,96},{144,112}... | collective-permute-start | bytes 589832 | tf_op jit(solution)/shard_map/ppermute | solution.py:20
  93.4 2.9 %collective-permute-start.7 = (bf16[98304]{0:T(1024)(128)(2,1)S(1)}, bf16[98304]{0:T(1024)(128)(2,1)S(1)}, u32[]{:S(2)}, u32[]{:S(2)}) collective-permute-start(bf16[98304]{0:T(1024)(128)(2,1)S(1)} %get-tuple-element.72), channel_id=1, source_target_pairs={{48,0},{64,16},{80,32},{96,48},{112,64},{128,80},{144,96},{160,112... | collective-permute-start | bytes 589832 | tf_op jit(solution)/shard_map/ppermute | solution.py:20
  96.3 1.9 %collective-permute-start.8 = (bf16[98304]{0:T(1024)(128)(2,1)S(1)}, bf16[98304]{0:T(1024)(128)(2,1)S(1)}, u32[]{:S(2)}, u32[]{:S(2)}) collective-permute-start(bf16[98304]{0:T(1024)(128)(2,1)S(1)} %get-tuple-element.73), channel_id=1, source_target_pairs={{64,0},{80,16},{96,32},{112,48},{128,64},{144,80},{160,96},{176,11... | collective-permute-start | bytes 589832 | tf_op jit(solution)/shard_map/ppermute | solution.py:20
  98.2 1.9 %collective-permute-start.9 = (bf16[98304]{0:T(1024)(128)(2,1)S(1)}, bf16[98304]{0:T(1024)(128)(2,1)S(1)}, u32[]{:S(2)}, u32[]{:S(2)}) collective-permute-start(bf16[98304]{0:T(1024)(128)(2,1)S(1)} %get-tuple-element.74), channel_id=1, source_target_pairs={{80,0},{96,16},{112,32},{128,48},{144,64},{160,80},{176,96},{192,1... | collective-permute-start | bytes 589832 | tf_op jit(solution)/shard_map/ppermute | solution.py:20
  100.2 0.6 collective-permute-done.6
  100.8 9.0 %collective-permute-done.7 = bf16[98304]{0:T(1024)(128)(2,1)S(1)} collective-permute-done((bf16[98304]{0:T(1024)(128)(2,1)S(1)}, bf16[98304]{0:T(1024)(128)(2,1)S(1)}, u32[]{:S(2)}, u32[]{:S(2)}) %collective-permute-start.7) | collective-permute-done | bytes 196640 | tf_op jit(solution)/shard_map/ppermute | solution.py:20
  109.8 7.3 %collective-permute-done.8 = bf16[98304]{0:T(1024)(128)(2,1)S(1)} collective-permute-done((bf16[98304]{0:T(1024)(128)(2,1)S(1)}, bf16[98304]{0:T(1024)(128)(2,1)S(1)}, u32[]{:S(2)}, u32[]{:S(2)}) %collective-permute-start.8) | collective-permute-done | bytes 196640 | tf_op jit(solution)/shard_map/ppermute | solution.py:20
  117.1 13.3 %collective-permute-done.9 = bf16[98304]{0:T(1024)(128)(2,1)S(1)} collective-permute-done((bf16[98304]{0:T(1024)(128)(2,1)S(1)}, bf16[98304]{0:T(1024)(128)(2,1)S(1)}, u32[]{:S(2)}, u32[]{:S(2)}) %collective-permute-start.9) | collective-permute-done | bytes 196640 | tf_op jit(solution)/shard_map/ppermute | solution.py:20
  130.6 0.3 fusion.11
  130.9 0.3 fusion.13
  132.1 0.7 copy.195
  132.9 1.0 fusion.31
  133.9 0.7 copy.196
  134.9 0.7 copy.192
  135.7 0.7 copy.193
  (104 shorter events, 6.0 us)
Async XLA Ops:
  0.6 17.5 %copy-start = (bf16[128,256]{1,0:T(8,128)(2,1)S(1)}, bf16[128,256]{1,0:T(8,128)(2,1)}, u32[]{:S(2)}) copy-start(bf16[128,256]{1,0:T(8,128)(2,1)} %param.13) | copy-start | bytes 196612
  0.6 15.0 %copy-start.3 = (bf16[128,256]{1,0:T(8,128)(2,1)S(1)}, bf16[128,256]{1,0:T(8,128)(2,1)}, u32[]{:S(2)}) copy-start(bf16[128,256]{1,0:T(8,128)(2,1)} %param.19) | copy-start | bytes 196612
  15.7 0.8 copy-start.2
  16.5 0.8 copy-start.1
  17.3 0.7 copy-start.9
  18.3 27.8 %collective-permute-start.4 = (bf16[98304]{0:T(1024)(128)(2,1)S(1)}, bf16[98304]{0:T(1024)(128)(2,1)S(1)}, u32[]{:S(2)}, u32[]{:S(2)}) collective-permute-start(bf16[98304]{0:T(1024)(128)(2,1)S(1)} %pad_maximum_fusion.5), channel_id=1, source_target_pairs={{0,80},{16,96},{32,112},{48,128},{64,144},{80,160},{96,176},{112,1... | collective-permute-start | bytes 589832 | tf_op jit(solution)/shard_map/ppermute | solution.py:20
  26.4 19.8 %collective-permute-start.3 = (bf16[98304]{0:T(1024)(128)(2,1)S(1)}, bf16[98304]{0:T(1024)(128)(2,1)S(1)}, u32[]{:S(2)}, u32[]{:S(2)}) collective-permute-start(bf16[98304]{0:T(1024)(128)(2,1)S(1)} %pad_maximum_fusion.5), channel_id=1, source_target_pairs={{0,64},{16,80},{32,96},{48,112},{64,128},{80,144},{96,160},{112,17... | collective-permute-start | bytes 589832 | tf_op jit(solution)/shard_map/ppermute | solution.py:20
  31.3 19.0 %collective-permute-start.2 = (bf16[98304]{0:T(1024)(128)(2,1)S(1)}, bf16[98304]{0:T(1024)(128)(2,1)S(1)}, u32[]{:S(2)}, u32[]{:S(2)}) collective-permute-start(bf16[98304]{0:T(1024)(128)(2,1)S(1)} %pad_maximum_fusion.5), channel_id=1, source_target_pairs={{0,48},{16,64},{32,80},{48,96},{64,112},{80,128},{96,144},{112,160... | collective-permute-start | bytes 589832 | tf_op jit(solution)/shard_map/ppermute | solution.py:20
  36.0 18.1 %collective-permute-start.1 = (bf16[98304]{0:T(1024)(128)(2,1)S(1)}, bf16[98304]{0:T(1024)(128)(2,1)S(1)}, u32[]{:S(2)}, u32[]{:S(2)}) collective-permute-start(bf16[98304]{0:T(1024)(128)(2,1)S(1)} %pad_maximum_fusion.5), channel_id=1, source_target_pairs={{0,32},{16,48},{32,64},{48,80},{64,96},{80,112},{96,128},{112,144}... | collective-permute-start | bytes 589832 | tf_op jit(solution)/shard_map/ppermute | solution.py:20
  38.7 17.6 %collective-permute-start = (bf16[98304]{0:T(1024)(128)(2,1)S(1)}, bf16[98304]{0:T(1024)(128)(2,1)S(1)}, u32[]{:S(2)}, u32[]{:S(2)}) collective-permute-start(bf16[98304]{0:T(1024)(128)(2,1)S(1)} %pad_maximum_fusion.5), channel_id=1, source_target_pairs={{0,16},{16,32},{32,48},{48,64},{64,80},{80,96},{96,112},{112,128},... | collective-permute-start | bytes 589832 | tf_op jit(solution)/shard_map/ppermute | solution.py:20
  42.7 0.8 copy-start.5
  43.6 0.8 copy-start.6
  44.4 0.8 copy-start.7
  56.9 0.8 copy-start.4
  57.0 0.8 copy-start.8
  82.6 17.6 %collective-permute-start.5 = (bf16[98304]{0:T(1024)(128)(2,1)S(1)}, bf16[98304]{0:T(1024)(128)(2,1)S(1)}, u32[]{:S(2)}, u32[]{:S(2)}) collective-permute-start(bf16[98304]{0:T(1024)(128)(2,1)S(1)} %get-tuple-element.70), channel_id=1, source_target_pairs={{16,0},{32,16},{48,32},{64,48},{80,64},{96,80},{112,96},{128,112},... | collective-permute-start | bytes 589832 | tf_op jit(solution)/shard_map/ppermute | solution.py:20
  91.2 9.6 %collective-permute-start.6 = (bf16[98304]{0:T(1024)(128)(2,1)S(1)}, bf16[98304]{0:T(1024)(128)(2,1)S(1)}, u32[]{:S(2)}, u32[]{:S(2)}) collective-permute-start(bf16[98304]{0:T(1024)(128)(2,1)S(1)} %get-tuple-element.71), channel_id=1, source_target_pairs={{32,0},{48,16},{64,32},{80,48},{96,64},{112,80},{128,96},{144,112}... | collective-permute-start | bytes 589832 | tf_op jit(solution)/shard_map/ppermute | solution.py:20
  93.4 16.4 %collective-permute-start.7 = (bf16[98304]{0:T(1024)(128)(2,1)S(1)}, bf16[98304]{0:T(1024)(128)(2,1)S(1)}, u32[]{:S(2)}, u32[]{:S(2)}) collective-permute-start(bf16[98304]{0:T(1024)(128)(2,1)S(1)} %get-tuple-element.72), channel_id=1, source_target_pairs={{48,0},{64,16},{80,32},{96,48},{112,64},{128,80},{144,96},{160,112... | collective-permute-start | bytes 589832 | tf_op jit(solution)/shard_map/ppermute | solution.py:20
  96.3 20.8 %collective-permute-start.8 = (bf16[98304]{0:T(1024)(128)(2,1)S(1)}, bf16[98304]{0:T(1024)(128)(2,1)S(1)}, u32[]{:S(2)}, u32[]{:S(2)}) collective-permute-start(bf16[98304]{0:T(1024)(128)(2,1)S(1)} %get-tuple-element.73), channel_id=1, source_target_pairs={{64,0},{80,16},{96,32},{112,48},{128,64},{144,80},{160,96},{176,11... | collective-permute-start | bytes 589832 | tf_op jit(solution)/shard_map/ppermute | solution.py:20
  98.2 32.2 %collective-permute-start.9 = (bf16[98304]{0:T(1024)(128)(2,1)S(1)}, bf16[98304]{0:T(1024)(128)(2,1)S(1)}, u32[]{:S(2)}, u32[]{:S(2)}) collective-permute-start(bf16[98304]{0:T(1024)(128)(2,1)S(1)} %get-tuple-element.74), channel_id=1, source_target_pairs={{80,0},{96,16},{112,32},{128,48},{144,64},{160,80},{176,96},{192,1... | collective-permute-start | bytes 589832 | tf_op jit(solution)/shard_map/ppermute | solution.py:20

commit v3 on v2

--- a/solution.py
+++ b/solution.py
@@ -21,7 +21,7 @@
 
 
 def tp_sum(value, axis):
-    return jnp.sum(lax.all_gather(value, axis), axis=0)
+    return lax.psum(value, axis)
 
 
 def packed(*parts):
@@ -53,7 +53,7 @@
 def entry_weights(labels, decay_rate):
     place = as_float(jnp.arange(labels.shape[0], dtype=jnp.int32))
     return jnp.where(
-        (labels == labels[0])[None, :], jnp.exp(-decay_rate[:, None] * place[None, :]), 0.0
+        (labels == labels[:1])[None, :], jnp.exp(-decay_rate[:, None] * place[None, :]), 0.0
     )
 
 
@@ -61,48 +61,42 @@
     count = labels.shape[0]
     place = as_float(jnp.arange(count, dtype=jnp.int32))
     return jnp.where(
-        (labels == labels[-1])[None, :],
+        (labels == labels[-1:])[None, :],
         jnp.exp(-decay_rate[:, None] * (count - 1 - place)[None, :]),
         0.0,
     )
 
 
-def forward_element(keys, values, labels, next_label, decay_rate):
+def forward_summary(keys, values, labels, link, decay_rate):
     count = labels.shape[0]
     place = as_float(jnp.arange(count, dtype=jnp.int32))
-    link = labels[-1] == next_label
     weight = jnp.where(
-        (labels == labels[-1])[None, :] & link,
+        (labels == labels[-1:])[None, :] & link[None, :],
         jnp.exp(-decay_rate[:, None] * (count - place)[None, :]),
         0.0,
     )
-    summary = jnp.einsum(
+    return jnp.einsum(
         "thd,the->hde",
         as_float(keys) * weight.T[:, :, None],
         as_float(values),
         precision=HIGH_PRECISION,
     )
-    factor = jnp.where(labels[0] == next_label, jnp.exp(-decay_rate * count), 0.0)
-    return (factor, summary)
-
-
-def backward_element(queries, grads, labels, prev_label, decay_rate):
+
+
+def backward_summary(queries, grads, labels, link, decay_rate):
     count = labels.shape[0]
     place = as_float(jnp.arange(count, dtype=jnp.int32))
-    link = labels[0] == prev_label
     weight = jnp.where(
-        (labels == labels[0])[None, :] & link,
+        (labels == labels[:1])[None, :] & link[None, :],
         jnp.exp(-decay_rate[:, None] * (place + 1.0)[None, :]),
         0.0,
     )
-    summary = jnp.einsum(
+    return jnp.einsum(
         "thd,the->hde",
         as_float(queries) * weight.T[:, :, None],
         as_float(grads),
         precision=HIGH_PRECISION,
     )
-    factor = jnp.where(link & (labels[0] == labels[-1]), jnp.exp(-decay_rate * count), 0.0)
-    return (factor, summary)
 
 
 def score_grads(probs, grads, value_part, delta):
@@ -137,8 +131,6 @@
     )
     window_labels = jnp.broadcast_to(window_blocks[:, None], (window_blocks.shape[0], BLK)).reshape(-1)
     own_labels = window_labels[REACH * tokens : (REACH + 1) * tokens]
-    prev_label = window_labels[REACH * tokens - 1]
-    next_label = window_labels[(REACH + 1) * tokens]
     key_labels = window_labels[tokens : (REACH + 1) * tokens]
 
     def split_heads(array):
@@ -151,31 +143,29 @@
     soft_keys = split_heads(soft_key)
     soft_values = split_heads(soft_value)
     soft_grads = split_heads(soft_grad)
-    _, summary = forward_element(keys, values, own_labels, next_label, decay_rate)
     span = 2 * REACH + 1
     firsts = window_blocks[::blocks_each]
     lasts = window_blocks[blocks_each - 1 :: blocks_each]
+    summary = forward_summary(
+        keys, values, own_labels, lasts[REACH : REACH + 1] == firsts[REACH + 1 : REACH + 2], decay_rate
+    )
     full_decay = jnp.exp(-decay_rate * tokens)
-    ahead = [
-        jnp.where(firsts[at] == firsts[at + 1], full_decay, 0.0) for at in range(span - 1)
-    ]
-    behind = [None] + [
-        jnp.where((firsts[at] == lasts[at - 1]) & (firsts[at] == lasts[at]), full_decay, 0.0)
-        for at in range(1, span)
-    ]
+    ahead = jnp.where((firsts[:-1] == firsts[1:])[:, None], full_decay[None, :], 0.0)
+    behind = jnp.where(
+        ((firsts[1:] == lasts[:-1]) & (firsts[1:] == lasts[1:]))[:, None], full_decay[None, :], 0.0
+    )
     kv_shape = soft_keys.shape
     state_shape = summary.shape
     forward_pack = packed(soft_keys, soft_values, summary.astype(jnp.bfloat16))
     received = []
     state_in = jnp.zeros_like(summary)
-    chain = jnp.ones_like(decay_rate)
     for back in range(1, REACH):
         got_key, got_value, got_state = unpacked(
             shifted(forward_pack, "seq", back), (kv_shape, kv_shape, state_shape)
         )
         received.append((got_key, got_value))
+        chain = jnp.prod(ahead[REACH - back + 1 : REACH], axis=0)
         state_in = state_in + chain[:, None, None] * as_float(got_state)
-        chain = chain * ahead[REACH - back]
     decay = decay_matrix(own_labels, decay_rate)
     scores = jnp.einsum("thd,shd->hts", queries, keys, preferred_element_type=jnp.float32)
     weights = (decay * scores).astype(jnp.bfloat16)
@@ -194,7 +184,9 @@
         jnp.bfloat16
     )
     grad_heads = split_heads(norm_grad)
-    _, back_summary = backward_element(queries, grad_heads, own_labels, prev_label, decay_rate)
+    back_summary = backward_summary(
+        queries, grad_heads, own_labels, firsts[REACH : REACH + 1] == lasts[REACH - 1 : REACH], decay_rate
+    )
     back_state = back_summary.astype(jnp.bfloat16)
     grad_scores_lin = jnp.einsum(
         "thd,shd->hts", grad_heads, values, preferred_element_type=jnp.float32
@@ -256,7 +248,6 @@
     soft_key_grad = key_terms[(REACH - 1) * tokens :]
     soft_value_grad = value_terms[(REACH - 1) * tokens :]
     reverse_in = jnp.zeros_like(back_summary)
-    chain = jnp.ones_like(decay_rate)
     for back in range(1, REACH):
         lower = (REACH - 1 - back) * tokens
         backward_pack = packed(
@@ -269,8 +260,8 @@
         )
         soft_key_grad = soft_key_grad + as_float(got_key)
         soft_value_grad = soft_value_grad + as_float(got_value)
+        chain = jnp.prod(behind[REACH : REACH + back - 1], axis=0)
         reverse_in = reverse_in + chain[:, None, None] * as_float(got_state)
-        chain = chain * behind[REACH + back]
     lin_key_grad = lin_key_grad + (
         jnp.einsum("she,hde->shd", as_float(values), reverse_in, precision=HIGH_PRECISION)
         * leave.T[:, :, None]

time: 137 us -> 144 us (1.051)
  blocking collectives: 18.1 us -> 33.5 us
  between operations: 14.1 us -> 3.95 us
  starting transfers between devices: 40 us -> 41.8 us
    psum x0 -> x1, blocking collectives: none -> 33.5 us  [tp_sum(): return lax.psum(value, axis)]
    all_gather x1 -> x0, blocking collectives: 18.1 us -> none  [tp_sum(): return jnp.sum(lax.all_gather(value, axis), axis=0)]
    ppermute x10, starting transfers between devices: 40 us -> 41.8 us  [shifted(): lax.ppermute(value, axis, [(source, source + steps) for source in range(f...]
    unnamed x41 -> x43, local copies, waits for them, and re-layouts: 10 us -> 11 us
where the time goes in v3:
time: 144 us; the launch traced here: 143 us
  starting transfers between devices  41.8 us (29%)
  waiting for transfers between devices  39.8 us (28%)
  blocking collectives  33.5 us (23%)
  local copies, waits for them, and re-layouts  14.4 us (10%)
  matrix products  6.12 us (4%)
  between operations  3.95 us (3%)
  other arithmetic  3.26 us (2%)
    ppermute x10, starting transfers between devices, shifted(): lax.ppermute(value, axis, [(source, source + steps) for source in range(f...  41.8 us
    ppermute x10, waiting for transfers between devices, shifted(): lax.ppermute(value, axis, [(source, source + steps) for source in range(f...  39.8 us
    psum x1, blocking collectives, tp_sum(): return lax.psum(value, axis)  33.5 us
    unnamed x43, local copies, waits for them, and re-layouts  11 us
  transfers between devices with their start and end apart: 10, of which 7 were waited for; matrix products, arithmetic and copies ran while one was open for 2% of the time, Pallas kernels for 0%

profile of v3, /device:TPU:321, one launch (start us, length us, event | category | flops | bytes accessed | tf_op | source)
XLA Modules:
  0.0 142.7 jit_solution(13414870239478945077)
XLA Ops:
  0.7 0.6 copy-done.10
  1.4 0.6 copy-done.9
  2.2 0.6 fusion.81
  5.4 0.9 copy.141
  6.4 0.8 copy-done.1
  7.6 8.0 %collective-permute-start.4 = (bf16[98304]{0:T(1024)(128)(2,1)S(1)}, bf16[98304]{0:T(1024)(128)(2,1)S(1)}, u32[]{:S(2)}, u32[]{:S(2)}) collective-permute-start(bf16[98304]{0:T(1024)(128)(2,1)S(1)} %pad_maximum_fusion.5), channel_id=1, source_target_pairs={{0,80},{16,96},{32,112},{48,128},{64,144},{80,160},{96,176},{112,1... | collective-permute-start | bytes 589832 | tf_op jit(solution)/shard_map/ppermute | solution.py:20
  15.6 4.9 %collective-permute-start.3 = (bf16[98304]{0:T(1024)(128)(2,1)S(1)}, bf16[98304]{0:T(1024)(128)(2,1)S(1)}, u32[]{:S(2)}, u32[]{:S(2)}) collective-permute-start(bf16[98304]{0:T(1024)(128)(2,1)S(1)} %pad_maximum_fusion.5), channel_id=1, source_target_pairs={{0,64},{16,80},{32,96},{48,112},{64,128},{80,144},{96,160},{112,17... | collective-permute-start | bytes 589832 | tf_op jit(solution)/shard_map/ppermute | solution.py:20
  20.5 4.8 %collective-permute-start.2 = (bf16[98304]{0:T(1024)(128)(2,1)S(1)}, bf16[98304]{0:T(1024)(128)(2,1)S(1)}, u32[]{:S(2)}, u32[]{:S(2)}) collective-permute-start(bf16[98304]{0:T(1024)(128)(2,1)S(1)} %pad_maximum_fusion.5), channel_id=1, source_target_pairs={{0,48},{16,64},{32,80},{48,96},{64,112},{80,128},{96,144},{112,160... | collective-permute-start | bytes 589832 | tf_op jit(solution)/shard_map/ppermute | solution.py:20
  25.3 2.6 %collective-permute-start.1 = (bf16[98304]{0:T(1024)(128)(2,1)S(1)}, bf16[98304]{0:T(1024)(128)(2,1)S(1)}, u32[]{:S(2)}, u32[]{:S(2)}) collective-permute-start(bf16[98304]{0:T(1024)(128)(2,1)S(1)} %pad_maximum_fusion.5), channel_id=1, source_target_pairs={{0,32},{16,48},{32,64},{48,80},{64,96},{80,112},{96,128},{112,144}... | collective-permute-start | bytes 589832 | tf_op jit(solution)/shard_map/ppermute | solution.py:20
  28.0 3.2 %collective-permute-start = (bf16[98304]{0:T(1024)(128)(2,1)S(1)}, bf16[98304]{0:T(1024)(128)(2,1)S(1)}, u32[]{:S(2)}, u32[]{:S(2)}) collective-permute-start(bf16[98304]{0:T(1024)(128)(2,1)S(1)} %pad_maximum_fusion.5), channel_id=1, source_target_pairs={{0,16},{16,32},{32,48},{48,64},{64,80},{80,96},{96,112},{112,128},... | collective-permute-start | bytes 589832 | tf_op jit(solution)/shard_map/ppermute | solution.py:20
  31.6 0.7 copy-done.3
  32.4 0.7 slice_compare_fusion
  33.3 0.7 copy-done.6
  34.2 0.7 copy-done.7
  35.3 0.3 fusion.25
  35.8 3.7 %collective-permute-done.2 = bf16[98304]{0:T(1024)(128)(2,1)S(1)} collective-permute-done((bf16[98304]{0:T(1024)(128)(2,1)S(1)}, bf16[98304]{0:T(1024)(128)(2,1)S(1)}, u32[]{:S(2)}, u32[]{:S(2)}) %collective-permute-start.2) | collective-permute-done | bytes 196640 | tf_op jit(solution)/shard_map/ppermute | solution.py:20
  39.6 3.8 %collective-permute-done.1 = bf16[98304]{0:T(1024)(128)(2,1)S(1)} collective-permute-done((bf16[98304]{0:T(1024)(128)(2,1)S(1)}, bf16[98304]{0:T(1024)(128)(2,1)S(1)}, u32[]{:S(2)}, u32[]{:S(2)}) %collective-permute-start.1) | collective-permute-done | bytes 196640 | tf_op jit(solution)/shard_map/ppermute | solution.py:20
  43.4 2.1 %collective-permute-done = bf16[98304]{0:T(1024)(128)(2,1)S(1)} collective-permute-done((bf16[98304]{0:T(1024)(128)(2,1)S(1)}, bf16[98304]{0:T(1024)(128)(2,1)S(1)}, u32[]{:S(2)}, u32[]{:S(2)}) %collective-permute-start) | collective-permute-done | bytes 196640 | tf_op jit(solution)/shard_map/ppermute | solution.py:20
  45.7 0.3 fusion.16
  46.0 0.2 multiply_reduce_fusion.1
  46.3 0.7 copy-done.4
  47.2 33.5 %psum.7 = f32[2,128]{1,0:T(2,128)S(1)} all-reduce(f32[2,128]{1,0:T(2,128)S(1)} %pad_maximum_fusion.6), channel_id=1, replica_groups=mesh['seq'=64,'tp'=16] {'tp'}, use_global_device_ids=true, to_apply=%region_5.6 | all-reduce | flops 256 | bytes 2048 | tf_op jit(solution)/shard_map/psum | solution.py:24
  80.9 0.2 fusion.20
  81.5 0.7 copy.119
  82.2 0.3 convolution_convert_fusion
  82.8 0.4 fusion.82
  83.2 1.5 %fusion.83 = (bf16[768,2,128]{0,2,1:T(8,128)(2,1)S(1)}, f32[768,2,128]{0,2,1:T(8,128)}) fusion(bf16[128,2,128]{0,2,1:T(8,128)(2,1)S(1)} %bitcast.309, f32[2,128]{1,0:T(2,128)S(1)} %get-tuple-element.78, bf16[768,2,128]{2,0,1:T(8,128)(2,1)S(1)} %constant_dynamic-update-slice_fusion, bf16[128,2,128]{0,2,1:T(8,128)(2,1)S(1)} %bitcast.252, ...), kind=kOutput, calls=%fused_computation.165 | convolution fusion | flops 101843968 | bytes 1803264 | tf_op jit(solution)/shard_map/htu,thd->uhd/dot_general | solution.py:245
  84.7 0.7 fusion.24
  86.1 0.3 fusion.8
  86.4 0.3 fusion.84
  87.1 9.3 %collective-permute-start.5 = (bf16[98304]{0:T(1024)(128)(2,1)S(1)}, bf16[98304]{0:T(1024)(128)(2,1)S(1)}, u32[]{:S(2)}, u32[]{:S(2)}) collective-permute-start(bf16[98304]{0:T(1024)(128)(2,1)S(1)} %get-tuple-element.58), channel_id=1, source_target_pairs={{16,0},{32,16},{48,32},{64,48},{80,64},{96,80},{112,96},{128,112},... | collective-permute-start | bytes 589832 | tf_op jit(solution)/shard_map/ppermute | solution.py:20
  96.5 0.3 fusion.18
  96.8 0.7 copy.122
  97.5 2.1 %collective-permute-start.6 = (bf16[98304]{0:T(1024)(128)(2,1)S(1)}, bf16[98304]{0:T(1024)(128)(2,1)S(1)}, u32[]{:S(2)}, u32[]{:S(2)}) collective-permute-start(bf16[98304]{0:T(1024)(128)(2,1)S(1)} %get-tuple-element.59), channel_id=1, source_target_pairs={{32,0},{48,16},{64,32},{80,48},{96,64},{112,80},{128,96},{144,112}... | collective-permute-start | bytes 589832 | tf_op jit(solution)/shard_map/ppermute | solution.py:20
  99.7 2.9 %collective-permute-start.7 = (bf16[98304]{0:T(1024)(128)(2,1)S(1)}, bf16[98304]{0:T(1024)(128)(2,1)S(1)}, u32[]{:S(2)}, u32[]{:S(2)}) collective-permute-start(bf16[98304]{0:T(1024)(128)(2,1)S(1)} %get-tuple-element.60), channel_id=1, source_target_pairs={{48,0},{64,16},{80,32},{96,48},{112,64},{128,80},{144,96},{160,112... | collective-permute-start | bytes 589832 | tf_op jit(solution)/shard_map/ppermute | solution.py:20
  102.6 1.9 %collective-permute-start.8 = (bf16[98304]{0:T(1024)(128)(2,1)S(1)}, bf16[98304]{0:T(1024)(128)(2,1)S(1)}, u32[]{:S(2)}, u32[]{:S(2)}) collective-permute-start(bf16[98304]{0:T(1024)(128)(2,1)S(1)} %get-tuple-element.61), channel_id=1, source_target_pairs={{64,0},{80,16},{96,32},{112,48},{128,64},{144,80},{160,96},{176,11... | collective-permute-start | bytes 589832 | tf_op jit(solution)/shard_map/ppermute | solution.py:20
  104.5 1.9 %collective-permute-start.9 = (bf16[98304]{0:T(1024)(128)(2,1)S(1)}, bf16[98304]{0:T(1024)(128)(2,1)S(1)}, u32[]{:S(2)}, u32[]{:S(2)}) collective-permute-start(bf16[98304]{0:T(1024)(128)(2,1)S(1)} %get-tuple-element.62), channel_id=1, source_target_pairs={{80,0},{96,16},{112,32},{128,48},{144,64},{160,80},{176,96},{192,1... | collective-permute-start | bytes 589832 | tf_op jit(solution)/shard_map/ppermute | solution.py:20
  106.5 0.6 collective-permute-done.6
  107.1 9.0 %collective-permute-done.7 = bf16[98304]{0:T(1024)(128)(2,1)S(1)} collective-permute-done((bf16[98304]{0:T(1024)(128)(2,1)S(1)}, bf16[98304]{0:T(1024)(128)(2,1)S(1)}, u32[]{:S(2)}, u32[]{:S(2)}) %collective-permute-start.7) | collective-permute-done | bytes 196640 | tf_op jit(solution)/shard_map/ppermute | solution.py:20
  116.1 7.2 %collective-permute-done.8 = bf16[98304]{0:T(1024)(128)(2,1)S(1)} collective-permute-done((bf16[98304]{0:T(1024)(128)(2,1)S(1)}, bf16[98304]{0:T(1024)(128)(2,1)S(1)}, u32[]{:S(2)}, u32[]{:S(2)}) %collective-permute-start.8) | collective-permute-done | bytes 196640 | tf_op jit(solution)/shard_map/ppermute | solution.py:20
  123.4 13.3 %collective-permute-done.9 = bf16[98304]{0:T(1024)(128)(2,1)S(1)} collective-permute-done((bf16[98304]{0:T(1024)(128)(2,1)S(1)}, bf16[98304]{0:T(1024)(128)(2,1)S(1)}, u32[]{:S(2)}, u32[]{:S(2)}) %collective-permute-start.9) | collective-permute-done | bytes 196640 | tf_op jit(solution)/shard_map/ppermute | solution.py:20
  136.9 0.3 fusion.11
  137.2 0.3 fusion.13
  138.4 0.7 copy.123
  139.2 1.0 fusion.31
  140.2 0.7 copy.124
  141.3 0.7 copy.120
  142.0 0.7 copy.121
  (109 shorter events, 5.9 us)
Async XLA Ops:
  0.6 6.7 %copy-start = (bf16[128,256]{1,0:T(8,128)(2,1)S(1)}, bf16[128,256]{1,0:T(8,128)(2,1)}, u32[]{:S(2)}) copy-start(bf16[128,256]{1,0:T(8,128)(2,1)} %param.13) | copy-start | bytes 196612
  0.7 0.7 copy-start.10
  1.4 0.7 copy-start.9
  5.4 0.9 copy-start.2
  6.3 0.8 copy-start.1
  7.6 28.2 %collective-permute-start.4 = (bf16[98304]{0:T(1024)(128)(2,1)S(1)}, bf16[98304]{0:T(1024)(128)(2,1)S(1)}, u32[]{:S(2)}, u32[]{:S(2)}) collective-permute-start(bf16[98304]{0:T(1024)(128)(2,1)S(1)} %pad_maximum_fusion.5), channel_id=1, source_target_pairs={{0,80},{16,96},{32,112},{48,128},{64,144},{80,160},{96,176},{112,1... | collective-permute-start | bytes 589832 | tf_op jit(solution)/shard_map/ppermute | solution.py:20
  15.6 20.2 %collective-permute-start.3 = (bf16[98304]{0:T(1024)(128)(2,1)S(1)}, bf16[98304]{0:T(1024)(128)(2,1)S(1)}, u32[]{:S(2)}, u32[]{:S(2)}) collective-permute-start(bf16[98304]{0:T(1024)(128)(2,1)S(1)} %pad_maximum_fusion.5), channel_id=1, source_target_pairs={{0,64},{16,80},{32,96},{48,112},{64,128},{80,144},{96,160},{112,17... | collective-permute-start | bytes 589832 | tf_op jit(solution)/shard_map/ppermute | solution.py:20
  20.5 19.0 %collective-permute-start.2 = (bf16[98304]{0:T(1024)(128)(2,1)S(1)}, bf16[98304]{0:T(1024)(128)(2,1)S(1)}, u32[]{:S(2)}, u32[]{:S(2)}) collective-permute-start(bf16[98304]{0:T(1024)(128)(2,1)S(1)} %pad_maximum_fusion.5), channel_id=1, source_target_pairs={{0,48},{16,64},{32,80},{48,96},{64,112},{80,128},{96,144},{112,160... | collective-permute-start | bytes 589832 | tf_op jit(solution)/shard_map/ppermute | solution.py:20
  25.3 18.1 %collective-permute-start.1 = (bf16[98304]{0:T(1024)(128)(2,1)S(1)}, bf16[98304]{0:T(1024)(128)(2,1)S(1)}, u32[]{:S(2)}, u32[]{:S(2)}) collective-permute-start(bf16[98304]{0:T(1024)(128)(2,1)S(1)} %pad_maximum_fusion.5), channel_id=1, source_target_pairs={{0,32},{16,48},{32,64},{48,80},{64,96},{80,112},{96,128},{112,144}... | collective-permute-start | bytes 589832 | tf_op jit(solution)/shard_map/ppermute | solution.py:20
  28.0 17.6 %collective-permute-start = (bf16[98304]{0:T(1024)(128)(2,1)S(1)}, bf16[98304]{0:T(1024)(128)(2,1)S(1)}, u32[]{:S(2)}, u32[]{:S(2)}) collective-permute-start(bf16[98304]{0:T(1024)(128)(2,1)S(1)} %pad_maximum_fusion.5), channel_id=1, source_target_pairs={{0,16},{16,32},{32,48},{48,64},{64,80},{80,96},{96,112},{112,128},... | collective-permute-start | bytes 589832 | tf_op jit(solution)/shard_map/ppermute | solution.py:20
  31.4 0.8 copy-start.3
  32.3 0.9 copy-start.5
  33.2 0.8 copy-start.6
  34.0 0.8 copy-start.7
  46.2 0.8 copy-start.4
  46.2 0.8 copy-start.8
  87.1 19.3 %collective-permute-start.5 = (bf16[98304]{0:T(1024)(128)(2,1)S(1)}, bf16[98304]{0:T(1024)(128)(2,1)S(1)}, u32[]{:S(2)}, u32[]{:S(2)}) collective-permute-start(bf16[98304]{0:T(1024)(128)(2,1)S(1)} %get-tuple-element.58), channel_id=1, source_target_pairs={{16,0},{32,16},{48,32},{64,48},{80,64},{96,80},{112,96},{128,112},... | collective-permute-start | bytes 589832 | tf_op jit(solution)/shard_map/ppermute | solution.py:20
  97.5 9.6 %collective-permute-start.6 = (bf16[98304]{0:T(1024)(128)(2,1)S(1)}, bf16[98304]{0:T(1024)(128)(2,1)S(1)}, u32[]{:S(2)}, u32[]{:S(2)}) collective-permute-start(bf16[98304]{0:T(1024)(128)(2,1)S(1)} %get-tuple-element.59), channel_id=1, source_target_pairs={{32,0},{48,16},{64,32},{80,48},{96,64},{112,80},{128,96},{144,112}... | collective-permute-start | bytes 589832 | tf_op jit(solution)/shard_map/ppermute | solution.py:20
  99.7 16.5 %collective-permute-start.7 = (bf16[98304]{0:T(1024)(128)(2,1)S(1)}, bf16[98304]{0:T(1024)(128)(2,1)S(1)}, u32[]{:S(2)}, u32[]{:S(2)}) collective-permute-start(bf16[98304]{0:T(1024)(128)(2,1)S(1)} %get-tuple-element.60), channel_id=1, source_target_pairs={{48,0},{64,16},{80,32},{96,48},{112,64},{128,80},{144,96},{160,112... | collective-permute-start | bytes 589832 | tf_op jit(solution)/shard_map/ppermute | solution.py:20
  102.6 20.8 %collective-permute-start.8 = (bf16[98304]{0:T(1024)(128)(2,1)S(1)}, bf16[98304]{0:T(1024)(128)(2,1)S(1)}, u32[]{:S(2)}, u32[]{:S(2)}) collective-permute-start(bf16[98304]{0:T(1024)(128)(2,1)S(1)} %get-tuple-element.61), channel_id=1, source_target_pairs={{64,0},{80,16},{96,32},{112,48},{128,64},{144,80},{160,96},{176,11... | collective-permute-start | bytes 589832 | tf_op jit(solution)/shard_map/ppermute | solution.py:20
  104.5 32.2 %collective-permute-start.9 = (bf16[98304]{0:T(1024)(128)(2,1)S(1)}, bf16[98304]{0:T(1024)(128)(2,1)S(1)}, u32[]{:S(2)}, u32[]{:S(2)}) collective-permute-start(bf16[98304]{0:T(1024)(128)(2,1)S(1)} %get-tuple-element.62), channel_id=1, source_target_pairs={{80,0},{96,16},{112,32},{128,48},{144,64},{160,80},{176,96},{192,1... | collective-permute-start | bytes 589832 | tf_op jit(solution)/shard_map/ppermute | solution.py:20

commit v4 on v3

--- a/solution.py
+++ b/solution.py
@@ -21,7 +21,7 @@
 
 
 def tp_sum(value, axis):
-    return lax.psum(value, axis)
+    return jnp.sum(lax.all_gather(value, axis), axis=0)
 
 
 def packed(*parts):
@@ -156,13 +156,23 @@
     )
     kv_shape = soft_keys.shape
     state_shape = summary.shape
-    forward_pack = packed(soft_keys, soft_values, summary.astype(jnp.bfloat16))
+    unit = packed(soft_keys, soft_values, summary.astype(jnp.bfloat16))
+    size = unit.shape[0]
+    two_back = shifted(unit, "seq", 2)
+    four_back = shifted(two_back, "seq", 2)
+    odd_back = shifted(jnp.concatenate([unit, two_back]), "seq", 1)
+    five_back = shifted(four_back, "seq", 1)
+    arrived = {
+        1: odd_back[:size],
+        2: two_back,
+        3: odd_back[size:],
+        4: four_back,
+        5: five_back,
+    }
     received = []
     state_in = jnp.zeros_like(summary)
     for back in range(1, REACH):
-        got_key, got_value, got_state = unpacked(
-            shifted(forward_pack, "seq", back), (kv_shape, kv_shape, state_shape)
-        )
+        got_key, got_value, got_state = unpacked(arrived[back], (kv_shape, kv_shape, state_shape))
         received.append((got_key, got_value))
         chain = jnp.prod(ahead[REACH - back + 1 : REACH], axis=0)
         state_in = state_in + chain[:, None, None] * as_float(got_state)
@@ -247,21 +257,33 @@
     )
     soft_key_grad = key_terms[(REACH - 1) * tokens :]
     soft_value_grad = value_terms[(REACH - 1) * tokens :]
-    reverse_in = jnp.zeros_like(back_summary)
+    items = {}
     for back in range(1, REACH):
         lower = (REACH - 1 - back) * tokens
-        backward_pack = packed(
-            key_terms[lower : lower + tokens].astype(jnp.bfloat16),
-            value_terms[lower : lower + tokens].astype(jnp.bfloat16),
-            back_state,
+        chain = jnp.prod(behind[REACH - back : REACH - 1], axis=0)
+        items[back] = packed(
+            key_terms[lower : lower + tokens],
+            value_terms[lower : lower + tokens],
+            chain[:, None, None] * back_summary,
         )
-        got_key, got_value, got_state = unpacked(
-            shifted(backward_pack, "seq", -back), (kv_shape, kv_shape, state_shape)
+    size = items[1].shape[0]
+
+    def wire(value):
+        return value.astype(jnp.bfloat16)
+
+    first = as_float(shifted(wire(jnp.concatenate([items[5], items[3], items[1]])), "seq", -1))
+    second = as_float(
+        shifted(
+            wire(jnp.concatenate([items[2] + first[size : 2 * size], items[4] + first[:size]])),
+            "seq",
+            -2,
         )
-        soft_key_grad = soft_key_grad + as_float(got_key)
-        soft_value_grad = soft_value_grad + as_float(got_value)
-        chain = jnp.prod(behind[REACH : REACH + back - 1], axis=0)
-        reverse_in = reverse_in + chain[:, None, None] * as_float(got_state)
+    )
+    third = as_float(shifted(wire(second[size:]), "seq", -2))
+    total = first[2 * size :] + second[:size] + third
+    got_key, got_value, reverse_in = unpacked(total, (kv_shape, kv_shape, state_shape))
+    soft_key_grad = soft_key_grad + got_key
+    soft_value_grad = soft_value_grad + got_value
     lin_key_grad = lin_key_grad + (
         jnp.einsum("she,hde->shd", as_float(values), reverse_in, precision=HIGH_PRECISION)
         * leave.T[:, :, None]

time: 144 us -> 112 us (0.78)
  the two profiles are of different devices: /device:TPU:321 before, /device:TPU:1 now
where the time goes in v4:
time: 112 us; the launch traced here: 111 us
  waiting for transfers between devices  36.3 us (32%)
  starting transfers between devices  31.9 us (28%)
  blocking collectives  14.8 us (13%)
  local copies, waits for them, and re-layouts  11.2 us (10%)
  matrix products  8.03 us (7%)
  other arithmetic  5.19 us (5%)
  between operations  4.03 us (4%)
    ppermute x7, waiting for transfers between devices, shifted(): lax.ppermute(value, axis, [(source, source + steps) for source in range(f...  36.3 us
    ppermute x7, starting transfers between devices, shifted(): lax.ppermute(value, axis, [(source, source + steps) for source in range(f...  31.9 us
    all_gather x1, blocking collectives, tp_sum(): return jnp.sum(lax.all_gather(value, axis), axis=0)  14.8 us
    unnamed x57, local copies, waits for them, and re-layouts  7.31 us
  transfers between devices with their start and end apart: 7, of which 6 were waited for; matrix products, arithmetic and copies ran while one was open for 5% of the time, Pallas kernels for 0%

profile of v4, /device:TPU:1, one launch (start us, length us, event | category | flops | bytes accessed | tf_op | source)
XLA Modules:
  0.0 111.4 jit_solution(9459887278279303254)
XLA Ops:
  0.8 0.7 multiply_exponential_fusion.2
  1.5 0.7 pad_add_fusion
  2.3 0.6 fusion.70
  5.5 0.9 copy.197
  6.4 0.9 copy.196
  7.3 1.0 copy.233
  8.3 0.2 convolution_convert_fusion
  8.6 4.4 %collective-permute-start = (bf16[98304]{0:T(1024)(128)(2,1)S(1)}, bf16[98304]{0:T(1024)(128)(2,1)S(1)}, u32[]{:S(2)}, u32[]{:S(2)}) collective-permute-start(bf16[98304]{0:T(1024)(128)(2,1)S(1)} %pad_maximum_fusion.2), channel_id=1, source_target_pairs={{0,32},{16,48},{32,64},{48,80},{64,96},{80,112},{96,128},{112,144}... | collective-permute-start | bytes 589832 | tf_op jit(solution)/shard_map/ppermute | solution.py:20
  13.5 0.7 slice_compare_fusion
  14.9 0.3 fusion.28
  15.2 0.2 fusion.20
  15.6 15.6 %collective-permute-start.1 = (bf16[196608]{0:T(1024)(128)(2,1)S(1)}, bf16[196608]{0:T(1024)(128)(2,1)S(1)}, u32[]{:S(2)}, u32[]{:S(2)}) collective-permute-start(bf16[196608]{0:T(1024)(128)(2,1)S(1)} %pad_maximum_fusion), channel_id=1, source_target_pairs={{0,16},{16,32},{32,48},{48,64},{64,80},{80,96},{96,112},{112,128},... | collective-permute-start | bytes 1179656 | tf_op jit(solution)/shard_map/ppermute | solution.py:20
  31.2 1.3 %collective-permute-start.2 = (bf16[98304]{0:T(1024)(128)(2,1)S(1)}, bf16[98304]{0:T(1024)(128)(2,1)S(1)}, u32[]{:S(2)}, u32[]{:S(2)}) collective-permute-start(bf16[98304]{0:T(1024)(128)(2,1)S(1)} %collective-permute-done), channel_id=1, source_target_pairs={{0,32},{16,48},{32,64},{48,80},{64,96},{80,112},{96,128},{112,144}... | collective-permute-start | bytes 589832 | tf_op jit(solution)/shard_map/ppermute | solution.py:20
  32.6 7.6 %collective-permute-done.2 = bf16[98304]{0:T(1024)(128)(2,1)S(1)} collective-permute-done((bf16[98304]{0:T(1024)(128)(2,1)S(1)}, bf16[98304]{0:T(1024)(128)(2,1)S(1)}, u32[]{:S(2)}, u32[]{:S(2)}) %collective-permute-start.2) | collective-permute-done | bytes 196640 | tf_op jit(solution)/shard_map/ppermute | solution.py:20
  40.1 2.7 %collective-permute-start.3 = (bf16[98304]{0:T(1024)(128)(2,1)S(1)}, bf16[98304]{0:T(1024)(128)(2,1)S(1)}, u32[]{:S(2)}, u32[]{:S(2)}) collective-permute-start(bf16[98304]{0:T(1024)(128)(2,1)S(1)} %collective-permute-done.2), channel_id=1, source_target_pairs={{0,16},{16,32},{32,48},{48,64},{64,80},{80,96},{96,112},{112,128},... | collective-permute-start | bytes 589832 | tf_op jit(solution)/shard_map/ppermute | solution.py:20
  42.9 2.6 %collective-permute-done.3 = bf16[98304]{0:T(1024)(128)(2,1)S(1)} collective-permute-done((bf16[98304]{0:T(1024)(128)(2,1)S(1)}, bf16[98304]{0:T(1024)(128)(2,1)S(1)}, u32[]{:S(2)}, u32[]{:S(2)}) %collective-permute-start.3) | collective-permute-done | bytes 196640 | tf_op jit(solution)/shard_map/ppermute | solution.py:20
  45.7 0.3 fusion.15
  46.0 0.2 multiply_reduce_fusion.1
  46.5 14.8 %all-gather.1 = f32[16,2,128]{2,1,0:T(2,128)S(1)} all-gather(f32[1,2,128]{2,1,0:T(2,128)S(1)} %maximum_bitcast_fusion), channel_id=2, replica_groups=mesh['seq'=64,'tp'=16] {'tp'}, dimensions={0}, use_global_device_ids=true | all-gather | bytes 17408 | tf_op jit(solution)/shard_map/all_gather | solution.py:24
  61.8 1.3 %fusion.71 = (f32[2,128]{1,0:T(2,128)S(1)}, f32[2,128,768]{1,2,0:T(8,128)}) fusion(bf16[768,2,128]{2,0,1:T(8,128)(2,1)S(1)} %constant_dynamic-update-slice_fusion, bf16[128,2,128]{0,2,1:T(8,128)(2,1)S(1)} %bitcast.248, pred[128,768]{0,1:T(8,128)(4,1)S(1)} %fusion.28), kind=kOutput, calls=%fused_computation.161 | convolution fusion | flops 51118848 | bytes 1344512 | tf_op jit(solution)/shard_map/sub | solution.py:238
  63.1 0.6 fusion.73
  63.7 0.4 copy-done.12
  64.1 0.7 fusion.24
  65.5 1.4 %fusion.8 = bf16[2,128,768]{1,2,0:T(8,128)(2,1)S(1)} fusion(bf16[768,2,128]{2,0,1:T(8,128)(2,1)S(1)} %copy-done.12, bf16[128,2,128]{0,2,1:T(8,128)(2,1)S(1)} %bitcast.286, f32[2,128]{1,0:T(2,128)S(1)} %bitcast.289, f32[2,128,768]{1,2,0:T(8,128)} %get-tuple-element.75, f32[2,128]{1,0:T(2,128)S(1)} %get-tuple-element.74), kind=kOutput, calls=%fused_computation.12 | convolution fusion | flops 51118080 | bytes 1640448 | tf_op jit(solution)/shard_map/thd,uhd->htu/dot_general | solution.py:103
  66.9 0.3 fusion.72
  67.4 0.3 broadcast_multiply_fusion.1
  67.8 5.2 %collective-permute-start.4 = (bf16[294912]{0:T(1024)(128)(2,1)S(1)}, bf16[294912]{0:T(1024)(128)(2,1)S(1)}, u32[]{:S(2)}, u32[]{:S(2)}) collective-permute-start(bf16[294912]{0:T(1024)(128)(2,1)S(1)} %constant_dynamic-update-slice_fusion.3), channel_id=1, source_target_pairs={{16,0},{32,16},{48,32},{64,48},{80,64},{96,80},{112,96},{128,112},... | collective-permute-start | bytes 1769480 | tf_op jit(solution)/shard_map/ppermute | solution.py:20
  73.3 0.2 fusion.21
  73.6 0.2 fusion.13
  73.8 11.2 %collective-permute-done.4 = bf16[294912]{0:T(1024)(128)(2,1)S(1)} collective-permute-done((bf16[294912]{0:T(1024)(128)(2,1)S(1)}, bf16[294912]{0:T(1024)(128)(2,1)S(1)}, u32[]{:S(2)}, u32[]{:S(2)}) %collective-permute-start.4) | collective-permute-done | bytes 589856 | tf_op jit(solution)/shard_map/ppermute | solution.py:20
  85.2 0.8 pad_maximum_fusion.1
  86.0 1.3 %collective-permute-start.5 = (bf16[196608]{0:T(1024)(128)(2,1)}, bf16[196608]{0:T(1024)(128)(2,1)S(1)}, u32[]{:S(2)}, u32[]{:S(2)}) collective-permute-start(bf16[196608]{0:T(1024)(128)(2,1)} %pad_maximum_fusion.1), channel_id=1, source_target_pairs={{32,0},{48,16},{64,32},{80,48},{96,64},{112,80},{128,96},{144,112}... | collective-permute-start | bytes 1179656 | tf_op jit(solution)/shard_map/ppermute | solution.py:20
  87.2 0.2 fusion.22
  87.4 0.7 copy.175
  88.2 0.3 fusion.19
  88.5 0.7 copy.178
  89.2 8.3 %collective-permute-done.5 = bf16[196608]{0:T(1024)(128)(2,1)S(1)} collective-permute-done((bf16[196608]{0:T(1024)(128)(2,1)}, bf16[196608]{0:T(1024)(128)(2,1)S(1)}, u32[]{:S(2)}, u32[]{:S(2)}) %collective-permute-start.5) | collective-permute-done | bytes 393248 | tf_op jit(solution)/shard_map/ppermute | solution.py:20
  97.6 1.3 %collective-permute-start.6 = (bf16[98304]{0:T(1024)(128)(2,1)S(1)}, bf16[98304]{0:T(1024)(128)(2,1)S(1)}, u32[]{:S(2)}, u32[]{:S(2)}) collective-permute-start(bf16[98304]{0:T(1024)(128)(2,1)S(1)} %slice.460), channel_id=1, source_target_pairs={{32,0},{48,16},{64,32},{80,48},{96,64},{112,80},{128,96},{144,112}... | collective-permute-start | bytes 589832 | tf_op jit(solution)/shard_map/ppermute | solution.py:20
  98.9 1.0 convolution_bitcast_fusion.4
  99.9 6.5 %collective-permute-done.6 = bf16[98304]{0:T(1024)(128)(2,1)S(1)} collective-permute-done((bf16[98304]{0:T(1024)(128)(2,1)S(1)}, bf16[98304]{0:T(1024)(128)(2,1)S(1)}, u32[]{:S(2)}, u32[]{:S(2)}) %collective-permute-start.6) | collective-permute-done | bytes 196640 | tf_op jit(solution)/shard_map/ppermute | solution.py:20
  106.5 0.3 fusion.12
  106.8 0.3 fusion.18
  107.1 0.7 copy.177
  107.9 0.9 fusion.30
  108.9 0.7 copy.180
  109.8 0.7 copy.179
  110.5 0.2 fusion.23
  110.7 0.7 copy.176
  (111 shorter events, 4.1 us)
Async XLA Ops:
  0.6 7.7 %copy-start = (bf16[128,256]{1,0:T(8,128)(2,1)S(1)}, bf16[128,256]{1,0:T(8,128)(2,1)}, u32[]{:S(2)}) copy-start(bf16[128,256]{1,0:T(8,128)(2,1)} %param.13) | copy-start | bytes 196612
  0.6 12.7 %copy-start.2 = (bf16[128,256]{1,0:T(8,128)(2,1)S(1)}, bf16[128,256]{1,0:T(8,128)(2,1)}, u32[]{:S(2)}) copy-start(bf16[128,256]{1,0:T(8,128)(2,1)} %param.19) | copy-start | bytes 196612
  0.7 12.6 %copy-start.1 = (bf16[128,256]{1,0:T(8,128)(2,1)S(1)}, bf16[128,256]{1,0:T(8,128)(2,1)}, u32[]{:S(2)}) copy-start(bf16[128,256]{1,0:T(8,128)(2,1)} %param.18) | copy-start | bytes 196612
  0.7 14.5 %copy-start.4 = (bf16[128,256]{1,0:T(8,128)(2,1)S(1)}, bf16[128,256]{1,0:T(8,128)(2,1)}, u32[]{:S(2)}) copy-start(bf16[128,256]{1,0:T(8,128)(2,1)} %param.12) | copy-start | bytes 196612
  0.7 13.6 %copy-start.8 = (bf16[128,256]{1,0:T(8,128)(2,1)S(1)}, bf16[128,256]{1,0:T(8,128)(2,1)}, u32[]{:S(2)}) copy-start(bf16[128,256]{1,0:T(8,128)(2,1)} %param.11) | copy-start | bytes 196612
  0.7 13.7 %copy-start.9 = (bf16[128,256]{1,0:T(8,128)(2,1)S(1)}, bf16[128,256]{1,0:T(8,128)(2,1)}, u32[]{:S(2)}) copy-start(bf16[128,256]{1,0:T(8,128)(2,1)} %param.17) | copy-start | bytes 196612
  0.7 13.8 %copy-start.10 = (bf16[128,256]{1,0:T(8,128)(2,1)S(1)}, bf16[128,256]{1,0:T(8,128)(2,1)}, u32[]{:S(2)}) copy-start(bf16[128,256]{1,0:T(8,128)(2,1)} %param.20) | copy-start | bytes 196612
  8.6 7.0 %collective-permute-start = (bf16[98304]{0:T(1024)(128)(2,1)S(1)}, bf16[98304]{0:T(1024)(128)(2,1)S(1)}, u32[]{:S(2)}, u32[]{:S(2)}) collective-permute-start(bf16[98304]{0:T(1024)(128)(2,1)S(1)} %pad_maximum_fusion.2), channel_id=1, source_target_pairs={{0,32},{16,48},{32,64},{48,80},{64,96},{80,112},{96,128},{112,144}... | collective-permute-start | bytes 589832 | tf_op jit(solution)/shard_map/ppermute | solution.py:20
  15.4 47.7 %copy-start.6 = (bf16[2,128,128]{2,1,0:T(8,128)(2,1)}, bf16[2,128,128]{2,1,0:T(8,128)(2,1)S(1)}, u32[]{:S(2)}) copy-start(bf16[2,128,128]{2,1,0:T(8,128)(2,1)S(1)} %fusion.20) | copy-start | bytes 196612
  15.6 29.9 %collective-permute-start.1 = (bf16[196608]{0:T(1024)(128)(2,1)S(1)}, bf16[196608]{0:T(1024)(128)(2,1)S(1)}, u32[]{:S(2)}, u32[]{:S(2)}) collective-permute-start(bf16[196608]{0:T(1024)(128)(2,1)S(1)} %pad_maximum_fusion), channel_id=1, source_target_pairs={{0,16},{16,32},{32,48},{48,64},{64,80},{80,96},{96,112},{112,128},... | collective-permute-start | bytes 1179656 | tf_op jit(solution)/shard_map/ppermute | solution.py:20
  31.2 8.9 %collective-permute-start.2 = (bf16[98304]{0:T(1024)(128)(2,1)S(1)}, bf16[98304]{0:T(1024)(128)(2,1)S(1)}, u32[]{:S(2)}, u32[]{:S(2)}) collective-permute-start(bf16[98304]{0:T(1024)(128)(2,1)S(1)} %collective-permute-done), channel_id=1, source_target_pairs={{0,32},{16,48},{32,64},{48,80},{64,96},{80,112},{96,128},{112,144}... | collective-permute-start | bytes 589832 | tf_op jit(solution)/shard_map/ppermute | solution.py:20
  40.1 5.3 %collective-permute-start.3 = (bf16[98304]{0:T(1024)(128)(2,1)S(1)}, bf16[98304]{0:T(1024)(128)(2,1)S(1)}, u32[]{:S(2)}, u32[]{:S(2)}) collective-permute-start(bf16[98304]{0:T(1024)(128)(2,1)S(1)} %collective-permute-done.2), channel_id=1, source_target_pairs={{0,16},{16,32},{32,48},{48,64},{64,80},{80,96},{96,112},{112,128},... | collective-permute-start | bytes 589832 | tf_op jit(solution)/shard_map/ppermute | solution.py:20
  45.5 0.9 copy-start.3
  45.5 0.9 copy-start.13
  61.8 1.3 %copy-start.11 = (bf16[768,2,128]{2,0,1:T(8,128)(2,1)}, bf16[768,2,128]{2,0,1:T(8,128)(2,1)S(1)}, u32[]{:S(2)}) copy-start(bf16[768,2,128]{2,0,1:T(8,128)(2,1)S(1)} %constant_dynamic-update-slice_fusion.1) | copy-start | bytes 1179652
  63.1 1.0 copy-start.12
  64.1 1.1 copy-start.7
  67.8 17.2 %collective-permute-start.4 = (bf16[294912]{0:T(1024)(128)(2,1)S(1)}, bf16[294912]{0:T(1024)(128)(2,1)S(1)}, u32[]{:S(2)}, u32[]{:S(2)}) collective-permute-start(bf16[294912]{0:T(1024)(128)(2,1)S(1)} %constant_dynamic-update-slice_fusion.3), channel_id=1, source_target_pairs={{16,0},{32,16},{48,32},{64,48},{80,64},{96,80},{112,96},{128,112},... | collective-permute-start | bytes 1769480 | tf_op jit(solution)/shard_map/ppermute | solution.py:20
  86.0 11.6 %collective-permute-start.5 = (bf16[196608]{0:T(1024)(128)(2,1)}, bf16[196608]{0:T(1024)(128)(2,1)S(1)}, u32[]{:S(2)}, u32[]{:S(2)}) collective-permute-start(bf16[196608]{0:T(1024)(128)(2,1)} %pad_maximum_fusion.1), channel_id=1, source_target_pairs={{32,0},{48,16},{64,32},{80,48},{96,64},{112,80},{128,96},{144,112}... | collective-permute-start | bytes 1179656 | tf_op jit(solution)/shard_map/ppermute | solution.py:20
  97.6 8.8 %collective-permute-start.6 = (bf16[98304]{0:T(1024)(128)(2,1)S(1)}, bf16[98304]{0:T(1024)(128)(2,1)S(1)}, u32[]{:S(2)}, u32[]{:S(2)}) collective-permute-start(bf16[98304]{0:T(1024)(128)(2,1)S(1)} %slice.460), channel_id=1, source_target_pairs={{32,0},{48,16},{64,32},{80,48},{96,64},{112,80},{128,96},{144,112}... | collective-permute-start | bytes 589832 | tf_op jit(solution)/shard_map/ppermute | solution.py:20
  99.9 6.9 %copy-start.5 = (bf16[128,256]{1,0:T(8,128)(2,1)S(1)}, bf16[128,256]{1,0:T(8,128)(2,1)}, u32[]{:S(2)}) copy-start(bf16[128,256]{1,0:T(8,128)(2,1)} %param.12) | copy-start | bytes 196612

commit v5 on v4

--- a/solution.py
+++ b/solution.py
@@ -21,7 +21,21 @@
 
 
 def tp_sum(value, axis):
-    return jnp.sum(lax.all_gather(value, axis), axis=0)
+    count = lax.axis_size(axis)
+    inner = math.isqrt(count)
+    if inner * inner != count:
+        return jnp.sum(lax.all_gather(value, axis), axis=0)
+    for stride in (1, inner):
+        parts = [value]
+        for step in range(1, inner):
+            pairs = []
+            for source in range(count):
+                digit = (source // stride) % inner
+                target = source + (((digit + step) % inner) - digit) * stride
+                pairs.append((source, target))
+            parts.append(lax.ppermute(value, axis, pairs))
+        value = sum(parts[1:], parts[0])
+    return value
 
 
 def packed(*parts):
@@ -186,38 +200,6 @@
     lin_out = inner + carried * entry.T[:, :, None]
     flat = lin_out.reshape(tokens, heads * HD)
     scaled_grad = norm_gain[None, :] * as_float(lin_grad)
-    sums = tp_sum(jnp.stack([jnp.sum(flat * flat, axis=1), jnp.sum(flat * scaled_grad, axis=1)]), "tp")
-    width = lax.axis_size("tp") * heads * HD
-    inverse = lax.rsqrt(sums[0] / width + NORM_EPS)
-    cross = sums[1] / width
-    norm_grad = (inverse[:, None] * scaled_grad - flat * (inverse**3 * cross)[:, None]).astype(
-        jnp.bfloat16
-    )
-    grad_heads = split_heads(norm_grad)
-    back_summary = backward_summary(
-        queries, grad_heads, own_labels, firsts[REACH : REACH + 1] == lasts[REACH - 1 : REACH], decay_rate
-    )
-    back_state = back_summary.astype(jnp.bfloat16)
-    grad_scores_lin = jnp.einsum(
-        "thd,shd->hts", grad_heads, values, preferred_element_type=jnp.float32
-    )
-    grad_weights = (decay * grad_scores_lin).astype(jnp.bfloat16)
-    lin_query_grad = jnp.einsum(
-        "hts,shd->thd", grad_weights, keys, preferred_element_type=jnp.float32
-    )
-    lin_query_grad = (
-        lin_query_grad
-        + jnp.einsum("the,hde->thd", as_float(grad_heads), state_in, precision=HIGH_PRECISION)
-        * entry.T[:, :, None]
-    )
-    lin_key_grad = jnp.einsum(
-        "hts,thd->shd", grad_weights, queries, preferred_element_type=jnp.float32
-    )
-
-    lin_value_grad = jnp.einsum(
-        "hts,the->she", weights, grad_heads, preferred_element_type=jnp.float32
-    )
-
     key_window = jnp.concatenate(
         [received[back - 1][0] for back in range(REACH - 1, 0, -1)] + [soft_keys], 0
     )
@@ -255,17 +237,56 @@
     value_terms = jnp.einsum(
         "htu,thd->uhd", probs_half, soft_grads, preferred_element_type=jnp.float32
     )
+    soft_items = [
+        packed(
+            key_terms[(REACH - 1 - back) * tokens : (REACH - back) * tokens],
+            value_terms[(REACH - 1 - back) * tokens : (REACH - back) * tokens],
+        ).astype(jnp.bfloat16)
+        for back in range(1, REACH)
+    ]
+    row_sums = jnp.stack([jnp.sum(flat * flat, axis=1), jnp.sum(flat * scaled_grad, axis=1)])
+    row_sums, soft_items = lax.optimization_barrier((row_sums, soft_items))
+    soft_arrived = [
+        shifted(item, "seq", -back) for back, item in zip(range(1, REACH), soft_items)
+    ]
+    sums = tp_sum(row_sums, "tp")
+    width = lax.axis_size("tp") * heads * HD
+    inverse = lax.rsqrt(sums[0] / width + NORM_EPS)
+    cross = sums[1] / width
+    norm_grad = (inverse[:, None] * scaled_grad - flat * (inverse**3 * cross)[:, None]).astype(
+        jnp.bfloat16
+    )
+    grad_heads = split_heads(norm_grad)
+    back_summary = backward_summary(
+        queries, grad_heads, own_labels, firsts[REACH : REACH + 1] == lasts[REACH - 1 : REACH], decay_rate
+    )
+    back_state = back_summary.astype(jnp.bfloat16)
+    grad_scores_lin = jnp.einsum(
+        "thd,shd->hts", grad_heads, values, preferred_element_type=jnp.float32
+    )
+    grad_weights = (decay * grad_scores_lin).astype(jnp.bfloat16)
+    lin_query_grad = jnp.einsum(
+        "hts,shd->thd", grad_weights, keys, preferred_element_type=jnp.float32
+    )
+    lin_query_grad = (
+        lin_query_grad
+        + jnp.einsum("the,hde->thd", as_float(grad_heads), state_in, precision=HIGH_PRECISION)
+        * entry.T[:, :, None]
+    )
+    lin_key_grad = jnp.einsum(
+        "hts,thd->shd", grad_weights, queries, preferred_element_type=jnp.float32
+    )
+
+    lin_value_grad = jnp.einsum(
+        "hts,the->she", weights, grad_heads, preferred_element_type=jnp.float32
+    )
+
     soft_key_grad = key_terms[(REACH - 1) * tokens :]
     soft_value_grad = value_terms[(REACH - 1) * tokens :]
     items = {}
     for back in range(1, REACH):
-        lower = (REACH - 1 - back) * tokens
         chain = jnp.prod(behind[REACH - back : REACH - 1], axis=0)
-        items[back] = packed(
-            key_terms[lower : lower + tokens],
-            value_terms[lower : lower + tokens],
-            chain[:, None, None] * back_summary,
-        )
+        items[back] = (chain[:, None, None] * back_summary).reshape(-1)
     size = items[1].shape[0]
 
     def wire(value):
@@ -280,10 +301,11 @@
         )
     )
     third = as_float(shifted(wire(second[size:]), "seq", -2))
-    total = first[2 * size :] + second[:size] + third
-    got_key, got_value, reverse_in = unpacked(total, (kv_shape, kv_shape, state_shape))
-    soft_key_grad = soft_key_grad + got_key
-    soft_value_grad = soft_value_grad + got_value
+    reverse_in = (first[2 * size :] + second[:size] + third).reshape(state_shape)
+    for got in soft_arrived:
+        got_key, got_value = unpacked(as_float(got), (kv_shape, kv_shape))
+        soft_key_grad = soft_key_grad + got_key
+        soft_value_grad = soft_value_grad + got_value
     lin_key_grad = lin_key_grad + (
         jnp.einsum("she,hde->shd", as_float(values), reverse_in, precision=HIGH_PRECISION)
         * leave.T[:, :, None]

time: 112 us -> 122 us (1.089)
  the two profiles are of different devices: /device:TPU:1 before, /device:TPU:98 now
where the time goes in v5:
time: 122 us; the launch traced here: 121 us
  starting transfers between devices  54.3 us (45%)
  waiting for transfers between devices  36.7 us (30%)
  local copies, waits for them, and re-layouts  14.4 us (12%)
  matrix products  8.14 us (7%)
  between operations  4.14 us (3%)
  other arithmetic  2.99 us (2%)
    ppermute x12, starting transfers between devices, shifted(): lax.ppermute(value, axis, [(source, source + steps) for source in range(f...  33.5 us
    ppermute x12, waiting for transfers between devices, shifted(): lax.ppermute(value, axis, [(source, source + steps) for source in range(f...  32.9 us
    ppermute x6, starting transfers between devices, tp_sum(): parts.append(lax.ppermute(value, axis, pairs))  20.8 us
    unnamed x43, local copies, waits for them, and re-layouts  11 us
    ppermute x6, waiting for transfers between devices, tp_sum(): parts.append(lax.ppermute(value, axis, pairs))  3.78 us
  transfers between devices with their start and end apart: 18, of which 8 were waited for; matrix products, arithmetic and copies ran while one was open for 7% of the time, Pallas kernels for 0%

profile of v5, /device:TPU:98, one launch (start us, length us, event | category | flops | bytes accessed | tf_op | source)
XLA Modules:
  0.0 120.6 jit_solution(2172998264757159989)
XLA Ops:
  0.7 0.6 copy-done.10
  1.4 0.6 copy-done.9
  2.2 0.6 fusion.80
  5.4 0.9 copy.141
  6.4 0.8 copy-done.4
  7.6 5.0 %collective-permute-start = (bf16[98304]{0:T(1024)(128)(2,1)S(1)}, bf16[98304]{0:T(1024)(128)(2,1)S(1)}, u32[]{:S(2)}, u32[]{:S(2)}) collective-permute-start(bf16[98304]{0:T(1024)(128)(2,1)S(1)} %pad_maximum_fusion.1), channel_id=1, source_target_pairs={{0,32},{16,48},{32,64},{48,80},{64,96},{80,112},{96,128},{112,144}... | collective-permute-start | bytes 589832 | tf_op jit(solution)/shard_map/ppermute | solution.py:20
  13.0 0.7 copy-done.2
  13.9 0.7 slice_compare_fusion
  14.8 0.7 copy-done.6
  15.6 0.7 copy-done.7
  17.3 1.9 %collective-permute-start.1 = (bf16[196608]{0:T(1024)(128)(2,1)S(1)}, bf16[196608]{0:T(1024)(128)(2,1)S(1)}, u32[]{:S(2)}, u32[]{:S(2)}) collective-permute-start(bf16[196608]{0:T(1024)(128)(2,1)S(1)} %pad_maximum_fusion), channel_id=1, source_target_pairs={{0,16},{16,32},{32,48},{48,64},{64,80},{80,96},{96,112},{112,128},... | collective-permute-start | bytes 1179656 | tf_op jit(solution)/shard_map/ppermute | solution.py:20
  19.2 5.1 %collective-permute-start.2 = (bf16[98304]{0:T(1024)(128)(2,1)S(1)}, bf16[98304]{0:T(1024)(128)(2,1)S(1)}, u32[]{:S(2)}, u32[]{:S(2)}) collective-permute-start(bf16[98304]{0:T(1024)(128)(2,1)S(1)} %collective-permute-done), channel_id=1, source_target_pairs={{0,32},{16,48},{32,64},{48,80},{64,96},{80,112},{96,128},{112,144}... | collective-permute-start | bytes 589832 | tf_op jit(solution)/shard_map/ppermute | solution.py:20
  24.4 5.3 %collective-permute-done.2 = bf16[98304]{0:T(1024)(128)(2,1)S(1)} collective-permute-done((bf16[98304]{0:T(1024)(128)(2,1)S(1)}, bf16[98304]{0:T(1024)(128)(2,1)S(1)}, u32[]{:S(2)}, u32[]{:S(2)}) %collective-permute-start.2) | collective-permute-done | bytes 196640 | tf_op jit(solution)/shard_map/ppermute | solution.py:20
  29.7 3.7 %collective-permute-start.3 = (bf16[98304]{0:T(1024)(128)(2,1)S(1)}, bf16[98304]{0:T(1024)(128)(2,1)S(1)}, u32[]{:S(2)}, u32[]{:S(2)}) collective-permute-start(bf16[98304]{0:T(1024)(128)(2,1)S(1)} %collective-permute-done.2), channel_id=1, source_target_pairs={{0,16},{16,32},{32,48},{48,64},{64,80},{80,96},{96,112},{112,128},... | collective-permute-start | bytes 589832 | tf_op jit(solution)/shard_map/ppermute | solution.py:20
  33.4 3.3 %collective-permute-done.3 = bf16[98304]{0:T(1024)(128)(2,1)S(1)} collective-permute-done((bf16[98304]{0:T(1024)(128)(2,1)S(1)}, bf16[98304]{0:T(1024)(128)(2,1)S(1)}, u32[]{:S(2)}, u32[]{:S(2)}) %collective-permute-start.3) | collective-permute-done | bytes 196640 | tf_op jit(solution)/shard_map/ppermute | solution.py:20
  37.8 1.3 %fusion.81 = (f32[2,128]{1,0:T(2,128)S(1)}, f32[2,128,768]{1,2,0:T(8,128)}) fusion(bf16[768,2,128]{2,0,1:T(8,128)(2,1)S(1)} %constant_dynamic-update-slice_fusion, bf16[128,2,128]{0,2,1:T(8,128)(2,1)S(1)} %bitcast.258, pred[128,768]{0,1:T(8,128)(4,1)S(1)} %fusion.25), kind=kOutput, calls=%fused_computation.170 | convolution fusion | flops 51118848 | bytes 1344512 | tf_op jit(solution)/shard_map/sub | solution.py:220
  39.1 1.5 %fusion.82 = (bf16[768,2,128]{0,2,1:T(8,128)(2,1)S(1)}, f32[768,2,128]{0,2,1:T(8,128)}) fusion(bf16[128,2,128]{0,2,1:T(8,128)(2,1)S(1)} %bitcast.298, f32[2,128]{1,0:T(2,128)S(1)} %get-tuple-element.87, bf16[768,2,128]{2,0,1:T(8,128)(2,1)S(1)} %constant_dynamic-update-slice_fusion, bf16[128,2,128]{0,2,1:T(8,128)(2,1)S(1)} %bitcast.259, ...), kind=kOutput, calls=%fused_computation.171 | convolution fusion | flops 101843968 | bytes 1803264 | tf_op jit(solution)/shard_map/htu,thd->uhd/dot_general | solution.py:237
  40.6 0.7 fusion.24
  42.0 1.4 %fusion.8 = bf16[2,128,768]{1,2,0:T(8,128)(2,1)S(1)} fusion(bf16[768,2,128]{2,0,1:T(8,128)(2,1)S(1)} %constant_dynamic-update-slice_fusion.1, bf16[128,2,128]{0,2,1:T(8,128)(2,1)S(1)} %bitcast.300, f32[2,128]{1,0:T(2,128)S(1)} %bitcast.303, f32[2,128,768]{1,2,0:T(8,128)} %get-tuple-element.88, f32[2,128]{1,0:T(2,128)S(1)} %get-tuple-element.87), kind=kOutput, calls=%fused_computation.12 | convolution fusion | flops 51118080 | bytes 1640448 | tf_op jit(solution)/shard_map/thd,uhd->htu/dot_general | solution.py:117
  44.1 0.7 copy-done.3
  45.0 4.9 %collective-permute-start.6 = (f32[2,128]{1,0:T(2,128)S(1)}, f32[2,128]{1,0:T(2,128)S(1)}, u32[]{:S(2)}, u32[]{:S(2)}) collective-permute-start(f32[2,128]{1,0:T(2,128)S(1)} %pad_maximum_fusion.9), channel_id=1, source_target_pairs={{0,3},{1,0},{2,1},{3,2},{4,7},{5,4},{6,5},{7,6},{8,11},{9,8},{10,9... | collective-permute-start | bytes 3080 | tf_op jit(solution)/shard_map/ppermute | solution.py:36
  50.0 2.5 %collective-permute-start.5 = (f32[2,128]{1,0:T(2,128)S(1)}, f32[2,128]{1,0:T(2,128)S(1)}, u32[]{:S(2)}, u32[]{:S(2)}) collective-permute-start(f32[2,128]{1,0:T(2,128)S(1)} %pad_maximum_fusion.9), channel_id=1, source_target_pairs={{0,2},{1,3},{2,0},{3,1},{4,6},{5,7},{6,4},{7,5},{8,10},{9,11},{10,... | collective-permute-start | bytes 3080 | tf_op jit(solution)/shard_map/ppermute | solution.py:36
  52.5 2.9 %collective-permute-start.4 = (f32[2,128]{1,0:T(2,128)S(1)}, f32[2,128]{1,0:T(2,128)S(1)}, u32[]{:S(2)}, u32[]{:S(2)}) collective-permute-start(f32[2,128]{1,0:T(2,128)S(1)} %pad_maximum_fusion.9), channel_id=1, source_target_pairs={{0,1},{1,2},{2,3},{3,0},{4,5},{5,6},{6,7},{7,4},{8,9},{9,10},{10,1... | collective-permute-start | bytes 3080 | tf_op jit(solution)/shard_map/ppermute | solution.py:36
  55.4 1.5 %collective-permute-done.5 = f32[2,128]{1,0:T(2,128)S(1)} collective-permute-done((f32[2,128]{1,0:T(2,128)S(1)}, f32[2,128]{1,0:T(2,128)S(1)}, u32[]{:S(2)}, u32[]{:S(2)}) %collective-permute-start.5) | collective-permute-done | bytes 1056 | tf_op jit(solution)/shard_map/ppermute | solution.py:36
  56.9 2.3 %collective-permute-done.4 = f32[2,128]{1,0:T(2,128)S(1)} collective-permute-done((f32[2,128]{1,0:T(2,128)S(1)}, f32[2,128]{1,0:T(2,128)S(1)}, u32[]{:S(2)}, u32[]{:S(2)}) %collective-permute-start.4) | collective-permute-done | bytes 1056 | tf_op jit(solution)/shard_map/ppermute | solution.py:36
  59.2 2.4 %collective-permute-start.9 = (f32[2,128]{1,0:T(2,128)S(1)}, f32[2,128]{1,0:T(2,128)S(1)}, u32[]{:S(2)}, u32[]{:S(2)}) collective-permute-start(f32[2,128]{1,0:T(2,128)S(1)} %add_add_fusion.1), channel_id=1, source_target_pairs={{0,12},{1,13},{2,14},{3,15},{4,0},{5,1},{6,2},{7,3},{8,4},{9,5},{1... | collective-permute-start | bytes 3080 | tf_op jit(solution)/shard_map/ppermute | solution.py:36
  61.6 4.3 %collective-permute-start.8 = (f32[2,128]{1,0:T(2,128)S(1)}, f32[2,128]{1,0:T(2,128)S(1)}, u32[]{:S(2)}, u32[]{:S(2)}) collective-permute-start(f32[2,128]{1,0:T(2,128)S(1)} %add_add_fusion.1), channel_id=1, source_target_pairs={{0,8},{1,9},{2,10},{3,11},{4,12},{5,13},{6,14},{7,15},{8,0},{9,1},... | collective-permute-start | bytes 3080 | tf_op jit(solution)/shard_map/ppermute | solution.py:36
  66.0 3.7 %collective-permute-start.7 = (f32[2,128]{1,0:T(2,128)S(1)}, f32[2,128]{1,0:T(2,128)S(1)}, u32[]{:S(2)}, u32[]{:S(2)}) collective-permute-start(f32[2,128]{1,0:T(2,128)S(1)} %add_add_fusion.1), channel_id=1, source_target_pairs={{0,4},{1,5},{2,6},{3,7},{4,8},{5,9},{6,10},{7,11},{8,12},{9,13},{1... | collective-permute-start | bytes 3080 | tf_op jit(solution)/shard_map/ppermute | solution.py:36
  69.7 0.3 fusion.19
  70.0 0.7 copy.122
  70.8 1.9 %collective-permute-start.13 = (bf16[65536]{0:T(1024)(128)(2,1)S(1)}, bf16[65536]{0:T(1024)(128)(2,1)S(1)}, u32[]{:S(2)}, u32[]{:S(2)}) collective-permute-start(bf16[65536]{0:T(1024)(128)(2,1)S(1)} %pad_maximum_fusion.3), channel_id=1, source_target_pairs={{16,0},{32,16},{48,32},{64,48},{80,64},{96,80},{112,96},{128,112},... | collective-permute-start | bytes 393224 | tf_op jit(solution)/shard_map/ppermute | solution.py:20
  72.7 3.8 %collective-permute-start.14 = (bf16[65536]{0:T(1024)(128)(2,1)S(1)}, bf16[65536]{0:T(1024)(128)(2,1)S(1)}, u32[]{:S(2)}, u32[]{:S(2)}) collective-permute-start(bf16[65536]{0:T(1024)(128)(2,1)S(1)} %pad_maximum_fusion.4), channel_id=1, source_target_pairs={{32,0},{48,16},{64,32},{80,48},{96,64},{112,80},{128,96},{144,112}... | collective-permute-start | bytes 393224 | tf_op jit(solution)/shard_map/ppermute | solution.py:20
  76.5 2.1 %collective-permute-start.15 = (bf16[65536]{0:T(1024)(128)(2,1)S(1)}, bf16[65536]{0:T(1024)(128)(2,1)S(1)}, u32[]{:S(2)}, u32[]{:S(2)}) collective-permute-start(bf16[65536]{0:T(1024)(128)(2,1)S(1)} %pad_maximum_fusion.5), channel_id=1, source_target_pairs={{48,0},{64,16},{80,32},{96,48},{112,64},{128,80},{144,96},{160,112... | collective-permute-start | bytes 393224 | tf_op jit(solution)/shard_map/ppermute | solution.py:20
  78.7 1.9 %collective-permute-start.16 = (bf16[65536]{0:T(1024)(128)(2,1)S(1)}, bf16[65536]{0:T(1024)(128)(2,1)S(1)}, u32[]{:S(2)}, u32[]{:S(2)}) collective-permute-start(bf16[65536]{0:T(1024)(128)(2,1)S(1)} %pad_maximum_fusion.6), channel_id=1, source_target_pairs={{64,0},{80,16},{96,32},{112,48},{128,64},{144,80},{160,96},{176,11... | collective-permute-start | bytes 393224 | tf_op jit(solution)/shard_map/ppermute | solution.py:20
  80.6 1.9 %collective-permute-start.17 = (bf16[65536]{0:T(1024)(128)(2,1)S(1)}, bf16[65536]{0:T(1024)(128)(2,1)S(1)}, u32[]{:S(2)}, u32[]{:S(2)}) collective-permute-start(bf16[65536]{0:T(1024)(128)(2,1)S(1)} %pad_maximum_fusion.7), channel_id=1, source_target_pairs={{80,0},{96,16},{112,32},{128,48},{144,64},{160,80},{176,96},{192,1... | collective-permute-start | bytes 393224 | tf_op jit(solution)/shard_map/ppermute | solution.py:20
  83.4 0.7 copy.119
  84.7 2.2 %collective-permute-start.10 = (bf16[98304]{0:T(1024)(128)(2,1)S(1)}, bf16[98304]{0:T(1024)(128)(2,1)S(1)}, u32[]{:S(2)}, u32[]{:S(2)}) collective-permute-start(bf16[98304]{0:T(1024)(128)(2,1)S(1)} %pad_maximum_fusion.2), channel_id=1, source_target_pairs={{16,0},{32,16},{48,32},{64,48},{80,64},{96,80},{112,96},{128,112},... | collective-permute-start | bytes 589832 | tf_op jit(solution)/shard_map/ppermute | solution.py:20
  87.0 5.5 %collective-permute-done.16 = bf16[65536]{0:T(1024)(128)(2,1)S(1)} collective-permute-done((bf16[65536]{0:T(1024)(128)(2,1)S(1)}, bf16[65536]{0:T(1024)(128)(2,1)S(1)}, u32[]{:S(2)}, u32[]{:S(2)}) %collective-permute-start.16) | collective-permute-done | bytes 131104 | tf_op jit(solution)/shard_map/ppermute | solution.py:20
  92.5 9.0 %collective-permute-done.17 = bf16[65536]{0:T(1024)(128)(2,1)S(1)} collective-permute-done((bf16[65536]{0:T(1024)(128)(2,1)S(1)}, bf16[65536]{0:T(1024)(128)(2,1)S(1)}, u32[]{:S(2)}, u32[]{:S(2)}) %collective-permute-start.17) | collective-permute-done | bytes 131104 | tf_op jit(solution)/shard_map/ppermute | solution.py:20
  102.1 1.9 %collective-permute-start.11 = (bf16[65536]{0:T(1024)(128)(2,1)S(1)}, bf16[65536]{0:T(1024)(128)(2,1)S(1)}, u32[]{:S(2)}, u32[]{:S(2)}) collective-permute-start(bf16[65536]{0:T(1024)(128)(2,1)S(1)} %pad_maximum_fusion.8), channel_id=1, source_target_pairs={{32,0},{48,16},{64,32},{80,48},{96,64},{112,80},{128,96},{144,112}... | collective-permute-start | bytes 393224 | tf_op jit(solution)/shard_map/ppermute | solution.py:20
  104.0 0.9 fusion.31
  105.0 6.1 %collective-permute-done.11 = bf16[65536]{0:T(1024)(128)(2,1)S(1)} collective-permute-done((bf16[65536]{0:T(1024)(128)(2,1)S(1)}, bf16[65536]{0:T(1024)(128)(2,1)S(1)}, u32[]{:S(2)}, u32[]{:S(2)}) %collective-permute-start.11) | collective-permute-done | bytes 131104 | tf_op jit(solution)/shard_map/ppermute | solution.py:20
  111.0 1.9 %collective-permute-start.12 = (bf16[32768]{0:T(1024)(128)(2,1)S(1)}, bf16[32768]{0:T(1024)(128)(2,1)S(1)}, u32[]{:S(2)}, u32[]{:S(2)}) collective-permute-start(bf16[32768]{0:T(1024)(128)(2,1)S(1)} %slice.569), channel_id=1, source_target_pairs={{32,0},{48,16},{64,32},{80,48},{96,64},{112,80},{128,96},{144,112}... | collective-permute-start | bytes 196616 | tf_op jit(solution)/shard_map/ppermute | solution.py:20
  113.0 0.7 copy.124
  113.9 0.7 copy.123
  114.6 3.8 %collective-permute-done.12 = bf16[32768]{0:T(1024)(128)(2,1)S(1)} collective-permute-done((bf16[32768]{0:T(1024)(128)(2,1)S(1)}, bf16[32768]{0:T(1024)(128)(2,1)S(1)}, u32[]{:S(2)}, u32[]{:S(2)}) %collective-permute-start.12) | collective-permute-done | bytes 65568 | tf_op jit(solution)/shard_map/ppermute | solution.py:20
  119.1 0.7 copy.120
  119.9 0.7 copy.121
  (130 shorter events, 7.8 us)
Async XLA Ops:
  0.6 6.7 %copy-start = (bf16[128,256]{1,0:T(8,128)(2,1)S(1)}, bf16[128,256]{1,0:T(8,128)(2,1)}, u32[]{:S(2)}) copy-start(bf16[128,256]{1,0:T(8,128)(2,1)} %param.13) | copy-start | bytes 196612
  0.7 0.7 copy-start.10
  1.4 0.7 copy-start.9
  5.4 0.9 copy-start.1
  6.3 0.8 copy-start.4
  7.6 9.7 %collective-permute-start = (bf16[98304]{0:T(1024)(128)(2,1)S(1)}, bf16[98304]{0:T(1024)(128)(2,1)S(1)}, u32[]{:S(2)}, u32[]{:S(2)}) collective-permute-start(bf16[98304]{0:T(1024)(128)(2,1)S(1)} %pad_maximum_fusion.1), channel_id=1, source_target_pairs={{0,32},{16,48},{32,64},{48,80},{64,96},{80,112},{96,128},{112,144}... | collective-permute-start | bytes 589832 | tf_op jit(solution)/shard_map/ppermute | solution.py:20
  12.9 0.8 copy-start.2
  13.7 0.9 copy-start.5
  14.7 0.8 copy-start.6
  15.5 0.8 copy-start.7
  17.3 19.4 %collective-permute-start.1 = (bf16[196608]{0:T(1024)(128)(2,1)S(1)}, bf16[196608]{0:T(1024)(128)(2,1)S(1)}, u32[]{:S(2)}, u32[]{:S(2)}) collective-permute-start(bf16[196608]{0:T(1024)(128)(2,1)S(1)} %pad_maximum_fusion), channel_id=1, source_target_pairs={{0,16},{16,32},{32,48},{48,64},{64,80},{80,96},{96,112},{112,128},... | collective-permute-start | bytes 1179656 | tf_op jit(solution)/shard_map/ppermute | solution.py:20
  19.2 10.5 %collective-permute-start.2 = (bf16[98304]{0:T(1024)(128)(2,1)S(1)}, bf16[98304]{0:T(1024)(128)(2,1)S(1)}, u32[]{:S(2)}, u32[]{:S(2)}) collective-permute-start(bf16[98304]{0:T(1024)(128)(2,1)S(1)} %collective-permute-done), channel_id=1, source_target_pairs={{0,32},{16,48},{32,64},{48,80},{64,96},{80,112},{96,128},{112,144}... | collective-permute-start | bytes 589832 | tf_op jit(solution)/shard_map/ppermute | solution.py:20
  29.7 7.0 %collective-permute-start.3 = (bf16[98304]{0:T(1024)(128)(2,1)S(1)}, bf16[98304]{0:T(1024)(128)(2,1)S(1)}, u32[]{:S(2)}, u32[]{:S(2)}) collective-permute-start(bf16[98304]{0:T(1024)(128)(2,1)S(1)} %collective-permute-done.2), channel_id=1, source_target_pairs={{0,16},{16,32},{32,48},{48,64},{64,80},{80,96},{96,112},{112,128},... | collective-permute-start | bytes 589832 | tf_op jit(solution)/shard_map/ppermute | solution.py:20
  44.0 0.8 copy-start.3
  44.0 0.8 copy-start.8
  45.0 10.4 %collective-permute-start.6 = (f32[2,128]{1,0:T(2,128)S(1)}, f32[2,128]{1,0:T(2,128)S(1)}, u32[]{:S(2)}, u32[]{:S(2)}) collective-permute-start(f32[2,128]{1,0:T(2,128)S(1)} %pad_maximum_fusion.9), channel_id=1, source_target_pairs={{0,3},{1,0},{2,1},{3,2},{4,7},{5,4},{6,5},{7,6},{8,11},{9,8},{10,9... | collective-permute-start | bytes 3080 | tf_op jit(solution)/shard_map/ppermute | solution.py:36
  50.0 7.0 %collective-permute-start.5 = (f32[2,128]{1,0:T(2,128)S(1)}, f32[2,128]{1,0:T(2,128)S(1)}, u32[]{:S(2)}, u32[]{:S(2)}) collective-permute-start(f32[2,128]{1,0:T(2,128)S(1)} %pad_maximum_fusion.9), channel_id=1, source_target_pairs={{0,2},{1,3},{2,0},{3,1},{4,6},{5,7},{6,4},{7,5},{8,10},{9,11},{10,... | collective-permute-start | bytes 3080 | tf_op jit(solution)/shard_map/ppermute | solution.py:36
  52.5 6.7 %collective-permute-start.4 = (f32[2,128]{1,0:T(2,128)S(1)}, f32[2,128]{1,0:T(2,128)S(1)}, u32[]{:S(2)}, u32[]{:S(2)}) collective-permute-start(f32[2,128]{1,0:T(2,128)S(1)} %pad_maximum_fusion.9), channel_id=1, source_target_pairs={{0,1},{1,2},{2,3},{3,0},{4,5},{5,6},{6,7},{7,4},{8,9},{9,10},{10,1... | collective-permute-start | bytes 3080 | tf_op jit(solution)/shard_map/ppermute | solution.py:36
  59.2 17.3 %collective-permute-start.9 = (f32[2,128]{1,0:T(2,128)S(1)}, f32[2,128]{1,0:T(2,128)S(1)}, u32[]{:S(2)}, u32[]{:S(2)}) collective-permute-start(f32[2,128]{1,0:T(2,128)S(1)} %add_add_fusion.1), channel_id=1, source_target_pairs={{0,12},{1,13},{2,14},{3,15},{4,0},{5,1},{6,2},{7,3},{8,4},{9,5},{1... | collective-permute-start | bytes 3080 | tf_op jit(solution)/shard_map/ppermute | solution.py:36
  61.6 17.0 %collective-permute-start.8 = (f32[2,128]{1,0:T(2,128)S(1)}, f32[2,128]{1,0:T(2,128)S(1)}, u32[]{:S(2)}, u32[]{:S(2)}) collective-permute-start(f32[2,128]{1,0:T(2,128)S(1)} %add_add_fusion.1), channel_id=1, source_target_pairs={{0,8},{1,9},{2,10},{3,11},{4,12},{5,13},{6,14},{7,15},{8,0},{9,1},... | collective-permute-start | bytes 3080 | tf_op jit(solution)/shard_map/ppermute | solution.py:36
  66.0 14.6 %collective-permute-start.7 = (f32[2,128]{1,0:T(2,128)S(1)}, f32[2,128]{1,0:T(2,128)S(1)}, u32[]{:S(2)}, u32[]{:S(2)}) collective-permute-start(f32[2,128]{1,0:T(2,128)S(1)} %add_add_fusion.1), channel_id=1, source_target_pairs={{0,4},{1,5},{2,6},{3,7},{4,8},{5,9},{6,10},{7,11},{8,12},{9,13},{1... | collective-permute-start | bytes 3080 | tf_op jit(solution)/shard_map/ppermute | solution.py:36
  70.8 13.9 %collective-permute-start.13 = (bf16[65536]{0:T(1024)(128)(2,1)S(1)}, bf16[65536]{0:T(1024)(128)(2,1)S(1)}, u32[]{:S(2)}, u32[]{:S(2)}) collective-permute-start(bf16[65536]{0:T(1024)(128)(2,1)S(1)} %pad_maximum_fusion.3), channel_id=1, source_target_pairs={{16,0},{32,16},{48,32},{64,48},{80,64},{96,80},{112,96},{128,112},... | collective-permute-start | bytes 393224 | tf_op jit(solution)/shard_map/ppermute | solution.py:20
  72.7 14.2 %collective-permute-start.14 = (bf16[65536]{0:T(1024)(128)(2,1)S(1)}, bf16[65536]{0:T(1024)(128)(2,1)S(1)}, u32[]{:S(2)}, u32[]{:S(2)}) collective-permute-start(bf16[65536]{0:T(1024)(128)(2,1)S(1)} %pad_maximum_fusion.4), channel_id=1, source_target_pairs={{32,0},{48,16},{64,32},{80,48},{96,64},{112,80},{128,96},{144,112}... | collective-permute-start | bytes 393224 | tf_op jit(solution)/shard_map/ppermute | solution.py:20
  76.5 10.4 %collective-permute-start.15 = (bf16[65536]{0:T(1024)(128)(2,1)S(1)}, bf16[65536]{0:T(1024)(128)(2,1)S(1)}, u32[]{:S(2)}, u32[]{:S(2)}) collective-permute-start(bf16[65536]{0:T(1024)(128)(2,1)S(1)} %pad_maximum_fusion.5), channel_id=1, source_target_pairs={{48,0},{64,16},{80,32},{96,48},{112,64},{128,80},{144,96},{160,112... | collective-permute-start | bytes 393224 | tf_op jit(solution)/shard_map/ppermute | solution.py:20
  78.7 13.8 %collective-permute-start.16 = (bf16[65536]{0:T(1024)(128)(2,1)S(1)}, bf16[65536]{0:T(1024)(128)(2,1)S(1)}, u32[]{:S(2)}, u32[]{:S(2)}) collective-permute-start(bf16[65536]{0:T(1024)(128)(2,1)S(1)} %pad_maximum_fusion.6), channel_id=1, source_target_pairs={{64,0},{80,16},{96,32},{112,48},{128,64},{144,80},{160,96},{176,11... | collective-permute-start | bytes 393224 | tf_op jit(solution)/shard_map/ppermute | solution.py:20
  80.6 20.8 %collective-permute-start.17 = (bf16[65536]{0:T(1024)(128)(2,1)S(1)}, bf16[65536]{0:T(1024)(128)(2,1)S(1)}, u32[]{:S(2)}, u32[]{:S(2)}) collective-permute-start(bf16[65536]{0:T(1024)(128)(2,1)S(1)} %pad_maximum_fusion.7), channel_id=1, source_target_pairs={{80,0},{96,16},{112,32},{128,48},{144,64},{160,80},{176,96},{192,1... | collective-permute-start | bytes 393224 | tf_op jit(solution)/shard_map/ppermute | solution.py:20
  84.7 17.3 %collective-permute-start.10 = (bf16[98304]{0:T(1024)(128)(2,1)S(1)}, bf16[98304]{0:T(1024)(128)(2,1)S(1)}, u32[]{:S(2)}, u32[]{:S(2)}) collective-permute-start(bf16[98304]{0:T(1024)(128)(2,1)S(1)} %pad_maximum_fusion.2), channel_id=1, source_target_pairs={{16,0},{32,16},{48,32},{64,48},{80,64},{96,80},{112,96},{128,112},... | collective-permute-start | bytes 589832 | tf_op jit(solution)/shard_map/ppermute | solution.py:20
  102.1 8.9 %collective-permute-start.11 = (bf16[65536]{0:T(1024)(128)(2,1)S(1)}, bf16[65536]{0:T(1024)(128)(2,1)S(1)}, u32[]{:S(2)}, u32[]{:S(2)}) collective-permute-start(bf16[65536]{0:T(1024)(128)(2,1)S(1)} %pad_maximum_fusion.8), channel_id=1, source_target_pairs={{32,0},{48,16},{64,32},{80,48},{96,64},{112,80},{128,96},{144,112}... | collective-permute-start | bytes 393224 | tf_op jit(solution)/shard_map/ppermute | solution.py:20
  111.0 7.4 %collective-permute-start.12 = (bf16[32768]{0:T(1024)(128)(2,1)S(1)}, bf16[32768]{0:T(1024)(128)(2,1)S(1)}, u32[]{:S(2)}, u32[]{:S(2)}) collective-permute-start(bf16[32768]{0:T(1024)(128)(2,1)S(1)} %slice.569), channel_id=1, source_target_pairs={{32,0},{48,16},{64,32},{80,48},{96,64},{112,80},{128,96},{144,112}... | collective-permute-start | bytes 196616 | tf_op jit(solution)/shard_map/ppermute | solution.py:20

commit v6 on v4

--- a/solution.py
+++ b/solution.py
@@ -186,7 +186,10 @@
     lin_out = inner + carried * entry.T[:, :, None]
     flat = lin_out.reshape(tokens, heads * HD)
     scaled_grad = norm_gain[None, :] * as_float(lin_grad)
-    sums = tp_sum(jnp.stack([jnp.sum(flat * flat, axis=1), jnp.sum(flat * scaled_grad, axis=1)]), "tp")
+    pieces = flat.reshape(tokens, 64, -1)
+    grad_pieces = scaled_grad.reshape(tokens, 64, -1)
+    sums = tp_sum(jnp.stack([jnp.sum(pieces * pieces, axis=2), jnp.sum(pieces * grad_pieces, axis=2)]).transpose(2, 0, 1), "tp")
+    sums = jnp.sum(sums, axis=0)
     width = lax.axis_size("tp") * heads * HD
     inverse = lax.rsqrt(sums[0] / width + NORM_EPS)
     cross = sums[1] / width

time: 112 us -> 183 us (1.63)
  waiting for transfers between devices: 36.3 us -> 108 us
  blocking collectives: 14.8 us -> 0 us
  between operations: 4.03 us -> 17.5 us
  other arithmetic: 5.19 us -> 8.98 us
  starting transfers between devices: 31.9 us -> 28.9 us
  matrix products: 8.03 us -> 6.14 us
    all_gather x0 -> x1, waiting for transfers between devices: none -> 74.3 us  [tp_sum(): return jnp.sum(lax.all_gather(value, axis), axis=0)]
    all_gather x1 -> x0, blocking collectives: 14.8 us -> none  [tp_sum(): return jnp.sum(lax.all_gather(value, axis), axis=0)]
    ppermute x7, starting transfers between devices: 31.9 us -> 28.9 us  [shifted(): lax.ppermute(value, axis, [(source, source + steps) for source in range(f...]
    ppermute x7, waiting for transfers between devices: 36.3 us -> 33.7 us  [shifted(): lax.ppermute(value, axis, [(source, source + steps) for source in range(f...]
    reduce_sum x2, other arithmetic: 0.13 us -> 2.48 us  [the longest x1 2.31 us: body(): sums = jnp.sum(sums, axis=0)]
    unnamed x57 -> x70, local copies, waits for them, and re-layouts: 7.31 us -> 7.1 us
  transfers between devices with their start and end apart: 7 -> 8, of which waited for: 6 -> 6; matrix products, arithmetic and copies ran while one was open for 5% -> 7% of each run, Pallas kernels for 0% -> 0%
where the time goes in v6:
time: 183 us; the launch traced here: 182 us
  waiting for transfers between devices  108 us (59%)
  starting transfers between devices  28.9 us (16%)
  between operations  17.5 us (10%)
  local copies, waits for them, and re-layouts  12.4 us (7%)
  other arithmetic  8.98 us (5%)
  matrix products  6.14 us (3%)
    all_gather x1, waiting for transfers between devices, tp_sum(): return jnp.sum(lax.all_gather(value, axis), axis=0)  74.3 us
    ppermute x7, waiting for transfers between devices, shifted(): lax.ppermute(value, axis, [(source, source + steps) for source in range(f...  33.7 us
    ppermute x7, starting transfers between devices, shifted(): lax.ppermute(value, axis, [(source, source + steps) for source in range(f...  28.9 us
    unnamed x70, local copies, waits for them, and re-layouts  7.1 us
  transfers between devices with their start and end apart: 8, of which 6 were waited for; matrix products, arithmetic and copies ran while one was open for 7% of the time, Pallas kernels for 0%

profile of v6, /device:TPU:1, one launch (start us, length us, event | category | flops | bytes accessed | tf_op | source)
XLA Modules:
  0.0 182.1 jit_solution(153365449053864763)
XLA Ops:
  7.3 0.7 multiply_exponential_fusion.2
  8.1 0.7 pad_add_fusion
  8.9 0.6 fusion.72
  12.1 0.9 copy.196
  13.0 0.9 copy.195
  13.9 1.0 copy.232
  14.9 0.7 multiply_exponential_fusion
  15.7 4.4 %collective-permute-start = (bf16[98304]{0:T(1024)(128)(2,1)S(1)}, bf16[98304]{0:T(1024)(128)(2,1)S(1)}, u32[]{:S(2)}, u32[]{:S(2)}) collective-permute-start(bf16[98304]{0:T(1024)(128)(2,1)S(1)} %pad_maximum_fusion.2), channel_id=1, source_target_pairs={{0,32},{16,48},{32,64},{48,80},{64,96},{80,112},{96,128},{112,144}... | collective-permute-start | bytes 589832 | tf_op jit(solution)/shard_map/ppermute | solution.py:20
  20.3 0.5 slice_reduce_fusion
  20.8 0.5 slice_reduce_fusion.4
  21.3 0.6 slice_reduce_fusion.1
  22.2 0.7 slice_compare_fusion
  23.8 0.3 fusion.28
  24.2 0.2 fusion.20
  24.5 13.9 %collective-permute-start.1 = (bf16[196608]{0:T(1024)(128)(2,1)S(1)}, bf16[196608]{0:T(1024)(128)(2,1)S(1)}, u32[]{:S(2)}, u32[]{:S(2)}) collective-permute-start(bf16[196608]{0:T(1024)(128)(2,1)S(1)} %pad_maximum_fusion), channel_id=1, source_target_pairs={{0,16},{16,32},{32,48},{48,64},{64,80},{80,96},{96,112},{112,128},... | collective-permute-start | bytes 1179656 | tf_op jit(solution)/shard_map/ppermute | solution.py:20
  38.4 1.3 collective-permute-start.2
  39.7 7.6 %collective-permute-done.2 = bf16[98304]{0:T(1024)(128)(2,1)S(1)} collective-permute-done((bf16[98304]{0:T(1024)(128)(2,1)S(1)}, bf16[98304]{0:T(1024)(128)(2,1)S(1)}, u32[]{:S(2)}, u32[]{:S(2)}) %collective-permute-start.2) | collective-permute-done | bytes 196640 | tf_op jit(solution)/shard_map/ppermute | solution.py:20
  47.3 2.7 %collective-permute-start.3 = (bf16[98304]{0:T(1024)(128)(2,1)S(1)}, bf16[98304]{0:T(1024)(128)(2,1)S(1)}, u32[]{:S(2)}, u32[]{:S(2)}) collective-permute-start(bf16[98304]{0:T(1024)(128)(2,1)S(1)} %collective-permute-done.2), channel_id=1, source_target_pairs={{0,16},{16,32},{32,48},{48,64},{64,80},{80,96},{96,112},{112,128},... | collective-permute-start | bytes 589832 | tf_op jit(solution)/shard_map/ppermute | solution.py:20
  50.1 2.6 %collective-permute-done.3 = bf16[98304]{0:T(1024)(128)(2,1)S(1)} collective-permute-done((bf16[98304]{0:T(1024)(128)(2,1)S(1)}, bf16[98304]{0:T(1024)(128)(2,1)S(1)}, u32[]{:S(2)}, u32[]{:S(2)}) %collective-permute-start.3) | collective-permute-done | bytes 196640 | tf_op jit(solution)/shard_map/ppermute | solution.py:20
  52.9 0.3 fusion.15
  53.2 0.2 fusion.16
  53.6 0.7 copy.123
  54.6 0.4 fusion.73
  55.0 0.7 fusion.24
  55.7 0.3 fusion.8
  55.9 0.3 fusion.19
  56.2 0.7 copy.175
  57.0 1.5 fusion.75
  59.0 0.3 fusion.74
  59.6 74.3 %all-gather.3.cloned.1.call-done = f32[1024,2,128]{2,1,0:T(2,128)} async-done(((f32[64,2,128]{2,1,0:T(2,128)}), f32[1024,2,128]{2,1,0:T(2,128)}) %all-gather.3.cloned.1.call-update) | async-done | bytes 1048592 | tf_op jit(solution)/shard_map/all_gather | solution.py:24
  133.9 2.3 %reduce_sum.51 = f32[2,128]{1,0:T(2,128)S(1)} reduce(f32[1024,2,128]{2,1,0:T(2,128)} %all-gather.3.cloned.1.call-done, f32[]{:T(128)} %constant.15.clone.1), dimensions={0}, to_apply=%region_5.6 | reduce | flops 261888 | bytes 1049604 | tf_op jit(solution)/shard_map/reduce_sum | solution.py:192
  136.4 0.3 broadcast_multiply_fusion.1
  136.8 4.0 %collective-permute-start.4 = (bf16[294912]{0:T(1024)(128)(2,1)S(1)}, bf16[294912]{0:T(1024)(128)(2,1)S(1)}, u32[]{:S(2)}, u32[]{:S(2)}) collective-permute-start(bf16[294912]{0:T(1024)(128)(2,1)S(1)} %constant_dynamic-update-slice_fusion.3), channel_id=1, source_target_pairs={{16,0},{32,16},{48,32},{64,48},{80,64},{96,80},{112,96},{128,112},... | collective-permute-start | bytes 1769480 | tf_op jit(solution)/shard_map/ppermute | solution.py:20
  140.8 1.0 fusion.64
  142.5 7.0 %collective-permute-done.4 = bf16[294912]{0:T(1024)(128)(2,1)S(1)} collective-permute-done((bf16[294912]{0:T(1024)(128)(2,1)S(1)}, bf16[294912]{0:T(1024)(128)(2,1)S(1)}, u32[]{:S(2)}, u32[]{:S(2)}) %collective-permute-start.4) | collective-permute-done | bytes 589856 | tf_op jit(solution)/shard_map/ppermute | solution.py:20
  149.7 1.3 collective-permute-start.5
  151.1 0.2 fusion.21
  151.5 0.7 copy.172
  152.2 8.9 %collective-permute-done.5 = bf16[196608]{0:T(1024)(128)(2,1)S(1)} collective-permute-done((bf16[196608]{0:T(1024)(128)(2,1)S(1)}, bf16[196608]{0:T(1024)(128)(2,1)S(1)}, u32[]{:S(2)}, u32[]{:S(2)}) %collective-permute-start.5) | collective-permute-done | bytes 393248 | tf_op jit(solution)/shard_map/ppermute | solution.py:20
  161.2 1.3 collective-permute-start.6
  162.6 7.6 %collective-permute-done.6 = bf16[98304]{0:T(1024)(128)(2,1)S(1)} collective-permute-done((bf16[98304]{0:T(1024)(128)(2,1)S(1)}, bf16[98304]{0:T(1024)(128)(2,1)S(1)}, u32[]{:S(2)}, u32[]{:S(2)}) %collective-permute-start.6) | collective-permute-done | bytes 196640 | tf_op jit(solution)/shard_map/ppermute | solution.py:20
  170.4 0.3 fusion.12
  170.6 0.3 fusion.18
  170.9 0.7 copy.174
  171.8 0.9 fusion.30
  172.7 0.7 copy.177
  173.6 0.7 copy.176
  174.5 0.7 copy.173
  (126 shorter events, 4.9 us)
Async XLA Ops:
  7.2 8.3 %copy-start = (bf16[128,256]{1,0:T(8,128)(2,1)S(1)}, bf16[128,256]{1,0:T(8,128)(2,1)}, u32[]{:S(2)}) copy-start(bf16[128,256]{1,0:T(8,128)(2,1)} %param.13) | copy-start | bytes 196612
  7.2 14.9 %copy-start.2 = (bf16[128,256]{1,0:T(8,128)(2,1)S(1)}, bf16[128,256]{1,0:T(8,128)(2,1)}, u32[]{:S(2)}) copy-start(bf16[128,256]{1,0:T(8,128)(2,1)} %param.19) | copy-start | bytes 196612
  7.2 14.8 %copy-start.1 = (bf16[128,256]{1,0:T(8,128)(2,1)S(1)}, bf16[128,256]{1,0:T(8,128)(2,1)}, u32[]{:S(2)}) copy-start(bf16[128,256]{1,0:T(8,128)(2,1)} %param.18) | copy-start | bytes 196612
  7.2 15.8 %copy-start.6 = (bf16[128,256]{1,0:T(8,128)(2,1)S(1)}, bf16[128,256]{1,0:T(8,128)(2,1)}, u32[]{:S(2)}) copy-start(bf16[128,256]{1,0:T(8,128)(2,1)} %param.16) | copy-start | bytes 196612
  7.2 15.9 %copy-start.7 = (bf16[128,256]{1,0:T(8,128)(2,1)S(1)}, bf16[128,256]{1,0:T(8,128)(2,1)}, u32[]{:S(2)}) copy-start(bf16[128,256]{1,0:T(8,128)(2,1)} %param.11) | copy-start | bytes 196612
  7.2 16.0 %copy-start.8 = (bf16[128,256]{1,0:T(8,128)(2,1)S(1)}, bf16[128,256]{1,0:T(8,128)(2,1)}, u32[]{:S(2)}) copy-start(bf16[128,256]{1,0:T(8,128)(2,1)} %param.17) | copy-start | bytes 196612
  7.2 16.2 %copy-start.9 = (bf16[128,256]{1,0:T(8,128)(2,1)S(1)}, bf16[128,256]{1,0:T(8,128)(2,1)}, u32[]{:S(2)}) copy-start(bf16[128,256]{1,0:T(8,128)(2,1)} %param.20) | copy-start | bytes 196612
  7.2 16.8 %copy-start.13 = (f32[256]{0:T(256)S(1)}, f32[256]{0:T(256)}, u32[]{:S(2)}) copy-start(f32[256]{0:T(256)} %param.15) | copy-start | bytes 3076
  7.3 126.6 %all-gather.3.cloned.1.call-start = ((), (), s32[]{:S(2)}) async-start(), calls=%async_computation | async-start | bytes 1114112 | tf_op jit(solution)/shard_map/all_gather | solution.py:24
  8.1 16.1 %copy-start.18 = (f32[2]{0:T(128)}, f32[2]{0:T(128)S(1)}, u32[]{:S(2)}) copy-start(f32[2]{0:T(128)S(1)} %get-tuple-element.73) | copy-start | bytes 28
  13.0 11.2 %copy-start.3 = (bf16[128,256]{1,0:T(8,128)(2,1)S(1)}, bf16[128,256]{1,0:T(8,128)(2,1)}, u32[]{:S(2)}) copy-start(bf16[128,256]{1,0:T(8,128)(2,1)} %param.12) | copy-start | bytes 196612
  15.7 8.7 %collective-permute-start = (bf16[98304]{0:T(1024)(128)(2,1)S(1)}, bf16[98304]{0:T(1024)(128)(2,1)S(1)}, u32[]{:S(2)}, u32[]{:S(2)}) collective-permute-start(bf16[98304]{0:T(1024)(128)(2,1)S(1)} %pad_maximum_fusion.2), channel_id=1, source_target_pairs={{0,32},{16,48},{32,64},{48,80},{64,96},{80,112},{96,128},{112,144}... | collective-permute-start | bytes 589832 | tf_op jit(solution)/shard_map/ppermute | solution.py:20
  22.0 2.5 %copy-start.10 = (f32[128,128]{1,0:T(8,128)}, f32[128,128]{1,0:T(8,128)S(1)}, u32[]{:S(2)}) copy-start(f32[128,128]{1,0:T(8,128)S(1)} %convert_maximum_fusion) | copy-start | bytes 196612
  24.4 28.8 %copy-start.4 = (bf16[2,128,128]{2,1,0:T(8,128)(2,1)}, bf16[2,128,128]{2,1,0:T(8,128)(2,1)S(1)}, u32[]{:S(2)}) copy-start(bf16[2,128,128]{2,1,0:T(8,128)(2,1)S(1)} %fusion.20) | copy-start | bytes 196612
  24.5 28.2 %collective-permute-start.1 = (bf16[196608]{0:T(1024)(128)(2,1)S(1)}, bf16[196608]{0:T(1024)(128)(2,1)S(1)}, u32[]{:S(2)}, u32[]{:S(2)}) collective-permute-start(bf16[196608]{0:T(1024)(128)(2,1)S(1)} %pad_maximum_fusion), channel_id=1, source_target_pairs={{0,16},{16,32},{32,48},{48,64},{64,80},{80,96},{96,112},{112,128},... | collective-permute-start | bytes 1179656 | tf_op jit(solution)/shard_map/ppermute | solution.py:20
  38.4 8.9 %collective-permute-start.2 = (bf16[98304]{0:T(1024)(128)(2,1)S(1)}, bf16[98304]{0:T(1024)(128)(2,1)S(1)}, u32[]{:S(2)}, u32[]{:S(2)}) collective-permute-start(bf16[98304]{0:T(1024)(128)(2,1)S(1)} %collective-permute-done), channel_id=1, source_target_pairs={{0,32},{16,48},{32,64},{48,80},{64,96},{80,112},{96,128},{112,144}... | collective-permute-start | bytes 589832 | tf_op jit(solution)/shard_map/ppermute | solution.py:20
  47.3 5.3 %collective-permute-start.3 = (bf16[98304]{0:T(1024)(128)(2,1)S(1)}, bf16[98304]{0:T(1024)(128)(2,1)S(1)}, u32[]{:S(2)}, u32[]{:S(2)}) collective-permute-start(bf16[98304]{0:T(1024)(128)(2,1)S(1)} %collective-permute-done.2), channel_id=1, source_target_pairs={{0,16},{16,32},{32,48},{48,64},{64,80},{80,96},{96,112},{112,128},... | collective-permute-start | bytes 589832 | tf_op jit(solution)/shard_map/ppermute | solution.py:20
  59.2 77.1 %copy-start.14 = (f32[128,2]{0,1:T(2,128)S(1)}, f32[128,2]{0,1:T(2,128)}, u32[]{:S(2)}) copy-start(f32[128,2]{0,1:T(2,128)} %get-tuple-element.62) | copy-start | bytes 3076
  59.2 77.1 %copy-start.15 = (f32[2]{0:T(128)S(1)}, f32[2]{0:T(128)}, u32[]{:S(2)}) copy-start(f32[2]{0:T(128)} %get-tuple-element.81) | copy-start | bytes 28
  59.3 77.1 %copy-start.16 = (f32[2]{0:T(128)S(1)}, f32[2]{0:T(128)}, u32[]{:S(2)}) copy-start(f32[2]{0:T(128)} %get-tuple-element.83) | copy-start | bytes 28
  59.3 77.1 %copy-start.17 = (f32[2]{0:T(128)S(1)}, f32[2]{0:T(128)}, u32[]{:S(2)}) copy-start(f32[2]{0:T(128)} %get-tuple-element.85) | copy-start | bytes 28
  136.8 12.7 %collective-permute-start.4 = (bf16[294912]{0:T(1024)(128)(2,1)S(1)}, bf16[294912]{0:T(1024)(128)(2,1)S(1)}, u32[]{:S(2)}, u32[]{:S(2)}) collective-permute-start(bf16[294912]{0:T(1024)(128)(2,1)S(1)} %constant_dynamic-update-slice_fusion.3), channel_id=1, source_target_pairs={{16,0},{32,16},{48,32},{64,48},{80,64},{96,80},{112,96},{128,112},... | collective-permute-start | bytes 1769480 | tf_op jit(solution)/shard_map/ppermute | solution.py:20
  149.6 1.5 copy-start.11
  149.6 1.5 copy-start.19
  149.7 12.8 %copy-start.5 = (bf16[2,128,128]{2,1,0:T(8,128)(2,1)S(1)}, bf16[2,128,128]{2,1,0:T(8,128)(2,1)}, u32[]{:S(2)}) copy-start(bf16[2,128,128]{2,1,0:T(8,128)(2,1)} %copy-done.4) | copy-start | bytes 196612
  149.7 11.4 %collective-permute-start.5 = (bf16[196608]{0:T(1024)(128)(2,1)S(1)}, bf16[196608]{0:T(1024)(128)(2,1)S(1)}, u32[]{:S(2)}, u32[]{:S(2)}) collective-permute-start(bf16[196608]{0:T(1024)(128)(2,1)S(1)} %pad_maximum_fusion.1), channel_id=1, source_target_pairs={{32,0},{48,16},{64,32},{80,48},{96,64},{112,80},{128,96},{144,112}... | collective-permute-start | bytes 1179656 | tf_op jit(solution)/shard_map/ppermute | solution.py:20
  161.2 9.2 %copy-start.12 = (f32[128,2]{0,1:T(2,128)S(1)}, f32[128,2]{0,1:T(2,128)}, u32[]{:S(2)}) copy-start(f32[128,2]{0,1:T(2,128)} %get-tuple-element.61) | copy-start | bytes 3076
  161.2 9.1 %collective-permute-start.6 = (bf16[98304]{0:T(1024)(128)(2,1)S(1)}, bf16[98304]{0:T(1024)(128)(2,1)S(1)}, u32[]{:S(2)}, u32[]{:S(2)}) collective-permute-start(bf16[98304]{0:T(1024)(128)(2,1)S(1)} %slice.460), channel_id=1, source_target_pairs={{32,0},{48,16},{64,32},{80,48},{96,64},{112,80},{128,96},{144,112}... | collective-permute-start | bytes 589832 | tf_op jit(solution)/shard_map/ppermute | solution.py:20
Sparse Core Ops, SparseCore 0:
  54.4 79.4 all-gather.2

commit v7 on v4

--- a/solution.py
+++ b/solution.py
@@ -12,6 +12,7 @@
 
 HIGH_PRECISION = lax.Precision.HIGHEST
 NORM_EPS = 1e-06
+TP = ("tp_outer", "tp_inner")
 
 
 def shifted(value, axis, steps):
@@ -20,8 +21,10 @@
     return lax.ppermute(value, axis, [(source, source + steps) for source in range(first, last)])
 
 
-def tp_sum(value, axis):
-    return jnp.sum(lax.all_gather(value, axis), axis=0)
+def tp_sum(value, axes):
+    for axis in reversed(axes):
+        value = jnp.sum(lax.all_gather(value, axis), axis=0)
+    return value
 
 
 def packed(*parts):
@@ -186,8 +189,8 @@
     lin_out = inner + carried * entry.T[:, :, None]
     flat = lin_out.reshape(tokens, heads * HD)
     scaled_grad = norm_gain[None, :] * as_float(lin_grad)
-    sums = tp_sum(jnp.stack([jnp.sum(flat * flat, axis=1), jnp.sum(flat * scaled_grad, axis=1)]), "tp")
-    width = lax.axis_size("tp") * heads * HD
+    sums = tp_sum(jnp.stack([jnp.sum(flat * flat, axis=1), jnp.sum(flat * scaled_grad, axis=1)]), TP)
+    width = lax.axis_size(TP) * heads * HD
     inverse = lax.rsqrt(sums[0] / width + NORM_EPS)
     cross = sums[1] / width
     norm_grad = (inverse[:, None] * scaled_grad - flat * (inverse**3 * cross)[:, None]).astype(
@@ -306,30 +309,39 @@
     )
 
 
+def split_mesh(mesh):
+    count = mesh.shape["tp"]
+    inner = math.isqrt(count)
+    if inner * inner != count:
+        inner = 1
+    devices = mesh.devices.reshape(mesh.shape["seq"], count // inner, inner)
+    return jax.sharding.Mesh(devices, ("seq",) + TP)
+
+
 def solution(mesh):
     return jax.shard_map(
         body,
-        mesh=mesh,
+        mesh=split_mesh(mesh),
         in_specs=(
-            P("seq", "tp"),
-            P("seq", "tp"),
-            P("seq", "tp"),
-            P("tp"),
-            P("tp"),
-            P("seq", "tp"),
-            P("seq", "tp"),
-            P("seq", "tp"),
-            P("seq", "tp"),
-            P("seq", "tp"),
+            P("seq", TP),
+            P("seq", TP),
+            P("seq", TP),
+            P(TP),
+            P(TP),
+            P("seq", TP),
+            P("seq", TP),
+            P("seq", TP),
+            P("seq", TP),
+            P("seq", TP),
             P(),
         ),
         out_specs=(
-            P("seq", "tp"),
-            P("seq", "tp"),
-            P("seq", "tp"),
-            P("seq", "tp"),
-            P("seq", "tp"),
-            P("seq", "tp"),
+            P("seq", TP),
+            P("seq", TP),
+            P("seq", TP),
+            P("seq", TP),
+            P("seq", TP),
+            P("seq", TP),
         ),
         check_vma=False,
     )

time: 112 us -> 107 us (0.955)
  blocking collectives: 14.8 us -> 10.5 us
  starting transfers between devices: 31.9 us -> 30.1 us
    all_gather x1 -> x2, blocking collectives: 14.8 us -> 10.5 us  [tp_sum(): value = jnp.sum(lax.all_gather(value, axis), axis=0)]
    ppermute x7, starting transfers between devices: 31.9 us -> 30.1 us  [shifted(): lax.ppermute(value, axis, [(source, source + steps) for source in range(f...]
  transfers between devices with their start and end apart: 7 -> 7, of which waited for: 6 -> 6; matrix products, arithmetic and copies ran while one was open for 5% -> 6% of each run, Pallas kernels for 0% -> 0%
where the time goes in v7:
time: 107 us; the launch traced here: 105 us
  waiting for transfers between devices  36.3 us (34%)
  starting transfers between devices  30.1 us (28%)
  local copies, waits for them, and re-layouts  11.2 us (10%)
  blocking collectives  10.5 us (10%)
  matrix products  8.02 us (7%)
  other arithmetic  5.17 us (5%)
  between operations  4.02 us (4%)
    ppermute x7, waiting for transfers between devices, shifted(): lax.ppermute(value, axis, [(source, source + steps) for source in range(f...  36.3 us
    ppermute x7, starting transfers between devices, shifted(): lax.ppermute(value, axis, [(source, source + steps) for source in range(f...  30.1 us
    all_gather x2, blocking collectives, tp_sum(): value = jnp.sum(lax.all_gather(value, axis), axis=0)  10.5 us
    unnamed x57, local copies, waits for them, and re-layouts  7.32 us
  transfers between devices with their start and end apart: 7, of which 6 were waited for; matrix products, arithmetic and copies ran while one was open for 6% of the time, Pallas kernels for 0%

profile of v7, /device:TPU:1, one launch (start us, length us, event | category | flops | bytes accessed | tf_op | source)
XLA Modules:
  0.0 105.3 jit_solution(13538039834838680584)
XLA Ops:
  0.8 0.7 multiply_exponential_fusion.2
  1.5 0.7 pad_add_fusion
  2.3 0.6 fusion.70
  5.5 0.9 copy.197
  6.4 0.9 copy.196
  7.3 1.0 copy.233
  8.3 0.2 convolution_convert_fusion
  8.6 4.4 %collective-permute-start = (bf16[98304]{0:T(1024)(128)(2,1)S(1)}, bf16[98304]{0:T(1024)(128)(2,1)S(1)}, u32[]{:S(2)}, u32[]{:S(2)}) collective-permute-start(bf16[98304]{0:T(1024)(128)(2,1)S(1)} %pad_maximum_fusion.2), channel_id=1, source_target_pairs={{0,32},{16,48},{32,64},{48,80},{64,96},{80,112},{96,128},{112,144}... | collective-permute-start | bytes 589832 | tf_op jit(solution)/shard_map/ppermute | solution.py:21
  13.5 0.7 slice_compare_fusion
  14.9 0.3 fusion.28
  15.2 0.2 fusion.20
  15.6 15.6 %collective-permute-start.1 = (bf16[196608]{0:T(1024)(128)(2,1)S(1)}, bf16[196608]{0:T(1024)(128)(2,1)S(1)}, u32[]{:S(2)}, u32[]{:S(2)}) collective-permute-start(bf16[196608]{0:T(1024)(128)(2,1)S(1)} %pad_maximum_fusion), channel_id=1, source_target_pairs={{0,16},{16,32},{32,48},{48,64},{64,80},{80,96},{96,112},{112,128},... | collective-permute-start | bytes 1179656 | tf_op jit(solution)/shard_map/ppermute | solution.py:21
  31.2 1.3 %collective-permute-start.2 = (bf16[98304]{0:T(1024)(128)(2,1)S(1)}, bf16[98304]{0:T(1024)(128)(2,1)S(1)}, u32[]{:S(2)}, u32[]{:S(2)}) collective-permute-start(bf16[98304]{0:T(1024)(128)(2,1)S(1)} %collective-permute-done), channel_id=1, source_target_pairs={{0,32},{16,48},{32,64},{48,80},{64,96},{80,112},{96,128},{112,144}... | collective-permute-start | bytes 589832 | tf_op jit(solution)/shard_map/ppermute | solution.py:21
  32.6 7.6 %collective-permute-done.2 = bf16[98304]{0:T(1024)(128)(2,1)S(1)} collective-permute-done((bf16[98304]{0:T(1024)(128)(2,1)S(1)}, bf16[98304]{0:T(1024)(128)(2,1)S(1)}, u32[]{:S(2)}, u32[]{:S(2)}) %collective-permute-start.2) | collective-permute-done | bytes 196640 | tf_op jit(solution)/shard_map/ppermute | solution.py:21
  40.1 2.7 %collective-permute-start.3 = (bf16[98304]{0:T(1024)(128)(2,1)S(1)}, bf16[98304]{0:T(1024)(128)(2,1)S(1)}, u32[]{:S(2)}, u32[]{:S(2)}) collective-permute-start(bf16[98304]{0:T(1024)(128)(2,1)S(1)} %collective-permute-done.2), channel_id=1, source_target_pairs={{0,16},{16,32},{32,48},{48,64},{64,80},{80,96},{96,112},{112,128},... | collective-permute-start | bytes 589832 | tf_op jit(solution)/shard_map/ppermute | solution.py:21
  42.9 2.6 %collective-permute-done.3 = bf16[98304]{0:T(1024)(128)(2,1)S(1)} collective-permute-done((bf16[98304]{0:T(1024)(128)(2,1)S(1)}, bf16[98304]{0:T(1024)(128)(2,1)S(1)}, u32[]{:S(2)}, u32[]{:S(2)}) %collective-permute-start.3) | collective-permute-done | bytes 196640 | tf_op jit(solution)/shard_map/ppermute | solution.py:21
  45.7 0.3 fusion.15
  46.0 0.2 multiply_reduce_fusion.1
  46.5 5.2 %all-gather.2 = f32[4,2,128]{2,1,0:T(2,128)S(1)} all-gather(f32[1,2,128]{2,1,0:T(2,128)S(1)} %maximum_bitcast_fusion), channel_id=2, replica_groups=mesh['seq'=64,'tp_outer'=4,'tp_inner'=4] {'tp_inner'}, dimensions={0}, use_global_device_ids=true | all-gather | bytes 5120 | tf_op jit(solution)/shard_map/all_gather | solution.py:26
  51.8 5.2 %all-gather.3 = f32[4,2,128]{2,1,0:T(2,128)S(1)} all-gather(f32[1,2,128]{2,1,0:T(2,128)S(1)} %bitcast.288), channel_id=3, replica_groups=mesh['seq'=64,'tp_outer'=4,'tp_inner'=4] {'tp_outer'}, dimensions={0}, use_global_device_ids=true | all-gather | bytes 5120 | tf_op jit(solution)/shard_map/all_gather | solution.py:26
  57.5 1.3 %fusion.71 = (f32[2,128]{1,0:T(2,128)S(1)}, f32[2,128,768]{1,2,0:T(8,128)}) fusion(bf16[768,2,128]{2,0,1:T(8,128)(2,1)S(1)} %constant_dynamic-update-slice_fusion, bf16[128,2,128]{0,2,1:T(8,128)(2,1)S(1)} %bitcast.249, pred[128,768]{0,1:T(8,128)(4,1)S(1)} %fusion.28), kind=kOutput, calls=%fused_computation.161 | convolution fusion | flops 51118848 | bytes 1344512 | tf_op jit(solution)/shard_map/sub | solution.py:241
  58.8 0.6 fusion.73
  59.4 0.4 copy-done.12
  59.8 0.7 fusion.24
  61.2 1.4 %fusion.8 = bf16[2,128,768]{1,2,0:T(8,128)(2,1)S(1)} fusion(bf16[768,2,128]{2,0,1:T(8,128)(2,1)S(1)} %copy-done.12, bf16[128,2,128]{0,2,1:T(8,128)(2,1)S(1)} %bitcast.287, f32[2,128]{1,0:T(2,128)S(1)} %bitcast.291, f32[2,128,768]{1,2,0:T(8,128)} %get-tuple-element.75, f32[2,128]{1,0:T(2,128)S(1)} %get-tuple-element.74), kind=kOutput, calls=%fused_computation.12 | convolution fusion | flops 51118080 | bytes 1640448 | tf_op jit(solution)/shard_map/thd,uhd->htu/dot_general | solution.py:106
  62.6 0.3 fusion.72
  63.1 0.3 broadcast_multiply_fusion.1
  63.5 3.5 %collective-permute-start.4 = (bf16[294912]{0:T(1024)(128)(2,1)S(1)}, bf16[294912]{0:T(1024)(128)(2,1)S(1)}, u32[]{:S(2)}, u32[]{:S(2)}) collective-permute-start(bf16[294912]{0:T(1024)(128)(2,1)S(1)} %constant_dynamic-update-slice_fusion.3), channel_id=1, source_target_pairs={{16,0},{32,16},{48,32},{64,48},{80,64},{96,80},{112,96},{128,112},... | collective-permute-start | bytes 1769480 | tf_op jit(solution)/shard_map/ppermute | solution.py:21
  67.3 0.2 fusion.21
  67.5 0.2 fusion.13
  67.7 11.2 %collective-permute-done.4 = bf16[294912]{0:T(1024)(128)(2,1)S(1)} collective-permute-done((bf16[294912]{0:T(1024)(128)(2,1)S(1)}, bf16[294912]{0:T(1024)(128)(2,1)S(1)}, u32[]{:S(2)}, u32[]{:S(2)}) %collective-permute-start.4) | collective-permute-done | bytes 589856 | tf_op jit(solution)/shard_map/ppermute | solution.py:21
  79.1 0.8 pad_maximum_fusion.1
  79.9 1.3 %collective-permute-start.5 = (bf16[196608]{0:T(1024)(128)(2,1)}, bf16[196608]{0:T(1024)(128)(2,1)S(1)}, u32[]{:S(2)}, u32[]{:S(2)}) collective-permute-start(bf16[196608]{0:T(1024)(128)(2,1)} %pad_maximum_fusion.1), channel_id=1, source_target_pairs={{32,0},{48,16},{64,32},{80,48},{96,64},{112,80},{128,96},{144,112}... | collective-permute-start | bytes 1179656 | tf_op jit(solution)/shard_map/ppermute | solution.py:21
  81.2 0.2 fusion.22
  81.3 0.7 copy.175
  82.1 0.3 fusion.19
  82.4 0.7 copy.178
  83.2 8.3 %collective-permute-done.5 = bf16[196608]{0:T(1024)(128)(2,1)S(1)} collective-permute-done((bf16[196608]{0:T(1024)(128)(2,1)}, bf16[196608]{0:T(1024)(128)(2,1)S(1)}, u32[]{:S(2)}, u32[]{:S(2)}) %collective-permute-start.5) | collective-permute-done | bytes 393248 | tf_op jit(solution)/shard_map/ppermute | solution.py:21
  91.5 1.3 %collective-permute-start.6 = (bf16[98304]{0:T(1024)(128)(2,1)S(1)}, bf16[98304]{0:T(1024)(128)(2,1)S(1)}, u32[]{:S(2)}, u32[]{:S(2)}) collective-permute-start(bf16[98304]{0:T(1024)(128)(2,1)S(1)} %slice.460), channel_id=1, source_target_pairs={{32,0},{48,16},{64,32},{80,48},{96,64},{112,80},{128,96},{144,112}... | collective-permute-start | bytes 589832 | tf_op jit(solution)/shard_map/ppermute | solution.py:21
  92.8 1.0 convolution_bitcast_fusion.4
  93.8 6.5 %collective-permute-done.6 = bf16[98304]{0:T(1024)(128)(2,1)S(1)} collective-permute-done((bf16[98304]{0:T(1024)(128)(2,1)S(1)}, bf16[98304]{0:T(1024)(128)(2,1)S(1)}, u32[]{:S(2)}, u32[]{:S(2)}) %collective-permute-start.6) | collective-permute-done | bytes 196640 | tf_op jit(solution)/shard_map/ppermute | solution.py:21
  100.5 0.3 fusion.12
  100.7 0.3 fusion.18
  101.0 0.7 copy.177
  101.9 0.9 fusion.30
  102.8 0.7 copy.180
  103.7 0.7 copy.179
  104.6 0.7 copy.176
  (113 shorter events, 4.2 us)
Async XLA Ops:
  0.6 7.7 %copy-start = (bf16[128,256]{1,0:T(8,128)(2,1)S(1)}, bf16[128,256]{1,0:T(8,128)(2,1)}, u32[]{:S(2)}) copy-start(bf16[128,256]{1,0:T(8,128)(2,1)} %param.13) | copy-start | bytes 196612
  0.6 12.7 %copy-start.2 = (bf16[128,256]{1,0:T(8,128)(2,1)S(1)}, bf16[128,256]{1,0:T(8,128)(2,1)}, u32[]{:S(2)}) copy-start(bf16[128,256]{1,0:T(8,128)(2,1)} %param.19) | copy-start | bytes 196612
  0.7 12.6 %copy-start.1 = (bf16[128,256]{1,0:T(8,128)(2,1)S(1)}, bf16[128,256]{1,0:T(8,128)(2,1)}, u32[]{:S(2)}) copy-start(bf16[128,256]{1,0:T(8,128)(2,1)} %param.18) | copy-start | bytes 196612
  0.7 14.5 %copy-start.4 = (bf16[128,256]{1,0:T(8,128)(2,1)S(1)}, bf16[128,256]{1,0:T(8,128)(2,1)}, u32[]{:S(2)}) copy-start(bf16[128,256]{1,0:T(8,128)(2,1)} %param.12) | copy-start | bytes 196612
  0.7 13.6 %copy-start.8 = (bf16[128,256]{1,0:T(8,128)(2,1)S(1)}, bf16[128,256]{1,0:T(8,128)(2,1)}, u32[]{:S(2)}) copy-start(bf16[128,256]{1,0:T(8,128)(2,1)} %param.11) | copy-start | bytes 196612
  0.7 13.7 %copy-start.9 = (bf16[128,256]{1,0:T(8,128)(2,1)S(1)}, bf16[128,256]{1,0:T(8,128)(2,1)}, u32[]{:S(2)}) copy-start(bf16[128,256]{1,0:T(8,128)(2,1)} %param.17) | copy-start | bytes 196612
  0.7 13.8 %copy-start.10 = (bf16[128,256]{1,0:T(8,128)(2,1)S(1)}, bf16[128,256]{1,0:T(8,128)(2,1)}, u32[]{:S(2)}) copy-start(bf16[128,256]{1,0:T(8,128)(2,1)} %param.20) | copy-start | bytes 196612
  8.6 7.0 %collective-permute-start = (bf16[98304]{0:T(1024)(128)(2,1)S(1)}, bf16[98304]{0:T(1024)(128)(2,1)S(1)}, u32[]{:S(2)}, u32[]{:S(2)}) collective-permute-start(bf16[98304]{0:T(1024)(128)(2,1)S(1)} %pad_maximum_fusion.2), channel_id=1, source_target_pairs={{0,32},{16,48},{32,64},{48,80},{64,96},{80,112},{96,128},{112,144}... | collective-permute-start | bytes 589832 | tf_op jit(solution)/shard_map/ppermute | solution.py:21
  15.4 43.4 %copy-start.6 = (bf16[2,128,128]{2,1,0:T(8,128)(2,1)}, bf16[2,128,128]{2,1,0:T(8,128)(2,1)S(1)}, u32[]{:S(2)}) copy-start(bf16[2,128,128]{2,1,0:T(8,128)(2,1)S(1)} %fusion.20) | copy-start | bytes 196612
  15.6 29.9 %collective-permute-start.1 = (bf16[196608]{0:T(1024)(128)(2,1)S(1)}, bf16[196608]{0:T(1024)(128)(2,1)S(1)}, u32[]{:S(2)}, u32[]{:S(2)}) collective-permute-start(bf16[196608]{0:T(1024)(128)(2,1)S(1)} %pad_maximum_fusion), channel_id=1, source_target_pairs={{0,16},{16,32},{32,48},{48,64},{64,80},{80,96},{96,112},{112,128},... | collective-permute-start | bytes 1179656 | tf_op jit(solution)/shard_map/ppermute | solution.py:21
  31.2 8.9 %collective-permute-start.2 = (bf16[98304]{0:T(1024)(128)(2,1)S(1)}, bf16[98304]{0:T(1024)(128)(2,1)S(1)}, u32[]{:S(2)}, u32[]{:S(2)}) collective-permute-start(bf16[98304]{0:T(1024)(128)(2,1)S(1)} %collective-permute-done), channel_id=1, source_target_pairs={{0,32},{16,48},{32,64},{48,80},{64,96},{80,112},{96,128},{112,144}... | collective-permute-start | bytes 589832 | tf_op jit(solution)/shard_map/ppermute | solution.py:21
  40.1 5.3 %collective-permute-start.3 = (bf16[98304]{0:T(1024)(128)(2,1)S(1)}, bf16[98304]{0:T(1024)(128)(2,1)S(1)}, u32[]{:S(2)}, u32[]{:S(2)}) collective-permute-start(bf16[98304]{0:T(1024)(128)(2,1)S(1)} %collective-permute-done.2), channel_id=1, source_target_pairs={{0,16},{16,32},{32,48},{48,64},{64,80},{80,96},{96,112},{112,128},... | collective-permute-start | bytes 589832 | tf_op jit(solution)/shard_map/ppermute | solution.py:21
  45.5 0.9 copy-start.3
  45.5 0.9 copy-start.13
  57.5 1.3 %copy-start.11 = (bf16[768,2,128]{2,0,1:T(8,128)(2,1)}, bf16[768,2,128]{2,0,1:T(8,128)(2,1)S(1)}, u32[]{:S(2)}) copy-start(bf16[768,2,128]{2,0,1:T(8,128)(2,1)S(1)} %constant_dynamic-update-slice_fusion.1) | copy-start | bytes 1179652
  58.8 1.0 copy-start.12
  59.8 1.1 %copy-start.7 = (f32[768,2,128]{0,2,1:T(8,128)}, f32[768,2,128]{0,2,1:T(8,128)S(1)}, u32[]{:S(2)}) copy-start(f32[768,2,128]{0,2,1:T(8,128)S(1)} %get-tuple-element.79) | copy-start | bytes 2359300
  63.5 15.4 %collective-permute-start.4 = (bf16[294912]{0:T(1024)(128)(2,1)S(1)}, bf16[294912]{0:T(1024)(128)(2,1)S(1)}, u32[]{:S(2)}, u32[]{:S(2)}) collective-permute-start(bf16[294912]{0:T(1024)(128)(2,1)S(1)} %constant_dynamic-update-slice_fusion.3), channel_id=1, source_target_pairs={{16,0},{32,16},{48,32},{64,48},{80,64},{96,80},{112,96},{128,112},... | collective-permute-start | bytes 1769480 | tf_op jit(solution)/shard_map/ppermute | solution.py:21
  79.9 11.6 %collective-permute-start.5 = (bf16[196608]{0:T(1024)(128)(2,1)}, bf16[196608]{0:T(1024)(128)(2,1)S(1)}, u32[]{:S(2)}, u32[]{:S(2)}) collective-permute-start(bf16[196608]{0:T(1024)(128)(2,1)} %pad_maximum_fusion.1), channel_id=1, source_target_pairs={{32,0},{48,16},{64,32},{80,48},{96,64},{112,80},{128,96},{144,112}... | collective-permute-start | bytes 1179656 | tf_op jit(solution)/shard_map/ppermute | solution.py:21
  91.5 8.8 %collective-permute-start.6 = (bf16[98304]{0:T(1024)(128)(2,1)S(1)}, bf16[98304]{0:T(1024)(128)(2,1)S(1)}, u32[]{:S(2)}, u32[]{:S(2)}) collective-permute-start(bf16[98304]{0:T(1024)(128)(2,1)S(1)} %slice.460), channel_id=1, source_target_pairs={{32,0},{48,16},{64,32},{80,48},{96,64},{112,80},{128,96},{144,112}... | collective-permute-start | bytes 589832 | tf_op jit(solution)/shard_map/ppermute | solution.py:21
  93.8 6.9 %copy-start.5 = (bf16[128,256]{1,0:T(8,128)(2,1)S(1)}, bf16[128,256]{1,0:T(8,128)(2,1)}, u32[]{:S(2)}) copy-start(bf16[128,256]{1,0:T(8,128)(2,1)} %param.12) | copy-start | bytes 196612

commit v8 on v7

--- a/solution.py
+++ b/solution.py
@@ -28,15 +28,15 @@
 
 
 def packed(*parts):
-    return jnp.concatenate([part.reshape(-1) for part in parts])
-
-
-def unpacked(flat, shapes):
+    return jnp.concatenate([part.reshape(-1, part.shape[-1]) for part in parts], 0)
+
+
+def unpacked(block, shapes):
     out, at = [], 0
     for shape in shapes:
-        size = math.prod(shape)
-        out.append(flat[at : at + size].reshape(shape))
-        at += size
+        rows = math.prod(shape) // block.shape[1]
+        out.append(block[at : at + rows].reshape(shape))
+        at += rows
     return out
 
 
@@ -103,7 +103,7 @@
 
 
 def score_grads(probs, grads, value_part, delta):
-    grad_probs = jnp.einsum("thd,uhd->htu", grads, value_part, preferred_element_type=jnp.float32)
+    grad_probs = jnp.einsum("thd,hud->htu", grads, value_part, preferred_element_type=jnp.float32)
     return (probs * (grad_probs - delta.T[:, :, None])).astype(jnp.bfloat16)
 
 
@@ -157,9 +157,11 @@
     behind = jnp.where(
         ((firsts[1:] == lasts[:-1]) & (firsts[1:] == lasts[1:]))[:, None], full_decay[None, :], 0.0
     )
-    kv_shape = soft_keys.shape
+    key_major = soft_keys.transpose(1, 0, 2)
+    value_major = soft_values.transpose(1, 0, 2)
+    kv_shape = key_major.shape
     state_shape = summary.shape
-    unit = packed(soft_keys, soft_values, summary.astype(jnp.bfloat16))
+    unit = packed(key_major, value_major, summary.astype(jnp.bfloat16))
     size = unit.shape[0]
     two_back = shifted(unit, "seq", 2)
     four_back = shifted(two_back, "seq", 2)
@@ -222,10 +224,10 @@
     )
 
     key_window = jnp.concatenate(
-        [received[back - 1][0] for back in range(REACH - 1, 0, -1)] + [soft_keys], 0
+        [received[back - 1][0] for back in range(REACH - 1, 0, -1)] + [key_major], 1
     )
     value_window = jnp.concatenate(
-        [received[back - 1][1] for back in range(REACH - 1, 0, -1)] + [soft_values], 0
+        [received[back - 1][1] for back in range(REACH - 1, 0, -1)] + [value_major], 1
     )
     query_place = jnp.arange(tokens, dtype=jnp.int32)
     key_place = jnp.arange(REACH * tokens, dtype=jnp.int32) - (REACH - 1) * tokens
@@ -233,7 +235,7 @@
         key_place[None, :] <= query_place[:, None]
     )
     soft_scores = (
-        jnp.einsum("thd,uhd->htu", soft_queries, key_window, preferred_element_type=jnp.float32)
+        jnp.einsum("thd,hud->htu", soft_queries, key_window, preferred_element_type=jnp.float32)
         * scale
     )
     soft_scores = jnp.where(visible[None], soft_scores, -jnp.inf)
@@ -243,30 +245,30 @@
     probs = expo / total[..., None]
     probs_half = probs.astype(jnp.bfloat16)
     attended = jnp.einsum(
-        "htu,uhd->thd", probs_half, value_window, preferred_element_type=jnp.float32
+        "htu,hud->thd", probs_half, value_window, preferred_element_type=jnp.float32
     )
     delta = jnp.sum(as_float(soft_grads) * attended, axis=-1)
     grad_scores = score_grads(probs, soft_grads, value_window, delta)
     soft_query_grad = (
-        jnp.einsum("htu,uhd->thd", grad_scores, key_window, preferred_element_type=jnp.float32)
+        jnp.einsum("htu,hud->thd", grad_scores, key_window, preferred_element_type=jnp.float32)
         * scale
     )
     key_terms = (
-        jnp.einsum("htu,thd->uhd", grad_scores, soft_queries, preferred_element_type=jnp.float32)
+        jnp.einsum("htu,thd->hud", grad_scores, soft_queries, preferred_element_type=jnp.float32)
         * scale
     )
     value_terms = jnp.einsum(
-        "htu,thd->uhd", probs_half, soft_grads, preferred_element_type=jnp.float32
-    )
-    soft_key_grad = key_terms[(REACH - 1) * tokens :]
-    soft_value_grad = value_terms[(REACH - 1) * tokens :]
+        "htu,thd->hud", probs_half, soft_grads, preferred_element_type=jnp.float32
+    )
+    soft_key_grad = key_terms[:, (REACH - 1) * tokens :]
+    soft_value_grad = value_terms[:, (REACH - 1) * tokens :]
     items = {}
     for back in range(1, REACH):
         lower = (REACH - 1 - back) * tokens
         chain = jnp.prod(behind[REACH - back : REACH - 1], axis=0)
         items[back] = packed(
-            key_terms[lower : lower + tokens],
-            value_terms[lower : lower + tokens],
+            key_terms[:, lower : lower + tokens],
+            value_terms[:, lower : lower + tokens],
             chain[:, None, None] * back_summary,
         )
     size = items[1].shape[0]
@@ -304,8 +306,8 @@
         merge_heads(lin_key_grad),
         merge_heads(lin_value_grad),
         merge_heads(soft_query_grad),
-        merge_heads(soft_key_grad),
-        merge_heads(soft_value_grad),
+        merge_heads(soft_key_grad.transpose(1, 0, 2)),
+        merge_heads(soft_value_grad.transpose(1, 0, 2)),
     )
 
 

time: 107 us -> 109 us (1.019)
  waiting for transfers between devices: 36.3 us -> 38.3 us
    ppermute x7, waiting for transfers between devices: 36.3 us -> 38.3 us  [shifted(): lax.ppermute(value, axis, [(source, source + steps) for source in range(f...]
    slice x20 -> x9, local copies, waits for them, and re-layouts: 1.3 us -> 0.17 us  [the longest x5 0.1 us: unpacked(): out.append(block[at:at + rows].reshape(shape))]
    unnamed x57 -> x47, local copies, waits for them, and re-layouts: 7.32 us -> 7.22 us
  transfers between devices with their start and end apart: 7 -> 7, of which waited for: 6 -> 6; matrix products, arithmetic and copies ran while one was open for 6% -> 4% of each run, Pallas kernels for 0% -> 0%
where the time goes in v8:
time: 109 us; the launch traced here: 108 us
  waiting for transfers between devices  38.3 us (35%)
  starting transfers between devices  30.1 us (28%)
  local copies, waits for them, and re-layouts  10.9 us (10%)
  blocking collectives  10.5 us (10%)
  matrix products  8.03 us (7%)
  other arithmetic  6.13 us (6%)
  between operations  3.86 us (4%)
    ppermute x7, waiting for transfers between devices, shifted(): lax.ppermute(value, axis, [(source, source + steps) for source in range(f...  38.3 us
    ppermute x7, starting transfers between devices, shifted(): lax.ppermute(value, axis, [(source, source + steps) for source in range(f...  30.1 us
    all_gather x2, blocking collectives, tp_sum(): value = jnp.sum(lax.all_gather(value, axis), axis=0)  10.5 us
    unnamed x47, local copies, waits for them, and re-layouts  7.22 us
  transfers between devices with their start and end apart: 7, of which 6 were waited for; matrix products, arithmetic and copies ran while one was open for 4% of the time, Pallas kernels for 0%

profile of v8, /device:TPU:1, one launch (start us, length us, event | category | flops | bytes accessed | tf_op | source)
XLA Modules:
  0.0 107.9 jit_solution(13726277644587342608)
XLA Ops:
  0.7 0.7 multiply_exponential_fusion.2
  1.4 0.7 pad_add_fusion
  2.2 0.6 fusion.88
  5.4 1.0 copy.94
  6.5 1.0 copy.96
  7.6 1.0 copy.189
  8.7 1.0 convolution_convert_fusion
  9.7 4.4 %collective-permute-start = (bf16[768,128]{1,0:T(8,128)(2,1)S(1)}, bf16[768,128]{1,0:T(8,128)(2,1)S(1)}, u32[]{:S(2)}, u32[]{:S(2)}) collective-permute-start(bf16[768,128]{1,0:T(8,128)(2,1)S(1)} %pad_maximum_fusion.2), channel_id=1, source_target_pairs={{0,32},{16,48},{32,64},{48,80},{64,96},{80,112},{96,128},{112,144}... | collective-permute-start | bytes 589832 | tf_op jit(solution)/shard_map/ppermute | solution.py:21
  14.4 0.7 slice_compare_fusion
  15.4 0.3 fusion.27
  15.7 0.2 fusion.19
  16.0 0.7 collective-permute-done
  16.7 15.6 %collective-permute-start.1 = (bf16[1536,128]{1,0:T(8,128)(2,1)S(1)}, bf16[1536,128]{1,0:T(8,128)(2,1)S(1)}, u32[]{:S(2)}, u32[]{:S(2)}) collective-permute-start(bf16[1536,128]{1,0:T(8,128)(2,1)S(1)} %pad_maximum_fusion), channel_id=1, source_target_pairs={{0,16},{16,32},{32,48},{48,64},{64,80},{80,96},{96,112},{112,128},... | collective-permute-start | bytes 1179656 | tf_op jit(solution)/shard_map/ppermute | solution.py:21
  32.4 1.3 %collective-permute-start.2 = (bf16[768,128]{1,0:T(8,128)(2,1)S(1)}, bf16[768,128]{1,0:T(8,128)(2,1)S(1)}, u32[]{:S(2)}, u32[]{:S(2)}) collective-permute-start(bf16[768,128]{1,0:T(8,128)(2,1)S(1)} %collective-permute-done), channel_id=1, source_target_pairs={{0,32},{16,48},{32,64},{48,80},{64,96},{80,112},{96,128},{112,144}... | collective-permute-start | bytes 589832 | tf_op jit(solution)/shard_map/ppermute | solution.py:21
  33.7 7.6 %collective-permute-done.2 = bf16[768,128]{1,0:T(8,128)(2,1)S(1)} collective-permute-done((bf16[768,128]{1,0:T(8,128)(2,1)S(1)}, bf16[768,128]{1,0:T(8,128)(2,1)S(1)}, u32[]{:S(2)}, u32[]{:S(2)}) %collective-permute-start.2) | collective-permute-done | bytes 196640 | tf_op jit(solution)/shard_map/ppermute | solution.py:21
  41.3 2.7 %collective-permute-start.3 = (bf16[768,128]{1,0:T(8,128)(2,1)S(1)}, bf16[768,128]{1,0:T(8,128)(2,1)S(1)}, u32[]{:S(2)}, u32[]{:S(2)}) collective-permute-start(bf16[768,128]{1,0:T(8,128)(2,1)S(1)} %collective-permute-done.2), channel_id=1, source_target_pairs={{0,16},{16,32},{32,48},{48,64},{64,80},{80,96},{96,112},{112,128},... | collective-permute-start | bytes 589832 | tf_op jit(solution)/shard_map/ppermute | solution.py:21
  44.1 2.6 %collective-permute-done.3 = bf16[768,128]{1,0:T(8,128)(2,1)S(1)} collective-permute-done((bf16[768,128]{1,0:T(8,128)(2,1)S(1)}, bf16[768,128]{1,0:T(8,128)(2,1)S(1)}, u32[]{:S(2)}, u32[]{:S(2)}) %collective-permute-start.3) | collective-permute-done | bytes 196640 | tf_op jit(solution)/shard_map/ppermute | solution.py:21
  46.9 0.3 fusion.14
  47.2 0.2 multiply_reduce_fusion.1
  47.7 5.2 %all-gather.2 = f32[4,2,128]{2,1,0:T(2,128)S(1)} all-gather(f32[1,2,128]{2,1,0:T(2,128)S(1)} %maximum_bitcast_fusion), channel_id=2, replica_groups=mesh['seq'=64,'tp_outer'=4,'tp_inner'=4] {'tp_inner'}, dimensions={0}, use_global_device_ids=true | all-gather | bytes 5120 | tf_op jit(solution)/shard_map/all_gather | solution.py:26
  52.9 5.2 %all-gather.3 = f32[4,2,128]{2,1,0:T(2,128)S(1)} all-gather(f32[1,2,128]{2,1,0:T(2,128)S(1)} %bitcast.322), channel_id=3, replica_groups=mesh['seq'=64,'tp_outer'=4,'tp_inner'=4] {'tp_outer'}, dimensions={0}, use_global_device_ids=true | all-gather | bytes 5120 | tf_op jit(solution)/shard_map/all_gather | solution.py:26
  58.9 1.3 %fusion.89 = (f32[2,128]{1,0:T(2,128)S(1)}, f32[2,128,768]{1,2,0:T(8,128)}) fusion(bf16[2,768,128]{2,1,0:T(8,128)(2,1)S(1)} %bitcast_dynamic-update-slice_fusion.1, pred[128,768]{0,1:T(8,128)(4,1)S(1)} %fusion.27, bf16[128,256]{1,0:T(8,128)(2,1)S(1)} %copy-done), kind=kOutput, calls=%fused_computation.166 | convolution fusion | flops 51118848 | bytes 1344512 | tf_op jit(solution)/shard_map/sub | solution.py:243
  60.2 0.6 fusion.93
  60.7 0.4 copy-done.8
  61.2 0.7 fusion.23
  61.9 1.4 %fusion.7 = bf16[2,128,768]{1,2,0:T(8,128)(2,1)S(1)} fusion(bf16[2,768,128]{2,1,0:T(8,128)(2,1)S(1)} %copy-done.8, bf16[128,2,128]{0,2,1:T(8,128)(2,1)S(1)} %bitcast.321, f32[2,128]{1,0:T(2,128)S(1)} %bitcast.325, f32[2,128,768]{1,2,0:T(8,128)} %get-tuple-element.75, f32[2,128]{1,0:T(2,128)S(1)} %get-tuple-element.74), kind=kOutput, calls=%fused_computation.10 | convolution fusion | flops 51118080 | bytes 1640448 | tf_op jit(solution)/shard_map/thd,hud->htu/dot_general | solution.py:106
  63.3 0.2 fusion.92
  63.6 0.3 broadcast_multiply_fusion.1
  64.0 3.5 %collective-permute-start.4 = (bf16[2304,128]{1,0:T(8,128)(2,1)S(1)}, bf16[2304,128]{1,0:T(8,128)(2,1)S(1)}, u32[]{:S(2)}, u32[]{:S(2)}) collective-permute-start(bf16[2304,128]{1,0:T(8,128)(2,1)S(1)} %constant_dynamic-update-slice_fusion.10), channel_id=1, source_target_pairs={{16,0},{32,16},{48,32},{64,48},{80,64},{96,80},{112,96},{128,112},... | collective-permute-start | bytes 1769480 | tf_op jit(solution)/shard_map/ppermute | solution.py:21
  67.5 0.2 fusion.20
  67.8 11.6 %collective-permute-done.4 = bf16[2304,128]{1,0:T(8,128)(2,1)S(1)} collective-permute-done((bf16[2304,128]{1,0:T(8,128)(2,1)S(1)}, bf16[2304,128]{1,0:T(8,128)(2,1)S(1)}, u32[]{:S(2)}, u32[]{:S(2)}) %collective-permute-start.4) | collective-permute-done | bytes 589856 | tf_op jit(solution)/shard_map/ppermute | solution.py:21
  79.6 0.8 pad_maximum_fusion.1
  80.4 1.3 %collective-permute-start.5 = (bf16[1536,128]{1,0:T(8,128)(2,1)}, bf16[1536,128]{1,0:T(8,128)(2,1)}, u32[]{:S(2)}, u32[]{:S(2)}) collective-permute-start(bf16[1536,128]{1,0:T(8,128)(2,1)} %pad_maximum_fusion.1), channel_id=1, source_target_pairs={{32,0},{48,16},{64,32},{80,48},{96,64},{112,80},{128,96},{144,112}... | collective-permute-start | bytes 1179656 | tf_op jit(solution)/shard_map/ppermute | solution.py:21
  81.9 0.7 copy.126
  82.6 0.3 fusion.18
  82.9 0.7 copy.129
  83.7 8.4 %collective-permute-done.5 = bf16[1536,128]{1,0:T(8,128)(2,1)} collective-permute-done((bf16[1536,128]{1,0:T(8,128)(2,1)}, bf16[1536,128]{1,0:T(8,128)(2,1)}, u32[]{:S(2)}, u32[]{:S(2)}) %collective-permute-start.5) | collective-permute-done | bytes 393248 | tf_op jit(solution)/shard_map/ppermute | solution.py:21
  92.1 0.9 slice.277
  93.1 1.3 %collective-permute-start.6 = (bf16[768,128]{1,0:T(8,128)(2,1)S(1)}, bf16[768,128]{1,0:T(8,128)(2,1)S(1)}, u32[]{:S(2)}, u32[]{:S(2)}) collective-permute-start(bf16[768,128]{1,0:T(8,128)(2,1)S(1)} %slice.277), channel_id=1, source_target_pairs={{32,0},{48,16},{64,32},{80,48},{96,64},{112,80},{128,96},{144,112}... | collective-permute-start | bytes 589832 | tf_op jit(solution)/shard_map/ppermute | solution.py:21
  94.5 7.4 %collective-permute-done.6 = bf16[768,128]{1,0:T(8,128)(2,1)S(1)} collective-permute-done((bf16[768,128]{1,0:T(8,128)(2,1)S(1)}, bf16[768,128]{1,0:T(8,128)(2,1)S(1)}, u32[]{:S(2)}, u32[]{:S(2)}) %collective-permute-start.6) | collective-permute-done | bytes 196640 | tf_op jit(solution)/shard_map/ppermute | solution.py:21
  101.9 1.0 fusion.26
  102.9 0.3 fusion.11
  103.2 0.3 fusion.17
  103.5 0.7 copy.128
  104.3 0.9 fusion.41
  105.3 0.8 copy.131
  106.2 0.8 copy.130
  107.1 0.7 copy.127
  (92 shorter events, 3.3 us)
Async XLA Ops:
  0.6 58.2 %copy-start = (bf16[128,256]{1,0:T(8,128)(2,1)S(1)}, bf16[128,256]{1,0:T(8,128)(2,1)}, u32[]{:S(2)}) copy-start(bf16[128,256]{1,0:T(8,128)(2,1)} %param.17) | copy-start | bytes 196612
  0.6 15.1 %copy-start.3 = (bf16[128,256]{1,0:T(8,128)(2,1)S(1)}, bf16[128,256]{1,0:T(8,128)(2,1)}, u32[]{:S(2)}) copy-start(bf16[128,256]{1,0:T(8,128)(2,1)} %param.12) | copy-start | bytes 196612
  0.7 14.5 %copy-start.5 = (bf16[128,256]{1,0:T(8,128)(2,1)S(1)}, bf16[128,256]{1,0:T(8,128)(2,1)}, u32[]{:S(2)}) copy-start(bf16[128,256]{1,0:T(8,128)(2,1)} %param.11) | copy-start | bytes 196612
  0.7 14.6 %copy-start.6 = (bf16[128,256]{1,0:T(8,128)(2,1)S(1)}, bf16[128,256]{1,0:T(8,128)(2,1)}, u32[]{:S(2)}) copy-start(bf16[128,256]{1,0:T(8,128)(2,1)} %param.20) | copy-start | bytes 196612
  9.7 7.0 %collective-permute-start = (bf16[768,128]{1,0:T(8,128)(2,1)S(1)}, bf16[768,128]{1,0:T(8,128)(2,1)S(1)}, u32[]{:S(2)}, u32[]{:S(2)}) collective-permute-start(bf16[768,128]{1,0:T(8,128)(2,1)S(1)} %pad_maximum_fusion.2), channel_id=1, source_target_pairs={{0,32},{16,48},{32,64},{48,80},{64,96},{80,112},{96,128},{112,144}... | collective-permute-start | bytes 589832 | tf_op jit(solution)/shard_map/ppermute | solution.py:21
  16.7 29.9 %collective-permute-start.1 = (bf16[1536,128]{1,0:T(8,128)(2,1)S(1)}, bf16[1536,128]{1,0:T(8,128)(2,1)S(1)}, u32[]{:S(2)}, u32[]{:S(2)}) collective-permute-start(bf16[1536,128]{1,0:T(8,128)(2,1)S(1)} %pad_maximum_fusion), channel_id=1, source_target_pairs={{0,16},{16,32},{32,48},{48,64},{64,80},{80,96},{96,112},{112,128},... | collective-permute-start | bytes 1179656 | tf_op jit(solution)/shard_map/ppermute | solution.py:21
  32.4 8.9 %collective-permute-start.2 = (bf16[768,128]{1,0:T(8,128)(2,1)S(1)}, bf16[768,128]{1,0:T(8,128)(2,1)S(1)}, u32[]{:S(2)}, u32[]{:S(2)}) collective-permute-start(bf16[768,128]{1,0:T(8,128)(2,1)S(1)} %collective-permute-done), channel_id=1, source_target_pairs={{0,32},{16,48},{32,64},{48,80},{64,96},{80,112},{96,128},{112,144}... | collective-permute-start | bytes 589832 | tf_op jit(solution)/shard_map/ppermute | solution.py:21
  33.7 13.4 %copy-start.1 = (bf16[128,256]{1,0:T(8,128)(2,1)S(1)}, bf16[128,256]{1,0:T(8,128)(2,1)}, u32[]{:S(2)}) copy-start(bf16[128,256]{1,0:T(8,128)(2,1)} %param.13) | copy-start | bytes 196612
  41.3 5.3 %collective-permute-start.3 = (bf16[768,128]{1,0:T(8,128)(2,1)S(1)}, bf16[768,128]{1,0:T(8,128)(2,1)S(1)}, u32[]{:S(2)}, u32[]{:S(2)}) collective-permute-start(bf16[768,128]{1,0:T(8,128)(2,1)S(1)} %collective-permute-done.2), channel_id=1, source_target_pairs={{0,16},{16,32},{32,48},{48,64},{64,80},{80,96},{96,112},{112,128},... | collective-permute-start | bytes 589832 | tf_op jit(solution)/shard_map/ppermute | solution.py:21
  46.7 0.9 copy-start.2
  46.7 0.9 copy-start.9
  58.4 1.8 %copy-start.7 = (bf16[2,768,128]{2,1,0:T(8,128)(2,1)}, bf16[2,768,128]{2,1,0:T(8,128)(2,1)S(1)}, u32[]{:S(2)}) copy-start(bf16[2,768,128]{2,1,0:T(8,128)(2,1)S(1)} %bitcast_dynamic-update-slice_fusion) | copy-start | bytes 1179652
  60.2 1.0 copy-start.8
  61.2 6.6 %copy-start.4 = (f32[2,768,128]{2,1,0:T(8,128)}, f32[2,768,128]{2,1,0:T(8,128)S(1)}, u32[]{:S(2)}) copy-start(f32[2,768,128]{2,1,0:T(8,128)S(1)} %get-tuple-element.79) | copy-start | bytes 2359300
  64.0 15.4 %collective-permute-start.4 = (bf16[2304,128]{1,0:T(8,128)(2,1)S(1)}, bf16[2304,128]{1,0:T(8,128)(2,1)S(1)}, u32[]{:S(2)}, u32[]{:S(2)}) collective-permute-start(bf16[2304,128]{1,0:T(8,128)(2,1)S(1)} %constant_dynamic-update-slice_fusion.10), channel_id=1, source_target_pairs={{16,0},{32,16},{48,32},{64,48},{80,64},{96,80},{112,96},{128,112},... | collective-permute-start | bytes 1769480 | tf_op jit(solution)/shard_map/ppermute | solution.py:21
  80.4 11.7 %collective-permute-start.5 = (bf16[1536,128]{1,0:T(8,128)(2,1)}, bf16[1536,128]{1,0:T(8,128)(2,1)}, u32[]{:S(2)}, u32[]{:S(2)}) collective-permute-start(bf16[1536,128]{1,0:T(8,128)(2,1)} %pad_maximum_fusion.1), channel_id=1, source_target_pairs={{32,0},{48,16},{64,32},{80,48},{96,64},{112,80},{128,96},{144,112}... | collective-permute-start | bytes 1179656 | tf_op jit(solution)/shard_map/ppermute | solution.py:21
  93.1 8.8 %collective-permute-start.6 = (bf16[768,128]{1,0:T(8,128)(2,1)S(1)}, bf16[768,128]{1,0:T(8,128)(2,1)S(1)}, u32[]{:S(2)}, u32[]{:S(2)}) collective-permute-start(bf16[768,128]{1,0:T(8,128)(2,1)S(1)} %slice.277), channel_id=1, source_target_pairs={{32,0},{48,16},{64,32},{80,48},{96,64},{112,80},{128,96},{144,112}... | collective-permute-start | bytes 589832 | tf_op jit(solution)/shard_map/ppermute | solution.py:21

commit v9 on v7

--- a/solution.py
+++ b/solution.py
@@ -162,15 +162,14 @@
     unit = packed(soft_keys, soft_values, summary.astype(jnp.bfloat16))
     size = unit.shape[0]
     two_back = shifted(unit, "seq", 2)
-    four_back = shifted(two_back, "seq", 2)
     odd_back = shifted(jnp.concatenate([unit, two_back]), "seq", 1)
-    five_back = shifted(four_back, "seq", 1)
+    far_back = shifted(jnp.concatenate([two_back, odd_back[size:]]), "seq", 2)
     arrived = {
         1: odd_back[:size],
         2: two_back,
         3: odd_back[size:],
-        4: four_back,
-        5: five_back,
+        4: far_back[:size],
+        5: far_back[size:],
     }
     received = []
     state_in = jnp.zeros_like(summary)

time: 107 us -> 108 us (level)
  the two profiles are of different devices: /device:TPU:1 before, /device:TPU:481 now
where the time goes in v9:
time: 108 us; the launch traced here: 107 us
  waiting for transfers between devices  39.9 us (37%)
  starting transfers between devices  23.5 us (22%)
  blocking collectives  15.7 us (15%)
  local copies, waits for them, and re-layouts  10.8 us (10%)
  matrix products  8.17 us (8%)
  other arithmetic  5.22 us (5%)
  between operations  4.03 us (4%)
    ppermute x6, waiting for transfers between devices, shifted(): lax.ppermute(value, axis, [(source, source + steps) for source in range(f...  39.9 us
    ppermute x6, starting transfers between devices, shifted(): lax.ppermute(value, axis, [(source, source + steps) for source in range(f...  23.5 us
    all_gather x2, blocking collectives, tp_sum(): value = jnp.sum(lax.all_gather(value, axis), axis=0)  15.7 us
    unnamed x55, local copies, waits for them, and re-layouts  6.92 us
  transfers between devices with their start and end apart: 6, of which 6 were waited for; matrix products, arithmetic and copies ran while one was open for 6% of the time, Pallas kernels for 0%

profile of v9, /device:TPU:481, one launch (start us, length us, event | category | flops | bytes accessed | tf_op | source)
XLA Modules:
  0.0 107.4 jit_solution(16505647549511752601)
XLA Ops:
  0.8 0.7 multiply_exponential_fusion.2
  1.5 0.7 pad_add_fusion
  2.3 0.6 fusion.69
  5.5 0.9 copy.197
  6.4 0.9 copy.196
  7.3 1.0 copy.233
  8.3 0.2 convolution_convert_fusion
  8.6 4.8 %collective-permute-start = (bf16[98304]{0:T(1024)(128)(2,1)S(1)}, bf16[98304]{0:T(1024)(128)(2,1)S(1)}, u32[]{:S(2)}, u32[]{:S(2)}) collective-permute-start(bf16[98304]{0:T(1024)(128)(2,1)S(1)} %pad_maximum_fusion.3), channel_id=1, source_target_pairs={{0,32},{16,48},{32,64},{48,80},{64,96},{80,112},{96,128},{112,144}... | collective-permute-start | bytes 589832 | tf_op jit(solution)/shard_map/ppermute | solution.py:21
  13.9 0.7 slice_compare_fusion
  15.3 0.3 fusion.28
  15.6 0.2 fusion.20
  15.8 1.0 collective-permute-done
  16.9 6.8 %collective-permute-start.1 = (bf16[196608]{0:T(1024)(128)(2,1)S(1)}, bf16[196608]{0:T(1024)(128)(2,1)S(1)}, u32[]{:S(2)}, u32[]{:S(2)}) collective-permute-start(bf16[196608]{0:T(1024)(128)(2,1)S(1)} %pad_maximum_fusion), channel_id=1, source_target_pairs={{0,16},{16,32},{32,48},{48,64},{64,80},{80,96},{96,112},{112,128},... | collective-permute-start | bytes 1179656 | tf_op jit(solution)/shard_map/ppermute | solution.py:21
  23.7 4.7 %collective-permute-done.1 = bf16[196608]{0:T(1024)(128)(2,1)S(1)} collective-permute-done((bf16[196608]{0:T(1024)(128)(2,1)S(1)}, bf16[196608]{0:T(1024)(128)(2,1)S(1)}, u32[]{:S(2)}, u32[]{:S(2)}) %collective-permute-start.1) | collective-permute-done | bytes 393248 | tf_op jit(solution)/shard_map/ppermute | solution.py:21
  28.4 1.9 %collective-permute-start.2 = (bf16[196608]{0:T(1024)(128)(2,1)S(1)}, bf16[196608]{0:T(1024)(128)(2,1)S(1)}, u32[]{:S(2)}, u32[]{:S(2)}) collective-permute-start(bf16[196608]{0:T(1024)(128)(2,1)S(1)} %pad_maximum_fusion.1), channel_id=1, source_target_pairs={{0,32},{16,48},{32,64},{48,80},{64,96},{80,112},{96,128},{112,144}... | collective-permute-start | bytes 1179656 | tf_op jit(solution)/shard_map/ppermute | solution.py:21
  30.4 10.4 %collective-permute-done.2 = bf16[196608]{0:T(1024)(128)(2,1)S(1)} collective-permute-done((bf16[196608]{0:T(1024)(128)(2,1)S(1)}, bf16[196608]{0:T(1024)(128)(2,1)S(1)}, u32[]{:S(2)}, u32[]{:S(2)}) %collective-permute-start.2) | collective-permute-done | bytes 393248 | tf_op jit(solution)/shard_map/ppermute | solution.py:21
  41.0 0.3 fusion.15
  41.3 0.2 multiply_reduce_fusion.1
  41.8 8.0 %all-gather.2 = f32[4,2,128]{2,1,0:T(2,128)S(1)} all-gather(f32[1,2,128]{2,1,0:T(2,128)S(1)} %maximum_bitcast_fusion), channel_id=2, replica_groups=mesh['seq'=64,'tp_outer'=4,'tp_inner'=4] {'tp_inner'}, dimensions={0}, use_global_device_ids=true | all-gather | bytes 5120 | tf_op jit(solution)/shard_map/all_gather | solution.py:26
  49.8 7.8 %all-gather.3 = f32[4,2,128]{2,1,0:T(2,128)S(1)} all-gather(f32[1,2,128]{2,1,0:T(2,128)S(1)} %bitcast.288), channel_id=3, replica_groups=mesh['seq'=64,'tp_outer'=4,'tp_inner'=4] {'tp_outer'}, dimensions={0}, use_global_device_ids=true | all-gather | bytes 5120 | tf_op jit(solution)/shard_map/all_gather | solution.py:26
  58.1 1.3 %fusion.70 = (f32[2,128]{1,0:T(2,128)S(1)}, f32[2,128,768]{1,2,0:T(8,128)}) fusion(bf16[768,2,128]{2,0,1:T(8,128)(2,1)S(1)} %constant_dynamic-update-slice_fusion, bf16[128,2,128]{0,2,1:T(8,128)(2,1)S(1)} %bitcast.251, pred[128,768]{0,1:T(8,128)(4,1)S(1)} %fusion.28), kind=kOutput, calls=%fused_computation.161 | convolution fusion | flops 51118848 | bytes 1344512 | tf_op jit(solution)/shard_map/sub | solution.py:240
  59.4 0.6 fusion.72
  60.0 0.7 fusion.24
  61.4 1.5 %fusion.8 = bf16[2,128,768]{1,2,0:T(8,128)(2,1)S(1)} fusion(bf16[768,2,128]{2,0,1:T(8,128)(2,1)} %copy-done.11, bf16[128,2,128]{0,2,1:T(8,128)(2,1)S(1)} %bitcast.287, f32[2,128]{1,0:T(2,128)S(1)} %bitcast.291, f32[2,128,768]{1,2,0:T(8,128)} %get-tuple-element.75, f32[2,128]{1,0:T(2,128)S(1)} %get-tuple-element.74), kind=kOutput, calls=%fused_computation.12 | convolution fusion | flops 51118080 | bytes 1640448 | tf_op jit(solution)/shard_map/thd,uhd->htu/dot_general | solution.py:106
  62.9 0.3 fusion.71
  63.5 0.3 broadcast_multiply_fusion.1
  63.9 6.3 %collective-permute-start.3 = (bf16[294912]{0:T(1024)(128)(2,1)S(1)}, bf16[294912]{0:T(1024)(128)(2,1)S(1)}, u32[]{:S(2)}, u32[]{:S(2)}) collective-permute-start(bf16[294912]{0:T(1024)(128)(2,1)S(1)} %constant_dynamic-update-slice_fusion.3), channel_id=1, source_target_pairs={{16,0},{32,16},{48,32},{64,48},{80,64},{96,80},{112,96},{128,112},... | collective-permute-start | bytes 1769480 | tf_op jit(solution)/shard_map/ppermute | solution.py:21
  70.4 0.2 fusion.21
  70.6 0.2 fusion.13
  70.8 8.6 %collective-permute-done.3 = bf16[294912]{0:T(1024)(128)(2,1)S(1)} collective-permute-done((bf16[294912]{0:T(1024)(128)(2,1)S(1)}, bf16[294912]{0:T(1024)(128)(2,1)S(1)}, u32[]{:S(2)}, u32[]{:S(2)}) %collective-permute-start.3) | collective-permute-done | bytes 589856 | tf_op jit(solution)/shard_map/ppermute | solution.py:21
  79.6 0.8 pad_maximum_fusion.2
  80.4 1.9 %collective-permute-start.4 = (bf16[196608]{0:T(1024)(128)(2,1)}, bf16[196608]{0:T(1024)(128)(2,1)S(1)}, u32[]{:S(2)}, u32[]{:S(2)}) collective-permute-start(bf16[196608]{0:T(1024)(128)(2,1)} %pad_maximum_fusion.2), channel_id=1, source_target_pairs={{32,0},{48,16},{64,32},{80,48},{96,64},{112,80},{128,96},{144,112}... | collective-permute-start | bytes 1179656 | tf_op jit(solution)/shard_map/ppermute | solution.py:21
  82.3 0.2 fusion.22
  82.5 0.7 copy.175
  83.2 0.3 fusion.19
  83.6 0.7 copy.178
  84.3 8.8 %collective-permute-done.4 = bf16[196608]{0:T(1024)(128)(2,1)S(1)} collective-permute-done((bf16[196608]{0:T(1024)(128)(2,1)}, bf16[196608]{0:T(1024)(128)(2,1)S(1)}, u32[]{:S(2)}, u32[]{:S(2)}) %collective-permute-start.4) | collective-permute-done | bytes 393248 | tf_op jit(solution)/shard_map/ppermute | solution.py:21
  93.1 1.9 %collective-permute-start.5 = (bf16[98304]{0:T(1024)(128)(2,1)S(1)}, bf16[98304]{0:T(1024)(128)(2,1)S(1)}, u32[]{:S(2)}, u32[]{:S(2)}) collective-permute-start(bf16[98304]{0:T(1024)(128)(2,1)S(1)} %slice.473), channel_id=1, source_target_pairs={{32,0},{48,16},{64,32},{80,48},{96,64},{112,80},{128,96},{144,112}... | collective-permute-start | bytes 589832 | tf_op jit(solution)/shard_map/ppermute | solution.py:21
  95.0 1.0 convolution_bitcast_fusion.4
  96.0 6.4 %collective-permute-done.5 = bf16[98304]{0:T(1024)(128)(2,1)S(1)} collective-permute-done((bf16[98304]{0:T(1024)(128)(2,1)S(1)}, bf16[98304]{0:T(1024)(128)(2,1)S(1)}, u32[]{:S(2)}, u32[]{:S(2)}) %collective-permute-start.5) | collective-permute-done | bytes 196640 | tf_op jit(solution)/shard_map/ppermute | solution.py:21
  102.5 0.3 fusion.12
  102.8 0.3 fusion.18
  103.1 0.7 copy.177
  103.9 0.9 fusion.30
  104.9 0.7 copy.180
  105.8 0.7 copy.179
  106.5 0.2 fusion.23
  106.7 0.7 copy.176
  (110 shorter events, 4.0 us)
Async XLA Ops:
  0.6 7.7 %copy-start = (bf16[128,256]{1,0:T(8,128)(2,1)S(1)}, bf16[128,256]{1,0:T(8,128)(2,1)}, u32[]{:S(2)}) copy-start(bf16[128,256]{1,0:T(8,128)(2,1)} %param.13) | copy-start | bytes 196612
  0.6 13.1 %copy-start.2 = (bf16[128,256]{1,0:T(8,128)(2,1)S(1)}, bf16[128,256]{1,0:T(8,128)(2,1)}, u32[]{:S(2)}) copy-start(bf16[128,256]{1,0:T(8,128)(2,1)} %param.19) | copy-start | bytes 196612
  0.7 13.0 %copy-start.1 = (bf16[128,256]{1,0:T(8,128)(2,1)S(1)}, bf16[128,256]{1,0:T(8,128)(2,1)}, u32[]{:S(2)}) copy-start(bf16[128,256]{1,0:T(8,128)(2,1)} %param.18) | copy-start | bytes 196612
  0.7 14.9 %copy-start.4 = (bf16[128,256]{1,0:T(8,128)(2,1)S(1)}, bf16[128,256]{1,0:T(8,128)(2,1)}, u32[]{:S(2)}) copy-start(bf16[128,256]{1,0:T(8,128)(2,1)} %param.12) | copy-start | bytes 196612
  0.7 14.0 %copy-start.8 = (bf16[128,256]{1,0:T(8,128)(2,1)S(1)}, bf16[128,256]{1,0:T(8,128)(2,1)}, u32[]{:S(2)}) copy-start(bf16[128,256]{1,0:T(8,128)(2,1)} %param.11) | copy-start | bytes 196612
  0.7 14.1 %copy-start.9 = (bf16[128,256]{1,0:T(8,128)(2,1)S(1)}, bf16[128,256]{1,0:T(8,128)(2,1)}, u32[]{:S(2)}) copy-start(bf16[128,256]{1,0:T(8,128)(2,1)} %param.17) | copy-start | bytes 196612
  0.7 14.2 %copy-start.10 = (bf16[128,256]{1,0:T(8,128)(2,1)S(1)}, bf16[128,256]{1,0:T(8,128)(2,1)}, u32[]{:S(2)}) copy-start(bf16[128,256]{1,0:T(8,128)(2,1)} %param.20) | copy-start | bytes 196612
  8.6 8.3 %collective-permute-start = (bf16[98304]{0:T(1024)(128)(2,1)S(1)}, bf16[98304]{0:T(1024)(128)(2,1)S(1)}, u32[]{:S(2)}, u32[]{:S(2)}) collective-permute-start(bf16[98304]{0:T(1024)(128)(2,1)S(1)} %pad_maximum_fusion.3), channel_id=1, source_target_pairs={{0,32},{16,48},{32,64},{48,80},{64,96},{80,112},{96,128},{112,144}... | collective-permute-start | bytes 589832 | tf_op jit(solution)/shard_map/ppermute | solution.py:21
  15.8 42.0 %copy-start.6 = (bf16[2,128,128]{2,1,0:T(8,128)(2,1)}, bf16[2,128,128]{2,1,0:T(8,128)(2,1)S(1)}, u32[]{:S(2)}) copy-start(bf16[2,128,128]{2,1,0:T(8,128)(2,1)S(1)} %fusion.20) | copy-start | bytes 196612
  16.9 11.5 %collective-permute-start.1 = (bf16[196608]{0:T(1024)(128)(2,1)S(1)}, bf16[196608]{0:T(1024)(128)(2,1)S(1)}, u32[]{:S(2)}, u32[]{:S(2)}) collective-permute-start(bf16[196608]{0:T(1024)(128)(2,1)S(1)} %pad_maximum_fusion), channel_id=1, source_target_pairs={{0,16},{16,32},{32,48},{48,64},{64,80},{80,96},{96,112},{112,128},... | collective-permute-start | bytes 1179656 | tf_op jit(solution)/shard_map/ppermute | solution.py:21
  28.4 12.4 %collective-permute-start.2 = (bf16[196608]{0:T(1024)(128)(2,1)S(1)}, bf16[196608]{0:T(1024)(128)(2,1)S(1)}, u32[]{:S(2)}, u32[]{:S(2)}) collective-permute-start(bf16[196608]{0:T(1024)(128)(2,1)S(1)} %pad_maximum_fusion.1), channel_id=1, source_target_pairs={{0,32},{16,48},{32,64},{48,80},{64,96},{80,112},{96,128},{112,144}... | collective-permute-start | bytes 1179656 | tf_op jit(solution)/shard_map/ppermute | solution.py:21
  30.4 11.3 %copy-start.3 = (bf16[128,256]{1,0:T(8,128)(2,1)S(1)}, bf16[128,256]{1,0:T(8,128)(2,1)}, u32[]{:S(2)}) copy-start(bf16[128,256]{1,0:T(8,128)(2,1)} %param.16) | copy-start | bytes 196612
  30.4 11.3 %copy-start.12 = (f32[256]{0:T(256)S(1)}, f32[256]{0:T(256)}, u32[]{:S(2)}) copy-start(f32[256]{0:T(256)} %param.15) | copy-start | bytes 3076
  58.0 2.7 %copy-start.11 = (bf16[768,2,128]{2,0,1:T(8,128)(2,1)}, bf16[768,2,128]{2,0,1:T(8,128)(2,1)S(1)}, u32[]{:S(2)}) copy-start(bf16[768,2,128]{2,0,1:T(8,128)(2,1)S(1)} %constant_dynamic-update-slice_fusion.1) | copy-start | bytes 1179652
  60.0 1.1 %copy-start.7 = (f32[768,2,128]{0,2,1:T(8,128)}, f32[768,2,128]{0,2,1:T(8,128)S(1)}, u32[]{:S(2)}) copy-start(f32[768,2,128]{0,2,1:T(8,128)S(1)} %get-tuple-element.79) | copy-start | bytes 2359300
  63.9 15.6 %collective-permute-start.3 = (bf16[294912]{0:T(1024)(128)(2,1)S(1)}, bf16[294912]{0:T(1024)(128)(2,1)S(1)}, u32[]{:S(2)}, u32[]{:S(2)}) collective-permute-start(bf16[294912]{0:T(1024)(128)(2,1)S(1)} %constant_dynamic-update-slice_fusion.3), channel_id=1, source_target_pairs={{16,0},{32,16},{48,32},{64,48},{80,64},{96,80},{112,96},{128,112},... | collective-permute-start | bytes 1769480 | tf_op jit(solution)/shard_map/ppermute | solution.py:21
  80.4 12.7 %collective-permute-start.4 = (bf16[196608]{0:T(1024)(128)(2,1)}, bf16[196608]{0:T(1024)(128)(2,1)S(1)}, u32[]{:S(2)}, u32[]{:S(2)}) collective-permute-start(bf16[196608]{0:T(1024)(128)(2,1)} %pad_maximum_fusion.2), channel_id=1, source_target_pairs={{32,0},{48,16},{64,32},{80,48},{96,64},{112,80},{128,96},{144,112}... | collective-permute-start | bytes 1179656 | tf_op jit(solution)/shard_map/ppermute | solution.py:21
  93.1 9.3 %collective-permute-start.5 = (bf16[98304]{0:T(1024)(128)(2,1)S(1)}, bf16[98304]{0:T(1024)(128)(2,1)S(1)}, u32[]{:S(2)}, u32[]{:S(2)}) collective-permute-start(bf16[98304]{0:T(1024)(128)(2,1)S(1)} %slice.473), channel_id=1, source_target_pairs={{32,0},{48,16},{64,32},{80,48},{96,64},{112,80},{128,96},{144,112}... | collective-permute-start | bytes 589832 | tf_op jit(solution)/shard_map/ppermute | solution.py:21
  96.0 6.8 %copy-start.5 = (bf16[128,256]{1,0:T(8,128)(2,1)S(1)}, bf16[128,256]{1,0:T(8,128)(2,1)}, u32[]{:S(2)}) copy-start(bf16[128,256]{1,0:T(8,128)(2,1)} %param.12) | copy-start | bytes 196612

commit v10 on v7

--- a/solution.py
+++ b/solution.py
@@ -53,28 +53,26 @@
     )
 
 
-def entry_weights(labels, decay_rate):
-    place = as_float(jnp.arange(labels.shape[0], dtype=jnp.int32))
-    return jnp.where(
-        (labels == labels[:1])[None, :], jnp.exp(-decay_rate[:, None] * place[None, :]), 0.0
-    )
-
-
-def exit_weights(labels, decay_rate):
-    count = labels.shape[0]
+def entry_weights(mask, decay_rate):
+    place = as_float(jnp.arange(mask.shape[0], dtype=jnp.int32))
+    return jnp.where(mask[None, :], jnp.exp(-decay_rate[:, None] * place[None, :]), 0.0)
+
+
+def exit_weights(mask, decay_rate):
+    count = mask.shape[0]
     place = as_float(jnp.arange(count, dtype=jnp.int32))
     return jnp.where(
-        (labels == labels[-1:])[None, :],
+        mask[None, :],
         jnp.exp(-decay_rate[:, None] * (count - 1 - place)[None, :]),
         0.0,
     )
 
 
-def forward_summary(keys, values, labels, link, decay_rate):
-    count = labels.shape[0]
+def forward_summary(keys, values, mask, decay_rate):
+    count = mask.shape[0]
     place = as_float(jnp.arange(count, dtype=jnp.int32))
     weight = jnp.where(
-        (labels == labels[-1:])[None, :] & link[None, :],
+        mask[None, :],
         jnp.exp(-decay_rate[:, None] * (count - place)[None, :]),
         0.0,
     )
@@ -86,11 +84,11 @@
     )
 
 
-def backward_summary(queries, grads, labels, link, decay_rate):
-    count = labels.shape[0]
+def backward_summary(queries, grads, mask, decay_rate):
+    count = mask.shape[0]
     place = as_float(jnp.arange(count, dtype=jnp.int32))
     weight = jnp.where(
-        (labels == labels[:1])[None, :] & link[None, :],
+        mask[None, :],
         jnp.exp(-decay_rate[:, None] * (place + 1.0)[None, :]),
         0.0,
     )
@@ -132,7 +130,9 @@
     window_blocks = lax.dynamic_slice_in_dim(
         padded, device * blocks_each, (2 * REACH + 1) * blocks_each
     )
-    window_labels = jnp.broadcast_to(window_blocks[:, None], (window_blocks.shape[0], BLK)).reshape(-1)
+    window_labels = lax.optimization_barrier(
+        jnp.broadcast_to(window_blocks[:, None], (window_blocks.shape[0], BLK)).reshape(-1)
+    )
     own_labels = window_labels[REACH * tokens : (REACH + 1) * tokens]
     key_labels = window_labels[tokens : (REACH + 1) * tokens]
 
@@ -149,9 +149,16 @@
     span = 2 * REACH + 1
     firsts = window_blocks[::blocks_each]
     lasts = window_blocks[blocks_each - 1 :: blocks_each]
-    summary = forward_summary(
-        keys, values, own_labels, lasts[REACH : REACH + 1] == firsts[REACH + 1 : REACH + 2], decay_rate
-    )
+    if blocks_each == 1:
+        same_first = same_last = jnp.ones((tokens,), bool)
+        same_next = own_labels == window_labels[(REACH + 1) * tokens : (REACH + 2) * tokens]
+        same_prev = own_labels == window_labels[(REACH - 1) * tokens : REACH * tokens]
+    else:
+        same_first = own_labels == own_labels[:1]
+        same_last = own_labels == own_labels[-1:]
+        same_next = same_last & (lasts[REACH : REACH + 1] == firsts[REACH + 1 : REACH + 2])
+        same_prev = same_first & (firsts[REACH : REACH + 1] == lasts[REACH - 1 : REACH])
+    summary = forward_summary(keys, values, same_next, decay_rate)
     full_decay = jnp.exp(-decay_rate * tokens)
     ahead = jnp.where((firsts[:-1] == firsts[1:])[:, None], full_decay[None, :], 0.0)
     behind = jnp.where(
@@ -182,8 +189,8 @@
     decay = decay_matrix(own_labels, decay_rate)
     scores = jnp.einsum("thd,shd->hts", queries, keys, preferred_element_type=jnp.float32)
     weights = (decay * scores).astype(jnp.bfloat16)
-    entry = entry_weights(own_labels, decay_rate)
-    leave = exit_weights(own_labels, decay_rate)
+    entry = entry_weights(same_first, decay_rate)
+    leave = exit_weights(same_last, decay_rate)
     inner = jnp.einsum("hts,shd->thd", weights, values, preferred_element_type=jnp.float32)
     carried = jnp.einsum("thd,hde->the", as_float(queries), state_in, precision=HIGH_PRECISION)
     lin_out = inner + carried * entry.T[:, :, None]
@@ -197,9 +204,7 @@
         jnp.bfloat16
     )
     grad_heads = split_heads(norm_grad)
-    back_summary = backward_summary(
-        queries, grad_heads, own_labels, firsts[REACH : REACH + 1] == lasts[REACH - 1 : REACH], decay_rate
-    )
+    back_summary = backward_summary(queries, grad_heads, same_prev, decay_rate)
     back_state = back_summary.astype(jnp.bfloat16)
     grad_scores_lin = jnp.einsum(
         "thd,shd->hts", grad_heads, values, preferred_element_type=jnp.float32

time: 107 us -> 104 us (0.972)
  between operations: 4.02 us -> 1.45 us
  transfers between devices with their start and end apart: 7 -> 7, of which waited for: 6 -> 6; matrix products, arithmetic and copies ran while one was open for 6% -> 5% of each run, Pallas kernels for 0% -> 0%
where the time goes in v10:
time: 104 us; the launch traced here: 102 us
  waiting for transfers between devices  37.1 us (36%)
  starting transfers between devices  30.1 us (29%)
  local copies, waits for them, and re-layouts  10.6 us (10%)
  blocking collectives  10.5 us (10%)
  matrix products  8.02 us (8%)
  other arithmetic  4.52 us (4%)
  between operations  1.45 us (1%)
    ppermute x7, waiting for transfers between devices, shifted(): lax.ppermute(value, axis, [(source, source + steps) for source in range(f...  37.1 us
    ppermute x7, starting transfers between devices, shifted(): lax.ppermute(value, axis, [(source, source + steps) for source in range(f...  30.1 us
    all_gather x2, blocking collectives, tp_sum(): value = jnp.sum(lax.all_gather(value, axis), axis=0)  10.5 us
    unnamed x57, local copies, waits for them, and re-layouts  7.32 us
  transfers between devices with their start and end apart: 7, of which 6 were waited for; matrix products, arithmetic and copies ran while one was open for 5% of the time, Pallas kernels for 0%

profile of v10, /device:TPU:1, one launch (start us, length us, event | category | flops | bytes accessed | tf_op | source)
XLA Modules:
  0.0 102.2 jit_solution(1199758398367106613)
XLA Ops:
  0.8 0.7 multiply_exponential_fusion.2
  1.5 0.7 pad_add_fusion
  2.4 0.9 copy.197
  3.3 0.9 copy.196
  4.2 1.0 copy.233
  5.2 0.2 convolution_convert_fusion
  5.5 4.4 %collective-permute-start = (bf16[98304]{0:T(1024)(128)(2,1)S(1)}, bf16[98304]{0:T(1024)(128)(2,1)S(1)}, u32[]{:S(2)}, u32[]{:S(2)}) collective-permute-start(bf16[98304]{0:T(1024)(128)(2,1)S(1)} %pad_maximum_fusion.2), channel_id=1, source_target_pairs={{0,32},{16,48},{32,64},{48,80},{64,96},{80,112},{96,128},{112,144}... | collective-permute-start | bytes 589832 | tf_op jit(solution)/shard_map/ppermute | solution.py:21
  11.1 0.3 fusion.28
  11.4 0.2 fusion.20
  11.7 0.8 collective-permute-done
  12.5 15.6 %collective-permute-start.1 = (bf16[196608]{0:T(1024)(128)(2,1)S(1)}, bf16[196608]{0:T(1024)(128)(2,1)S(1)}, u32[]{:S(2)}, u32[]{:S(2)}) collective-permute-start(bf16[196608]{0:T(1024)(128)(2,1)S(1)} %pad_maximum_fusion), channel_id=1, source_target_pairs={{0,16},{16,32},{32,48},{48,64},{64,80},{80,96},{96,112},{112,128},... | collective-permute-start | bytes 1179656 | tf_op jit(solution)/shard_map/ppermute | solution.py:21
  28.1 1.3 %collective-permute-start.2 = (bf16[98304]{0:T(1024)(128)(2,1)S(1)}, bf16[98304]{0:T(1024)(128)(2,1)S(1)}, u32[]{:S(2)}, u32[]{:S(2)}) collective-permute-start(bf16[98304]{0:T(1024)(128)(2,1)S(1)} %collective-permute-done), channel_id=1, source_target_pairs={{0,32},{16,48},{32,64},{48,80},{64,96},{80,112},{96,128},{112,144}... | collective-permute-start | bytes 589832 | tf_op jit(solution)/shard_map/ppermute | solution.py:21
  29.5 7.6 %collective-permute-done.2 = bf16[98304]{0:T(1024)(128)(2,1)S(1)} collective-permute-done((bf16[98304]{0:T(1024)(128)(2,1)S(1)}, bf16[98304]{0:T(1024)(128)(2,1)S(1)}, u32[]{:S(2)}, u32[]{:S(2)}) %collective-permute-start.2) | collective-permute-done | bytes 196640 | tf_op jit(solution)/shard_map/ppermute | solution.py:21
  37.0 2.7 %collective-permute-start.3 = (bf16[98304]{0:T(1024)(128)(2,1)S(1)}, bf16[98304]{0:T(1024)(128)(2,1)S(1)}, u32[]{:S(2)}, u32[]{:S(2)}) collective-permute-start(bf16[98304]{0:T(1024)(128)(2,1)S(1)} %collective-permute-done.2), channel_id=1, source_target_pairs={{0,16},{16,32},{32,48},{48,64},{64,80},{80,96},{96,112},{112,128},... | collective-permute-start | bytes 589832 | tf_op jit(solution)/shard_map/ppermute | solution.py:21
  39.8 2.6 %collective-permute-done.3 = bf16[98304]{0:T(1024)(128)(2,1)S(1)} collective-permute-done((bf16[98304]{0:T(1024)(128)(2,1)S(1)}, bf16[98304]{0:T(1024)(128)(2,1)S(1)}, u32[]{:S(2)}, u32[]{:S(2)}) %collective-permute-start.3) | collective-permute-done | bytes 196640 | tf_op jit(solution)/shard_map/ppermute | solution.py:21
  42.6 0.3 fusion.15
  42.9 0.2 multiply_reduce_fusion.1
  43.4 5.2 %all-gather.2 = f32[4,2,128]{2,1,0:T(2,128)S(1)} all-gather(f32[1,2,128]{2,1,0:T(2,128)S(1)} %maximum_bitcast_fusion), channel_id=2, replica_groups=mesh['seq'=64,'tp_outer'=4,'tp_inner'=4] {'tp_inner'}, dimensions={0}, use_global_device_ids=true | all-gather | bytes 5120 | tf_op jit(solution)/shard_map/all_gather | solution.py:26
  48.6 5.2 %all-gather.3 = f32[4,2,128]{2,1,0:T(2,128)S(1)} all-gather(f32[1,2,128]{2,1,0:T(2,128)S(1)} %bitcast.285), channel_id=3, replica_groups=mesh['seq'=64,'tp_outer'=4,'tp_inner'=4] {'tp_outer'}, dimensions={0}, use_global_device_ids=true | all-gather | bytes 5120 | tf_op jit(solution)/shard_map/all_gather | solution.py:26
  54.4 1.3 %fusion.71 = (f32[2,128]{1,0:T(2,128)S(1)}, f32[2,128,768]{1,2,0:T(8,128)}) fusion(bf16[768,2,128]{2,0,1:T(8,128)(2,1)S(1)} %constant_dynamic-update-slice_fusion, bf16[128,2,128]{0,2,1:T(8,128)(2,1)S(1)} %bitcast.246, pred[128,768]{0,1:T(8,128)(4,1)S(1)} %fusion.28), kind=kOutput, calls=%fused_computation.162 | convolution fusion | flops 51118848 | bytes 1344512 | tf_op jit(solution)/shard_map/sub | solution.py:246
  55.7 0.6 fusion.73
  56.3 0.4 copy-done.12
  56.7 0.7 fusion.24
  58.1 1.4 %fusion.8 = bf16[2,128,768]{1,2,0:T(8,128)(2,1)S(1)} fusion(bf16[768,2,128]{2,0,1:T(8,128)(2,1)S(1)} %copy-done.12, bf16[128,2,128]{0,2,1:T(8,128)(2,1)S(1)} %bitcast.284, f32[2,128]{1,0:T(2,128)S(1)} %bitcast.288, f32[2,128,768]{1,2,0:T(8,128)} %get-tuple-element.74, f32[2,128]{1,0:T(2,128)S(1)} %get-tuple-element.73), kind=kOutput, calls=%fused_computation.12 | convolution fusion | flops 51118080 | bytes 1640448 | tf_op jit(solution)/shard_map/thd,uhd->htu/dot_general | solution.py:104
  59.5 0.3 fusion.72
  60.0 0.3 broadcast_multiply_fusion.1
  60.4 3.5 %collective-permute-start.4 = (bf16[294912]{0:T(1024)(128)(2,1)S(1)}, bf16[294912]{0:T(1024)(128)(2,1)S(1)}, u32[]{:S(2)}, u32[]{:S(2)}) collective-permute-start(bf16[294912]{0:T(1024)(128)(2,1)S(1)} %constant_dynamic-update-slice_fusion.3), channel_id=1, source_target_pairs={{16,0},{32,16},{48,32},{64,48},{80,64},{96,80},{112,96},{128,112},... | collective-permute-start | bytes 1769480 | tf_op jit(solution)/shard_map/ppermute | solution.py:21
  64.2 0.2 fusion.21
  64.4 0.2 fusion.13
  64.6 11.2 %collective-permute-done.4 = bf16[294912]{0:T(1024)(128)(2,1)S(1)} collective-permute-done((bf16[294912]{0:T(1024)(128)(2,1)S(1)}, bf16[294912]{0:T(1024)(128)(2,1)S(1)}, u32[]{:S(2)}, u32[]{:S(2)}) %collective-permute-start.4) | collective-permute-done | bytes 589856 | tf_op jit(solution)/shard_map/ppermute | solution.py:21
  76.0 0.8 pad_maximum_fusion.1
  76.8 1.3 %collective-permute-start.5 = (bf16[196608]{0:T(1024)(128)(2,1)}, bf16[196608]{0:T(1024)(128)(2,1)S(1)}, u32[]{:S(2)}, u32[]{:S(2)}) collective-permute-start(bf16[196608]{0:T(1024)(128)(2,1)} %pad_maximum_fusion.1), channel_id=1, source_target_pairs={{32,0},{48,16},{64,32},{80,48},{96,64},{112,80},{128,96},{144,112}... | collective-permute-start | bytes 1179656 | tf_op jit(solution)/shard_map/ppermute | solution.py:21
  78.1 0.2 fusion.22
  78.2 0.7 copy.175
  79.0 0.3 fusion.19
  79.3 0.7 copy.178
  80.1 8.3 %collective-permute-done.5 = bf16[196608]{0:T(1024)(128)(2,1)S(1)} collective-permute-done((bf16[196608]{0:T(1024)(128)(2,1)}, bf16[196608]{0:T(1024)(128)(2,1)S(1)}, u32[]{:S(2)}, u32[]{:S(2)}) %collective-permute-start.5) | collective-permute-done | bytes 393248 | tf_op jit(solution)/shard_map/ppermute | solution.py:21
  88.4 1.3 %collective-permute-start.6 = (bf16[98304]{0:T(1024)(128)(2,1)S(1)}, bf16[98304]{0:T(1024)(128)(2,1)S(1)}, u32[]{:S(2)}, u32[]{:S(2)}) collective-permute-start(bf16[98304]{0:T(1024)(128)(2,1)S(1)} %slice.451), channel_id=1, source_target_pairs={{32,0},{48,16},{64,32},{80,48},{96,64},{112,80},{128,96},{144,112}... | collective-permute-start | bytes 589832 | tf_op jit(solution)/shard_map/ppermute | solution.py:21
  89.7 1.0 convolution_bitcast_fusion.4
  90.7 6.5 %collective-permute-done.6 = bf16[98304]{0:T(1024)(128)(2,1)S(1)} collective-permute-done((bf16[98304]{0:T(1024)(128)(2,1)S(1)}, bf16[98304]{0:T(1024)(128)(2,1)S(1)}, u32[]{:S(2)}, u32[]{:S(2)}) %collective-permute-start.6) | collective-permute-done | bytes 196640 | tf_op jit(solution)/shard_map/ppermute | solution.py:21
  97.4 0.2 fusion.12
  97.6 0.3 fusion.18
  97.9 0.7 copy.177
  98.8 0.9 fusion.30
  99.7 0.7 copy.180
  100.6 0.7 copy.179
  101.3 0.2 fusion.23
  101.5 0.7 copy.176
  (114 shorter events, 4.1 us)
Async XLA Ops:
  0.6 4.6 %copy-start = (bf16[128,256]{1,0:T(8,128)(2,1)S(1)}, bf16[128,256]{1,0:T(8,128)(2,1)}, u32[]{:S(2)}) copy-start(bf16[128,256]{1,0:T(8,128)(2,1)} %param.13) | copy-start | bytes 196612
  0.6 9.6 %copy-start.2 = (bf16[128,256]{1,0:T(8,128)(2,1)S(1)}, bf16[128,256]{1,0:T(8,128)(2,1)}, u32[]{:S(2)}) copy-start(bf16[128,256]{1,0:T(8,128)(2,1)} %param.19) | copy-start | bytes 196612
  0.7 9.5 %copy-start.1 = (bf16[128,256]{1,0:T(8,128)(2,1)S(1)}, bf16[128,256]{1,0:T(8,128)(2,1)}, u32[]{:S(2)}) copy-start(bf16[128,256]{1,0:T(8,128)(2,1)} %param.18) | copy-start | bytes 196612
  0.7 10.7 %copy-start.4 = (bf16[128,256]{1,0:T(8,128)(2,1)S(1)}, bf16[128,256]{1,0:T(8,128)(2,1)}, u32[]{:S(2)}) copy-start(bf16[128,256]{1,0:T(8,128)(2,1)} %param.12) | copy-start | bytes 196612
  0.7 9.8 %copy-start.8 = (bf16[128,256]{1,0:T(8,128)(2,1)S(1)}, bf16[128,256]{1,0:T(8,128)(2,1)}, u32[]{:S(2)}) copy-start(bf16[128,256]{1,0:T(8,128)(2,1)} %param.11) | copy-start | bytes 196612
  0.7 9.9 %copy-start.9 = (bf16[128,256]{1,0:T(8,128)(2,1)S(1)}, bf16[128,256]{1,0:T(8,128)(2,1)}, u32[]{:S(2)}) copy-start(bf16[128,256]{1,0:T(8,128)(2,1)} %param.17) | copy-start | bytes 196612
  0.7 10.0 %copy-start.10 = (bf16[128,256]{1,0:T(8,128)(2,1)S(1)}, bf16[128,256]{1,0:T(8,128)(2,1)}, u32[]{:S(2)}) copy-start(bf16[128,256]{1,0:T(8,128)(2,1)} %param.20) | copy-start | bytes 196612
  5.5 7.0 %collective-permute-start = (bf16[98304]{0:T(1024)(128)(2,1)S(1)}, bf16[98304]{0:T(1024)(128)(2,1)S(1)}, u32[]{:S(2)}, u32[]{:S(2)}) collective-permute-start(bf16[98304]{0:T(1024)(128)(2,1)S(1)} %pad_maximum_fusion.2), channel_id=1, source_target_pairs={{0,32},{16,48},{32,64},{48,80},{64,96},{80,112},{96,128},{112,144}... | collective-permute-start | bytes 589832 | tf_op jit(solution)/shard_map/ppermute | solution.py:21
  11.6 44.1 %copy-start.6 = (bf16[2,128,128]{2,1,0:T(8,128)(2,1)}, bf16[2,128,128]{2,1,0:T(8,128)(2,1)S(1)}, u32[]{:S(2)}) copy-start(bf16[2,128,128]{2,1,0:T(8,128)(2,1)S(1)} %fusion.20) | copy-start | bytes 196612
  12.5 29.9 %collective-permute-start.1 = (bf16[196608]{0:T(1024)(128)(2,1)S(1)}, bf16[196608]{0:T(1024)(128)(2,1)S(1)}, u32[]{:S(2)}, u32[]{:S(2)}) collective-permute-start(bf16[196608]{0:T(1024)(128)(2,1)S(1)} %pad_maximum_fusion), channel_id=1, source_target_pairs={{0,16},{16,32},{32,48},{48,64},{64,80},{80,96},{96,112},{112,128},... | collective-permute-start | bytes 1179656 | tf_op jit(solution)/shard_map/ppermute | solution.py:21
  28.1 8.9 %collective-permute-start.2 = (bf16[98304]{0:T(1024)(128)(2,1)S(1)}, bf16[98304]{0:T(1024)(128)(2,1)S(1)}, u32[]{:S(2)}, u32[]{:S(2)}) collective-permute-start(bf16[98304]{0:T(1024)(128)(2,1)S(1)} %collective-permute-done), channel_id=1, source_target_pairs={{0,32},{16,48},{32,64},{48,80},{64,96},{80,112},{96,128},{112,144}... | collective-permute-start | bytes 589832 | tf_op jit(solution)/shard_map/ppermute | solution.py:21
  37.0 5.3 %collective-permute-start.3 = (bf16[98304]{0:T(1024)(128)(2,1)S(1)}, bf16[98304]{0:T(1024)(128)(2,1)S(1)}, u32[]{:S(2)}, u32[]{:S(2)}) collective-permute-start(bf16[98304]{0:T(1024)(128)(2,1)S(1)} %collective-permute-done.2), channel_id=1, source_target_pairs={{0,16},{16,32},{32,48},{48,64},{64,80},{80,96},{96,112},{112,128},... | collective-permute-start | bytes 589832 | tf_op jit(solution)/shard_map/ppermute | solution.py:21
  42.4 0.9 copy-start.3
  42.4 0.9 copy-start.13
  54.4 1.3 %copy-start.11 = (bf16[768,2,128]{2,0,1:T(8,128)(2,1)}, bf16[768,2,128]{2,0,1:T(8,128)(2,1)S(1)}, u32[]{:S(2)}) copy-start(bf16[768,2,128]{2,0,1:T(8,128)(2,1)S(1)} %constant_dynamic-update-slice_fusion.1) | copy-start | bytes 1179652
  55.7 1.0 copy-start.12
  56.7 1.1 %copy-start.7 = (f32[768,2,128]{0,2,1:T(8,128)}, f32[768,2,128]{0,2,1:T(8,128)S(1)}, u32[]{:S(2)}) copy-start(f32[768,2,128]{0,2,1:T(8,128)S(1)} %get-tuple-element.78) | copy-start | bytes 2359300
  60.4 15.4 %collective-permute-start.4 = (bf16[294912]{0:T(1024)(128)(2,1)S(1)}, bf16[294912]{0:T(1024)(128)(2,1)S(1)}, u32[]{:S(2)}, u32[]{:S(2)}) collective-permute-start(bf16[294912]{0:T(1024)(128)(2,1)S(1)} %constant_dynamic-update-slice_fusion.3), channel_id=1, source_target_pairs={{16,0},{32,16},{48,32},{64,48},{80,64},{96,80},{112,96},{128,112},... | collective-permute-start | bytes 1769480 | tf_op jit(solution)/shard_map/ppermute | solution.py:21
  76.8 11.6 %collective-permute-start.5 = (bf16[196608]{0:T(1024)(128)(2,1)}, bf16[196608]{0:T(1024)(128)(2,1)S(1)}, u32[]{:S(2)}, u32[]{:S(2)}) collective-permute-start(bf16[196608]{0:T(1024)(128)(2,1)} %pad_maximum_fusion.1), channel_id=1, source_target_pairs={{32,0},{48,16},{64,32},{80,48},{96,64},{112,80},{128,96},{144,112}... | collective-permute-start | bytes 1179656 | tf_op jit(solution)/shard_map/ppermute | solution.py:21
  88.4 8.8 %collective-permute-start.6 = (bf16[98304]{0:T(1024)(128)(2,1)S(1)}, bf16[98304]{0:T(1024)(128)(2,1)S(1)}, u32[]{:S(2)}, u32[]{:S(2)}) collective-permute-start(bf16[98304]{0:T(1024)(128)(2,1)S(1)} %slice.451), channel_id=1, source_target_pairs={{32,0},{48,16},{64,32},{80,48},{96,64},{112,80},{128,96},{144,112}... | collective-permute-start | bytes 589832 | tf_op jit(solution)/shard_map/ppermute | solution.py:21
  90.7 6.9 %copy-start.5 = (bf16[128,256]{1,0:T(8,128)(2,1)S(1)}, bf16[128,256]{1,0:T(8,128)(2,1)}, u32[]{:S(2)}) copy-start(bf16[128,256]{1,0:T(8,128)(2,1)} %param.12) | copy-start | bytes 196612

commit v11 on v10

--- a/solution.py
+++ b/solution.py
@@ -171,7 +171,7 @@
     two_back = shifted(unit, "seq", 2)
     four_back = shifted(two_back, "seq", 2)
     odd_back = shifted(jnp.concatenate([unit, two_back]), "seq", 1)
-    five_back = shifted(four_back, "seq", 1)
+    five_back = shifted(two_back, "seq", 3)
     arrived = {
         1: odd_back[:size],
         2: two_back,

time: 104 us -> 102 us (0.981)
  the two profiles are of different devices: /device:TPU:1 before, /device:TPU:481 now
where the time goes in v11:
time: 102 us
  waiting for transfers between devices  36.7 us (36%)
  starting transfers between devices  24.7 us (24%)
  blocking collectives  15.7 us (15%)
  local copies, waits for them, and re-layouts  10.6 us (10%)
  matrix products  8.02 us (8%)
  other arithmetic  4.53 us (4%)
  between operations  1.44 us (1%)
    ppermute x7, waiting for transfers between devices, shifted(): lax.ppermute(value, axis, [(source, source + steps) for source in range(f...  36.7 us
    ppermute x7, starting transfers between devices, shifted(): lax.ppermute(value, axis, [(source, source + steps) for source in range(f...  24.7 us
    all_gather x2, blocking collectives, tp_sum(): value = jnp.sum(lax.all_gather(value, axis), axis=0)  15.7 us
    unnamed x57, local copies, waits for them, and re-layouts  7.31 us
  transfers between devices with their start and end apart: 7, of which 6 were waited for; matrix products, arithmetic and copies ran while one was open for 5% of the time, Pallas kernels for 0%

profile of v11, /device:TPU:481, one launch (start us, length us, event | category | flops | bytes accessed | tf_op | source)
XLA Modules:
  0.0 101.6 jit_solution(3517715684867913422)
XLA Ops:
  0.8 0.7 multiply_exponential_fusion.2
  1.5 0.7 pad_add_fusion
  2.4 0.9 copy.197
  3.3 0.9 copy.196
  4.2 1.0 copy.233
  5.2 0.2 convolution_convert_fusion
  5.5 4.8 %collective-permute-start = (bf16[98304]{0:T(1024)(128)(2,1)S(1)}, bf16[98304]{0:T(1024)(128)(2,1)S(1)}, u32[]{:S(2)}, u32[]{:S(2)}) collective-permute-start(bf16[98304]{0:T(1024)(128)(2,1)S(1)} %pad_maximum_fusion.2), channel_id=1, source_target_pairs={{0,32},{16,48},{32,64},{48,80},{64,96},{80,112},{96,128},{112,144}... | collective-permute-start | bytes 589832 | tf_op jit(solution)/shard_map/ppermute | solution.py:21
  11.5 0.3 fusion.28
  11.8 0.2 fusion.20
  12.0 1.7 %collective-permute-done = bf16[98304]{0:T(1024)(128)(2,1)S(1)} collective-permute-done((bf16[98304]{0:T(1024)(128)(2,1)S(1)}, bf16[98304]{0:T(1024)(128)(2,1)S(1)}, u32[]{:S(2)}, u32[]{:S(2)}) %collective-permute-start) | collective-permute-done | bytes 196640 | tf_op jit(solution)/shard_map/ppermute | solution.py:21
  13.8 6.8 %collective-permute-start.1 = (bf16[196608]{0:T(1024)(128)(2,1)S(1)}, bf16[196608]{0:T(1024)(128)(2,1)S(1)}, u32[]{:S(2)}, u32[]{:S(2)}) collective-permute-start(bf16[196608]{0:T(1024)(128)(2,1)S(1)} %pad_maximum_fusion), channel_id=1, source_target_pairs={{0,16},{16,32},{32,48},{48,64},{64,80},{80,96},{96,112},{112,128},... | collective-permute-start | bytes 1179656 | tf_op jit(solution)/shard_map/ppermute | solution.py:21
  20.6 1.9 %collective-permute-start.3 = (bf16[98304]{0:T(1024)(128)(2,1)S(1)}, bf16[98304]{0:T(1024)(128)(2,1)S(1)}, u32[]{:S(2)}, u32[]{:S(2)}) collective-permute-start(bf16[98304]{0:T(1024)(128)(2,1)S(1)} %collective-permute-done), channel_id=1, source_target_pairs={{0,48},{16,64},{32,80},{48,96},{64,112},{80,128},{96,144},{112,160... | collective-permute-start | bytes 589832 | tf_op jit(solution)/shard_map/ppermute | solution.py:21
  22.5 1.9 %collective-permute-start.2 = (bf16[98304]{0:T(1024)(128)(2,1)S(1)}, bf16[98304]{0:T(1024)(128)(2,1)S(1)}, u32[]{:S(2)}, u32[]{:S(2)}) collective-permute-start(bf16[98304]{0:T(1024)(128)(2,1)S(1)} %collective-permute-done), channel_id=1, source_target_pairs={{0,32},{16,48},{32,64},{48,80},{64,96},{80,112},{96,128},{112,144}... | collective-permute-start | bytes 589832 | tf_op jit(solution)/shard_map/ppermute | solution.py:21
  24.5 9.3 %collective-permute-done.3 = bf16[98304]{0:T(1024)(128)(2,1)S(1)} collective-permute-done((bf16[98304]{0:T(1024)(128)(2,1)S(1)}, bf16[98304]{0:T(1024)(128)(2,1)S(1)}, u32[]{:S(2)}, u32[]{:S(2)}) %collective-permute-start.3) | collective-permute-done | bytes 196640 | tf_op jit(solution)/shard_map/ppermute | solution.py:21
  33.8 2.0 %collective-permute-done.2 = bf16[98304]{0:T(1024)(128)(2,1)S(1)} collective-permute-done((bf16[98304]{0:T(1024)(128)(2,1)S(1)}, bf16[98304]{0:T(1024)(128)(2,1)S(1)}, u32[]{:S(2)}, u32[]{:S(2)}) %collective-permute-start.2) | collective-permute-done | bytes 196640 | tf_op jit(solution)/shard_map/ppermute | solution.py:21
  36.1 0.3 fusion.15
  36.4 0.2 multiply_reduce_fusion.1
  36.9 8.0 %all-gather.2 = f32[4,2,128]{2,1,0:T(2,128)S(1)} all-gather(f32[1,2,128]{2,1,0:T(2,128)S(1)} %maximum_bitcast_fusion), channel_id=2, replica_groups=mesh['seq'=64,'tp_outer'=4,'tp_inner'=4] {'tp_inner'}, dimensions={0}, use_global_device_ids=true | all-gather | bytes 5120 | tf_op jit(solution)/shard_map/all_gather | solution.py:26
  44.9 7.7 %all-gather.3 = f32[4,2,128]{2,1,0:T(2,128)S(1)} all-gather(f32[1,2,128]{2,1,0:T(2,128)S(1)} %bitcast.285), channel_id=3, replica_groups=mesh['seq'=64,'tp_outer'=4,'tp_inner'=4] {'tp_outer'}, dimensions={0}, use_global_device_ids=true | all-gather | bytes 5120 | tf_op jit(solution)/shard_map/all_gather | solution.py:26
  53.0 1.3 %fusion.71 = (f32[2,128]{1,0:T(2,128)S(1)}, f32[2,128,768]{1,2,0:T(8,128)}) fusion(bf16[768,2,128]{2,0,1:T(8,128)(2,1)S(1)} %constant_dynamic-update-slice_fusion, bf16[128,2,128]{0,2,1:T(8,128)(2,1)S(1)} %bitcast.246, pred[128,768]{0,1:T(8,128)(4,1)S(1)} %fusion.28), kind=kOutput, calls=%fused_computation.162 | convolution fusion | flops 51118848 | bytes 1344512 | tf_op jit(solution)/shard_map/sub | solution.py:246
  54.3 0.6 fusion.73
  54.9 0.4 copy-done.12
  55.3 0.7 fusion.24
  56.7 1.4 %fusion.8 = bf16[2,128,768]{1,2,0:T(8,128)(2,1)S(1)} fusion(bf16[768,2,128]{2,0,1:T(8,128)(2,1)S(1)} %copy-done.12, bf16[128,2,128]{0,2,1:T(8,128)(2,1)S(1)} %bitcast.284, f32[2,128]{1,0:T(2,128)S(1)} %bitcast.288, f32[2,128,768]{1,2,0:T(8,128)} %get-tuple-element.74, f32[2,128]{1,0:T(2,128)S(1)} %get-tuple-element.73), kind=kOutput, calls=%fused_computation.12 | convolution fusion | flops 51118080 | bytes 1640448 | tf_op jit(solution)/shard_map/thd,uhd->htu/dot_general | solution.py:104
  58.1 0.3 fusion.72
  58.6 0.3 broadcast_multiply_fusion.1
  59.0 5.5 %collective-permute-start.4 = (bf16[294912]{0:T(1024)(128)(2,1)S(1)}, bf16[294912]{0:T(1024)(128)(2,1)S(1)}, u32[]{:S(2)}, u32[]{:S(2)}) collective-permute-start(bf16[294912]{0:T(1024)(128)(2,1)S(1)} %constant_dynamic-update-slice_fusion.3), channel_id=1, source_target_pairs={{16,0},{32,16},{48,32},{64,48},{80,64},{96,80},{112,96},{128,112},... | collective-permute-start | bytes 1769480 | tf_op jit(solution)/shard_map/ppermute | solution.py:21
  64.8 0.2 fusion.21
  65.0 0.2 fusion.13
  65.2 8.8 %collective-permute-done.4 = bf16[294912]{0:T(1024)(128)(2,1)S(1)} collective-permute-done((bf16[294912]{0:T(1024)(128)(2,1)S(1)}, bf16[294912]{0:T(1024)(128)(2,1)S(1)}, u32[]{:S(2)}, u32[]{:S(2)}) %collective-permute-start.4) | collective-permute-done | bytes 589856 | tf_op jit(solution)/shard_map/ppermute | solution.py:21
  74.3 0.8 pad_maximum_fusion.1
  75.0 1.9 %collective-permute-start.5 = (bf16[196608]{0:T(1024)(128)(2,1)}, bf16[196608]{0:T(1024)(128)(2,1)S(1)}, u32[]{:S(2)}, u32[]{:S(2)}) collective-permute-start(bf16[196608]{0:T(1024)(128)(2,1)} %pad_maximum_fusion.1), channel_id=1, source_target_pairs={{32,0},{48,16},{64,32},{80,48},{96,64},{112,80},{128,96},{144,112}... | collective-permute-start | bytes 1179656 | tf_op jit(solution)/shard_map/ppermute | solution.py:21
  76.9 0.2 fusion.22
  77.1 0.7 copy.175
  77.8 0.3 fusion.19
  78.2 0.7 copy.178
  78.9 8.6 %collective-permute-done.5 = bf16[196608]{0:T(1024)(128)(2,1)S(1)} collective-permute-done((bf16[196608]{0:T(1024)(128)(2,1)}, bf16[196608]{0:T(1024)(128)(2,1)S(1)}, u32[]{:S(2)}, u32[]{:S(2)}) %collective-permute-start.5) | collective-permute-done | bytes 393248 | tf_op jit(solution)/shard_map/ppermute | solution.py:21
  87.5 1.9 %collective-permute-start.6 = (bf16[98304]{0:T(1024)(128)(2,1)S(1)}, bf16[98304]{0:T(1024)(128)(2,1)S(1)}, u32[]{:S(2)}, u32[]{:S(2)}) collective-permute-start(bf16[98304]{0:T(1024)(128)(2,1)S(1)} %slice.451), channel_id=1, source_target_pairs={{32,0},{48,16},{64,32},{80,48},{96,64},{112,80},{128,96},{144,112}... | collective-permute-start | bytes 589832 | tf_op jit(solution)/shard_map/ppermute | solution.py:21
  89.4 1.0 convolution_bitcast_fusion.4
  90.4 6.2 %collective-permute-done.6 = bf16[98304]{0:T(1024)(128)(2,1)S(1)} collective-permute-done((bf16[98304]{0:T(1024)(128)(2,1)S(1)}, bf16[98304]{0:T(1024)(128)(2,1)S(1)}, u32[]{:S(2)}, u32[]{:S(2)}) %collective-permute-start.6) | collective-permute-done | bytes 196640 | tf_op jit(solution)/shard_map/ppermute | solution.py:21
  96.7 0.3 fusion.12
  97.0 0.3 fusion.18
  97.3 0.7 copy.177
  98.1 0.9 fusion.30
  99.1 0.7 copy.180
  99.9 0.7 copy.179
  100.7 0.2 fusion.23
  100.8 0.7 copy.176
  (114 shorter events, 4.1 us)
Async XLA Ops:
  0.6 4.6 %copy-start = (bf16[128,256]{1,0:T(8,128)(2,1)S(1)}, bf16[128,256]{1,0:T(8,128)(2,1)}, u32[]{:S(2)}) copy-start(bf16[128,256]{1,0:T(8,128)(2,1)} %param.13) | copy-start | bytes 196612
  0.6 10.0 %copy-start.2 = (bf16[128,256]{1,0:T(8,128)(2,1)S(1)}, bf16[128,256]{1,0:T(8,128)(2,1)}, u32[]{:S(2)}) copy-start(bf16[128,256]{1,0:T(8,128)(2,1)} %param.19) | copy-start | bytes 196612
  0.7 9.8 %copy-start.1 = (bf16[128,256]{1,0:T(8,128)(2,1)S(1)}, bf16[128,256]{1,0:T(8,128)(2,1)}, u32[]{:S(2)}) copy-start(bf16[128,256]{1,0:T(8,128)(2,1)} %param.18) | copy-start | bytes 196612
  0.7 11.1 %copy-start.4 = (bf16[128,256]{1,0:T(8,128)(2,1)S(1)}, bf16[128,256]{1,0:T(8,128)(2,1)}, u32[]{:S(2)}) copy-start(bf16[128,256]{1,0:T(8,128)(2,1)} %param.12) | copy-start | bytes 196612
  0.7 10.2 %copy-start.8 = (bf16[128,256]{1,0:T(8,128)(2,1)S(1)}, bf16[128,256]{1,0:T(8,128)(2,1)}, u32[]{:S(2)}) copy-start(bf16[128,256]{1,0:T(8,128)(2,1)} %param.11) | copy-start | bytes 196612
  0.7 10.3 %copy-start.9 = (bf16[128,256]{1,0:T(8,128)(2,1)S(1)}, bf16[128,256]{1,0:T(8,128)(2,1)}, u32[]{:S(2)}) copy-start(bf16[128,256]{1,0:T(8,128)(2,1)} %param.17) | copy-start | bytes 196612
  0.7 10.4 %copy-start.10 = (bf16[128,256]{1,0:T(8,128)(2,1)S(1)}, bf16[128,256]{1,0:T(8,128)(2,1)}, u32[]{:S(2)}) copy-start(bf16[128,256]{1,0:T(8,128)(2,1)} %param.20) | copy-start | bytes 196612
  5.5 8.3 %collective-permute-start = (bf16[98304]{0:T(1024)(128)(2,1)S(1)}, bf16[98304]{0:T(1024)(128)(2,1)S(1)}, u32[]{:S(2)}, u32[]{:S(2)}) collective-permute-start(bf16[98304]{0:T(1024)(128)(2,1)S(1)} %pad_maximum_fusion.2), channel_id=1, source_target_pairs={{0,32},{16,48},{32,64},{48,80},{64,96},{80,112},{96,128},{112,144}... | collective-permute-start | bytes 589832 | tf_op jit(solution)/shard_map/ppermute | solution.py:21
  12.0 42.3 %copy-start.6 = (bf16[2,128,128]{2,1,0:T(8,128)(2,1)}, bf16[2,128,128]{2,1,0:T(8,128)(2,1)S(1)}, u32[]{:S(2)}) copy-start(bf16[2,128,128]{2,1,0:T(8,128)(2,1)S(1)} %fusion.20) | copy-start | bytes 196612
  13.8 22.1 %collective-permute-start.1 = (bf16[196608]{0:T(1024)(128)(2,1)S(1)}, bf16[196608]{0:T(1024)(128)(2,1)S(1)}, u32[]{:S(2)}, u32[]{:S(2)}) collective-permute-start(bf16[196608]{0:T(1024)(128)(2,1)S(1)} %pad_maximum_fusion), channel_id=1, source_target_pairs={{0,16},{16,32},{32,48},{48,64},{64,80},{80,96},{96,112},{112,128},... | collective-permute-start | bytes 1179656 | tf_op jit(solution)/shard_map/ppermute | solution.py:21
  20.6 13.1 %collective-permute-start.3 = (bf16[98304]{0:T(1024)(128)(2,1)S(1)}, bf16[98304]{0:T(1024)(128)(2,1)S(1)}, u32[]{:S(2)}, u32[]{:S(2)}) collective-permute-start(bf16[98304]{0:T(1024)(128)(2,1)S(1)} %collective-permute-done), channel_id=1, source_target_pairs={{0,48},{16,64},{32,80},{48,96},{64,112},{80,128},{96,144},{112,160... | collective-permute-start | bytes 589832 | tf_op jit(solution)/shard_map/ppermute | solution.py:21
  22.5 13.3 %collective-permute-start.2 = (bf16[98304]{0:T(1024)(128)(2,1)S(1)}, bf16[98304]{0:T(1024)(128)(2,1)S(1)}, u32[]{:S(2)}, u32[]{:S(2)}) collective-permute-start(bf16[98304]{0:T(1024)(128)(2,1)S(1)} %collective-permute-done), channel_id=1, source_target_pairs={{0,32},{16,48},{32,64},{48,80},{64,96},{80,112},{96,128},{112,144}... | collective-permute-start | bytes 589832 | tf_op jit(solution)/shard_map/ppermute | solution.py:21
  35.8 0.9 copy-start.3
  35.9 0.9 copy-start.13
  53.0 1.3 %copy-start.11 = (bf16[768,2,128]{2,0,1:T(8,128)(2,1)}, bf16[768,2,128]{2,0,1:T(8,128)(2,1)S(1)}, u32[]{:S(2)}) copy-start(bf16[768,2,128]{2,0,1:T(8,128)(2,1)S(1)} %constant_dynamic-update-slice_fusion.1) | copy-start | bytes 1179652
  54.3 1.0 copy-start.12
  55.3 1.1 %copy-start.7 = (f32[768,2,128]{0,2,1:T(8,128)}, f32[768,2,128]{0,2,1:T(8,128)S(1)}, u32[]{:S(2)}) copy-start(f32[768,2,128]{0,2,1:T(8,128)S(1)} %get-tuple-element.78) | copy-start | bytes 2359300
  59.0 15.1 %collective-permute-start.4 = (bf16[294912]{0:T(1024)(128)(2,1)S(1)}, bf16[294912]{0:T(1024)(128)(2,1)S(1)}, u32[]{:S(2)}, u32[]{:S(2)}) collective-permute-start(bf16[294912]{0:T(1024)(128)(2,1)S(1)} %constant_dynamic-update-slice_fusion.3), channel_id=1, source_target_pairs={{16,0},{32,16},{48,32},{64,48},{80,64},{96,80},{112,96},{128,112},... | collective-permute-start | bytes 1769480 | tf_op jit(solution)/shard_map/ppermute | solution.py:21
  75.0 12.5 %collective-permute-start.5 = (bf16[196608]{0:T(1024)(128)(2,1)}, bf16[196608]{0:T(1024)(128)(2,1)S(1)}, u32[]{:S(2)}, u32[]{:S(2)}) collective-permute-start(bf16[196608]{0:T(1024)(128)(2,1)} %pad_maximum_fusion.1), channel_id=1, source_target_pairs={{32,0},{48,16},{64,32},{80,48},{96,64},{112,80},{128,96},{144,112}... | collective-permute-start | bytes 1179656 | tf_op jit(solution)/shard_map/ppermute | solution.py:21
  87.5 9.1 %collective-permute-start.6 = (bf16[98304]{0:T(1024)(128)(2,1)S(1)}, bf16[98304]{0:T(1024)(128)(2,1)S(1)}, u32[]{:S(2)}, u32[]{:S(2)}) collective-permute-start(bf16[98304]{0:T(1024)(128)(2,1)S(1)} %slice.451), channel_id=1, source_target_pairs={{32,0},{48,16},{64,32},{80,48},{96,64},{112,80},{128,96},{144,112}... | collective-permute-start | bytes 589832 | tf_op jit(solution)/shard_map/ppermute | solution.py:21
  90.4 6.6 %copy-start.5 = (bf16[128,256]{1,0:T(8,128)(2,1)S(1)}, bf16[128,256]{1,0:T(8,128)(2,1)}, u32[]{:S(2)}) copy-start(bf16[128,256]{1,0:T(8,128)(2,1)} %param.12) | copy-start | bytes 196612

commit v12 on v11

--- a/solution.py
+++ b/solution.py
@@ -279,16 +279,13 @@
     def wire(value):
         return value.astype(jnp.bfloat16)
 
-    first = as_float(shifted(wire(jnp.concatenate([items[5], items[3], items[1]])), "seq", -1))
-    second = as_float(
-        shifted(
-            wire(jnp.concatenate([items[2] + first[size : 2 * size], items[4] + first[:size]])),
-            "seq",
-            -2,
-        )
-    )
-    third = as_float(shifted(wire(second[size:]), "seq", -2))
-    total = first[2 * size :] + second[:size] + third
+    first = as_float(shifted(wire(jnp.concatenate([items[1], items[3], items[4]])), "seq", -1))
+    second = as_float(shifted(wire(jnp.concatenate([items[2], items[5]])), "seq", -2))
+    third = as_float(shifted(wire(first[size : 2 * size]), "seq", -2))
+    fourth = as_float(
+        shifted(wire(first[2 * size :] + second[size:]), "seq", -3)
+    )
+    total = first[:size] + second[:size] + third + fourth
     got_key, got_value, reverse_in = unpacked(total, (kv_shape, kv_shape, state_shape))
     soft_key_grad = soft_key_grad + got_key
     soft_value_grad = soft_value_grad + got_value

time: 102 us -> 111 us (1.088)
  the two profiles are of different devices: /device:TPU:481 before, /device:TPU:193 now
where the time goes in v12:
time: 111 us
  waiting for transfers between devices  33.9 us (31%)
  starting transfers between devices  30 us (27%)
  local copies, waits for them, and re-layouts  20.1 us (18%)
  blocking collectives  15.7 us (14%)
  matrix products  6.15 us (6%)
  other arithmetic  3.84 us (3%)
  between operations  1.35 us (1%)
    ppermute x8, waiting for transfers between devices, shifted(): lax.ppermute(value, axis, [(source, source + steps) for source in range(f...  33.9 us
    ppermute x8, starting transfers between devices, shifted(): lax.ppermute(value, axis, [(source, source + steps) for source in range(f...  30 us
    all_gather x2, blocking collectives, tp_sum(): value = jnp.sum(lax.all_gather(value, axis), axis=0)  15.7 us
    unnamed x56, local copies, waits for them, and re-layouts  15.6 us
  transfers between devices with their start and end apart: 8, of which 6 were waited for; matrix products, arithmetic and copies ran while one was open for 7% of the time, Pallas kernels for 0%

profile of v12, /device:TPU:193, one launch (start us, length us, event | category | flops | bytes accessed | tf_op | source)
XLA Modules:
  0.0 110.9 jit_solution(17991495916143063014)
XLA Ops:
  0.8 0.7 multiply_exponential_fusion.2
  1.5 0.7 pad_add_fusion
  2.4 0.9 copy.197
  3.3 0.9 copy.196
  4.2 1.0 copy.233
  5.5 3.5 %collective-permute-start = (bf16[98304]{0:T(1024)(128)(2,1)S(1)}, bf16[98304]{0:T(1024)(128)(2,1)S(1)}, u32[]{:S(2)}, u32[]{:S(2)}) collective-permute-start(bf16[98304]{0:T(1024)(128)(2,1)S(1)} %pad_maximum_fusion.1), channel_id=1, source_target_pairs={{0,32},{16,48},{32,64},{48,80},{64,96},{80,112},{96,128},{112,144}... | collective-permute-start | bytes 589832 | tf_op jit(solution)/shard_map/ppermute | solution.py:21
  10.8 2.3 %collective-permute-done = bf16[98304]{0:T(1024)(128)(2,1)S(1)} collective-permute-done((bf16[98304]{0:T(1024)(128)(2,1)S(1)}, bf16[98304]{0:T(1024)(128)(2,1)S(1)}, u32[]{:S(2)}, u32[]{:S(2)}) %collective-permute-start) | collective-permute-done | bytes 196640 | tf_op jit(solution)/shard_map/ppermute | solution.py:21
  13.2 5.6 %collective-permute-start.1 = (bf16[196608]{0:T(1024)(128)(2,1)S(1)}, bf16[196608]{0:T(1024)(128)(2,1)S(1)}, u32[]{:S(2)}, u32[]{:S(2)}) collective-permute-start(bf16[196608]{0:T(1024)(128)(2,1)S(1)} %pad_maximum_fusion), channel_id=1, source_target_pairs={{0,16},{16,32},{32,48},{48,64},{64,80},{80,96},{96,112},{112,128},... | collective-permute-start | bytes 1179656 | tf_op jit(solution)/shard_map/ppermute | solution.py:21
  18.8 5.0 %collective-permute-start.3 = (bf16[98304]{0:T(1024)(128)(2,1)S(1)}, bf16[98304]{0:T(1024)(128)(2,1)S(1)}, u32[]{:S(2)}, u32[]{:S(2)}) collective-permute-start(bf16[98304]{0:T(1024)(128)(2,1)S(1)} %collective-permute-done), channel_id=1, source_target_pairs={{0,48},{16,64},{32,80},{48,96},{64,112},{80,128},{96,144},{112,160... | collective-permute-start | bytes 589832 | tf_op jit(solution)/shard_map/ppermute | solution.py:21
  23.9 2.3 %collective-permute-start.2 = (bf16[98304]{0:T(1024)(128)(2,1)S(1)}, bf16[98304]{0:T(1024)(128)(2,1)S(1)}, u32[]{:S(2)}, u32[]{:S(2)}) collective-permute-start(bf16[98304]{0:T(1024)(128)(2,1)S(1)} %collective-permute-done), channel_id=1, source_target_pairs={{0,32},{16,48},{32,64},{48,80},{64,96},{80,112},{96,128},{112,144}... | collective-permute-start | bytes 589832 | tf_op jit(solution)/shard_map/ppermute | solution.py:21
  26.2 3.4 %collective-permute-done.3 = bf16[98304]{0:T(1024)(128)(2,1)S(1)} collective-permute-done((bf16[98304]{0:T(1024)(128)(2,1)S(1)}, bf16[98304]{0:T(1024)(128)(2,1)S(1)}, u32[]{:S(2)}, u32[]{:S(2)}) %collective-permute-start.3) | collective-permute-done | bytes 196640 | tf_op jit(solution)/shard_map/ppermute | solution.py:21
  29.6 4.2 %collective-permute-done.2 = bf16[98304]{0:T(1024)(128)(2,1)S(1)} collective-permute-done((bf16[98304]{0:T(1024)(128)(2,1)S(1)}, bf16[98304]{0:T(1024)(128)(2,1)S(1)}, u32[]{:S(2)}, u32[]{:S(2)}) %collective-permute-start.2) | collective-permute-done | bytes 196640 | tf_op jit(solution)/shard_map/ppermute | solution.py:21
  33.9 0.7 copy-done.8
  35.6 8.0 %all-gather.2 = f32[4,2,128]{2,1,0:T(2,128)S(1)} all-gather(f32[1,2,128]{2,1,0:T(2,128)S(1)} %maximum_bitcast_fusion), channel_id=2, replica_groups=mesh['seq'=64,'tp_outer'=4,'tp_inner'=4] {'tp_inner'}, dimensions={0}, use_global_device_ids=true | all-gather | bytes 5120 | tf_op jit(solution)/shard_map/all_gather | solution.py:26
  43.6 7.7 %all-gather.3 = f32[4,2,128]{2,1,0:T(2,128)S(1)} all-gather(f32[1,2,128]{2,1,0:T(2,128)S(1)} %bitcast.285), channel_id=3, replica_groups=mesh['seq'=64,'tp_outer'=4,'tp_inner'=4] {'tp_outer'}, dimensions={0}, use_global_device_ids=true | all-gather | bytes 5120 | tf_op jit(solution)/shard_map/all_gather | solution.py:26
  52.0 0.4 fusion.69
  52.4 1.5 %fusion.71 = (bf16[768,2,128]{0,2,1:T(8,128)(2,1)S(1)}, f32[768,2,128]{0,2,1:T(8,128)}) fusion(bf16[128,2,128]{0,2,1:T(8,128)(2,1)S(1)} %bitcast.282, f32[2,128]{1,0:T(2,128)S(1)} %get-tuple-element.71, bf16[768,2,128]{2,0,1:T(8,128)(2,1)S(1)} %constant_dynamic-update-slice_fusion, bf16[128,2,128]{0,2,1:T(8,128)(2,1)S(1)} %bitcast.241, ...), kind=kOutput, calls=%fused_computation.166 | convolution fusion | flops 101843968 | bytes 1803264 | tf_op jit(solution)/shard_map/htu,thd->uhd/dot_general | solution.py:263
  53.9 0.7 fusion.24
  56.2 0.6 constant_dynamic-update-slice_fusion.3
  56.8 0.6 constant_dynamic-update-slice_fusion.2
  57.5 0.6 constant_dynamic-update-slice_fusion.12
  58.4 0.6 constant_dynamic-update-slice_fusion.10
  59.0 0.6 constant_dynamic-update-slice_fusion.8
  59.7 0.6 constant_dynamic-update-slice_fusion.6
  60.3 0.6 constant_dynamic-update-slice_fusion.4
  60.9 0.6 constant_dynamic-update-slice_fusion.16
  61.5 0.6 constant_dynamic-update-slice_fusion.15
  62.1 0.6 constant_dynamic-update-slice_fusion.14
  62.8 6.9 %collective-permute-start.4 = (bf16[294912]{0:T(1024)(128)(2,1)}, bf16[294912]{0:T(1024)(128)(2,1)S(1)}, u32[]{:S(2)}, u32[]{:S(2)}) collective-permute-start(bf16[294912]{0:T(1024)(128)(2,1)} %constant_dynamic-update-slice_fusion.14), channel_id=1, source_target_pairs={{16,0},{32,16},{48,32},{64,48},{80,64},{96,80},{112,96},{128,112},... | collective-permute-start | bytes 1769480 | tf_op jit(solution)/shard_map/ppermute | solution.py:21
  69.7 0.6 constant_dynamic-update-slice_fusion.13
  70.3 0.6 constant_dynamic-update-slice_fusion.11
  71.0 0.6 constant_dynamic-update-slice_fusion.9
  71.6 0.6 constant_dynamic-update-slice_fusion.7
  72.2 0.6 constant_dynamic-update-slice_fusion.5
  73.0 1.9 %collective-permute-start.5 = (bf16[196608]{0:T(1024)(128)(2,1)}, bf16[196608]{0:T(1024)(128)(2,1)S(1)}, u32[]{:S(2)}, u32[]{:S(2)}) collective-permute-start(bf16[196608]{0:T(1024)(128)(2,1)} %constant_dynamic-update-slice_fusion.5), channel_id=1, source_target_pairs={{32,0},{48,16},{64,32},{80,48},{96,64},{112,80},{128,96},{144,112}... | collective-permute-start | bytes 1179656 | tf_op jit(solution)/shard_map/ppermute | solution.py:21
  75.1 0.7 copy.175
  75.9 0.3 fusion.19
  76.2 0.7 copy.178
  77.0 10.1 %collective-permute-done.5 = bf16[196608]{0:T(1024)(128)(2,1)S(1)} collective-permute-done((bf16[196608]{0:T(1024)(128)(2,1)}, bf16[196608]{0:T(1024)(128)(2,1)S(1)}, u32[]{:S(2)}, u32[]{:S(2)}) %collective-permute-start.5) | collective-permute-done | bytes 393248 | tf_op jit(solution)/shard_map/ppermute | solution.py:21
  87.2 1.9 %collective-permute-start.6 = (bf16[98304]{0:T(1024)(128)(2,1)S(1)}, bf16[98304]{0:T(1024)(128)(2,1)S(1)}, u32[]{:S(2)}, u32[]{:S(2)}) collective-permute-start(bf16[98304]{0:T(1024)(128)(2,1)S(1)} %slice.449), channel_id=1, source_target_pairs={{32,0},{48,16},{64,32},{80,48},{96,64},{112,80},{128,96},{144,112}... | collective-permute-start | bytes 589832 | tf_op jit(solution)/shard_map/ppermute | solution.py:21
  89.2 2.6 %collective-permute-start.7 = (bf16[98304]{0:T(1024)(128)(2,1)S(1)}, bf16[98304]{0:T(1024)(128)(2,1)S(1)}, u32[]{:S(2)}, u32[]{:S(2)}) collective-permute-start(bf16[98304]{0:T(1024)(128)(2,1)S(1)} %fusion.25), channel_id=1, source_target_pairs={{48,0},{64,16},{80,32},{96,48},{112,64},{128,80},{144,96},{160,112... | collective-permute-start | bytes 589832 | tf_op jit(solution)/shard_map/ppermute | solution.py:21
  92.0 3.7 %collective-permute-done.6 = bf16[98304]{0:T(1024)(128)(2,1)S(1)} collective-permute-done((bf16[98304]{0:T(1024)(128)(2,1)S(1)}, bf16[98304]{0:T(1024)(128)(2,1)S(1)}, u32[]{:S(2)}, u32[]{:S(2)}) %collective-permute-start.6) | collective-permute-done | bytes 196640 | tf_op jit(solution)/shard_map/ppermute | solution.py:21
  95.7 10.2 %collective-permute-done.7 = bf16[98304]{0:T(1024)(128)(2,1)S(1)} collective-permute-done((bf16[98304]{0:T(1024)(128)(2,1)S(1)}, bf16[98304]{0:T(1024)(128)(2,1)S(1)}, u32[]{:S(2)}, u32[]{:S(2)}) %collective-permute-start.7) | collective-permute-done | bytes 196640 | tf_op jit(solution)/shard_map/ppermute | solution.py:21
  106.6 0.7 copy.177
  107.5 0.9 fusion.30
  108.4 0.7 copy.180
  109.3 0.7 copy.179
  110.2 0.7 copy.176
  (114 shorter events, 7.5 us)
Async XLA Ops:
  0.6 4.6 %copy-start = (bf16[128,256]{1,0:T(8,128)(2,1)S(1)}, bf16[128,256]{1,0:T(8,128)(2,1)}, u32[]{:S(2)}) copy-start(bf16[128,256]{1,0:T(8,128)(2,1)} %param.13) | copy-start | bytes 196612
  0.6 8.8 %copy-start.2 = (bf16[128,256]{1,0:T(8,128)(2,1)S(1)}, bf16[128,256]{1,0:T(8,128)(2,1)}, u32[]{:S(2)}) copy-start(bf16[128,256]{1,0:T(8,128)(2,1)} %param.19) | copy-start | bytes 196612
  0.7 8.6 %copy-start.1 = (bf16[128,256]{1,0:T(8,128)(2,1)S(1)}, bf16[128,256]{1,0:T(8,128)(2,1)}, u32[]{:S(2)}) copy-start(bf16[128,256]{1,0:T(8,128)(2,1)} %param.18) | copy-start | bytes 196612
  0.7 9.9 %copy-start.4 = (bf16[128,256]{1,0:T(8,128)(2,1)S(1)}, bf16[128,256]{1,0:T(8,128)(2,1)}, u32[]{:S(2)}) copy-start(bf16[128,256]{1,0:T(8,128)(2,1)} %param.12) | copy-start | bytes 196612
  0.7 8.9 %copy-start.5 = (bf16[128,256]{1,0:T(8,128)(2,1)S(1)}, bf16[128,256]{1,0:T(8,128)(2,1)}, u32[]{:S(2)}) copy-start(bf16[128,256]{1,0:T(8,128)(2,1)} %param.11) | copy-start | bytes 196612
  0.7 9.1 %copy-start.6 = (bf16[128,256]{1,0:T(8,128)(2,1)S(1)}, bf16[128,256]{1,0:T(8,128)(2,1)}, u32[]{:S(2)}) copy-start(bf16[128,256]{1,0:T(8,128)(2,1)} %param.17) | copy-start | bytes 196612
  0.7 9.2 %copy-start.7 = (bf16[128,256]{1,0:T(8,128)(2,1)S(1)}, bf16[128,256]{1,0:T(8,128)(2,1)}, u32[]{:S(2)}) copy-start(bf16[128,256]{1,0:T(8,128)(2,1)} %param.20) | copy-start | bytes 196612
  5.5 7.7 %collective-permute-start = (bf16[98304]{0:T(1024)(128)(2,1)S(1)}, bf16[98304]{0:T(1024)(128)(2,1)S(1)}, u32[]{:S(2)}, u32[]{:S(2)}) collective-permute-start(bf16[98304]{0:T(1024)(128)(2,1)S(1)} %pad_maximum_fusion.1), channel_id=1, source_target_pairs={{0,32},{16,48},{32,64},{48,80},{64,96},{80,112},{96,128},{112,144}... | collective-permute-start | bytes 589832 | tf_op jit(solution)/shard_map/ppermute | solution.py:21
  13.2 21.4 %collective-permute-start.1 = (bf16[196608]{0:T(1024)(128)(2,1)S(1)}, bf16[196608]{0:T(1024)(128)(2,1)S(1)}, u32[]{:S(2)}, u32[]{:S(2)}) collective-permute-start(bf16[196608]{0:T(1024)(128)(2,1)S(1)} %pad_maximum_fusion), channel_id=1, source_target_pairs={{0,16},{16,32},{32,48},{48,64},{64,80},{80,96},{96,112},{112,128},... | collective-permute-start | bytes 1179656 | tf_op jit(solution)/shard_map/ppermute | solution.py:21
  18.8 10.8 %collective-permute-start.3 = (bf16[98304]{0:T(1024)(128)(2,1)S(1)}, bf16[98304]{0:T(1024)(128)(2,1)S(1)}, u32[]{:S(2)}, u32[]{:S(2)}) collective-permute-start(bf16[98304]{0:T(1024)(128)(2,1)S(1)} %collective-permute-done), channel_id=1, source_target_pairs={{0,48},{16,64},{32,80},{48,96},{64,112},{80,128},{96,144},{112,160... | collective-permute-start | bytes 589832 | tf_op jit(solution)/shard_map/ppermute | solution.py:21
  23.9 9.9 %collective-permute-start.2 = (bf16[98304]{0:T(1024)(128)(2,1)S(1)}, bf16[98304]{0:T(1024)(128)(2,1)S(1)}, u32[]{:S(2)}, u32[]{:S(2)}) collective-permute-start(bf16[98304]{0:T(1024)(128)(2,1)S(1)} %collective-permute-done), channel_id=1, source_target_pairs={{0,32},{16,48},{32,64},{48,80},{64,96},{80,112},{96,128},{112,144}... | collective-permute-start | bytes 589832 | tf_op jit(solution)/shard_map/ppermute | solution.py:21
  33.9 0.7 copy-start.8
  33.9 1.6 %copy-start.3 = (bf16[128,256]{1,0:T(8,128)(2,1)S(1)}, bf16[128,256]{1,0:T(8,128)(2,1)}, u32[]{:S(2)}) copy-start(bf16[128,256]{1,0:T(8,128)(2,1)} %param.16) | copy-start | bytes 196612
  33.9 1.6 %copy-start.10 = (f32[256]{0:T(256)S(1)}, f32[256]{0:T(256)}, u32[]{:S(2)}) copy-start(f32[256]{0:T(256)} %param.15) | copy-start | bytes 3076
  34.8 17.0 %copy-start.9 = (bf16[768,2,128]{2,0,1:T(8,128)(2,1)S(1)}, bf16[768,2,128]{2,0,1:T(8,128)(2,1)}, u32[]{:S(2)}) copy-start(bf16[768,2,128]{2,0,1:T(8,128)(2,1)} %copy-done.8) | copy-start | bytes 1179652
  62.8 24.4 %collective-permute-start.4 = (bf16[294912]{0:T(1024)(128)(2,1)}, bf16[294912]{0:T(1024)(128)(2,1)S(1)}, u32[]{:S(2)}, u32[]{:S(2)}) collective-permute-start(bf16[294912]{0:T(1024)(128)(2,1)} %constant_dynamic-update-slice_fusion.14), channel_id=1, source_target_pairs={{16,0},{32,16},{48,32},{64,48},{80,64},{96,80},{112,96},{128,112},... | collective-permute-start | bytes 1769480 | tf_op jit(solution)/shard_map/ppermute | solution.py:21
  73.0 14.0 %collective-permute-start.5 = (bf16[196608]{0:T(1024)(128)(2,1)}, bf16[196608]{0:T(1024)(128)(2,1)S(1)}, u32[]{:S(2)}, u32[]{:S(2)}) collective-permute-start(bf16[196608]{0:T(1024)(128)(2,1)} %constant_dynamic-update-slice_fusion.5), channel_id=1, source_target_pairs={{32,0},{48,16},{64,32},{80,48},{96,64},{112,80},{128,96},{144,112}... | collective-permute-start | bytes 1179656 | tf_op jit(solution)/shard_map/ppermute | solution.py:21
  87.2 8.5 %collective-permute-start.6 = (bf16[98304]{0:T(1024)(128)(2,1)S(1)}, bf16[98304]{0:T(1024)(128)(2,1)S(1)}, u32[]{:S(2)}, u32[]{:S(2)}) collective-permute-start(bf16[98304]{0:T(1024)(128)(2,1)S(1)} %slice.449), channel_id=1, source_target_pairs={{32,0},{48,16},{64,32},{80,48},{96,64},{112,80},{128,96},{144,112}... | collective-permute-start | bytes 589832 | tf_op jit(solution)/shard_map/ppermute | solution.py:21
  89.2 16.7 %collective-permute-start.7 = (bf16[98304]{0:T(1024)(128)(2,1)S(1)}, bf16[98304]{0:T(1024)(128)(2,1)S(1)}, u32[]{:S(2)}, u32[]{:S(2)}) collective-permute-start(bf16[98304]{0:T(1024)(128)(2,1)S(1)} %fusion.25), channel_id=1, source_target_pairs={{48,0},{64,16},{80,32},{96,48},{112,64},{128,80},{144,96},{160,112... | collective-permute-start | bytes 589832 | tf_op jit(solution)/shard_map/ppermute | solution.py:21

commit v13 on v11

--- a/solution.py
+++ b/solution.py
@@ -3,6 +3,7 @@
 import jax
 import jax.numpy as jnp
 from jax import lax
+from jax.experimental.layout import Layout, with_layout_constraint
 from jax.sharding import PartitionSpec as P
 
 HD = 128
@@ -302,7 +303,9 @@
     )
 
     def merge_heads(array):
-        return array.reshape(tokens, heads * HD).astype(jnp.bfloat16)
+        return with_layout_constraint(
+            array.reshape(tokens, heads * HD).astype(jnp.bfloat16), Layout(major_to_minor=(0, 1))
+        )
 
     return (
         merge_heads(lin_query_grad),

time: 102 us -> 101 us (level)
  local copies, waits for them, and re-layouts: 10.6 us -> 9.29 us
    unnamed x57 -> x49, local copies, waits for them, and re-layouts: 7.31 us -> 2.84 us
    convert_element_type x1 -> x5, local copies, waits for them, and re-layouts: 0.12 us -> 3.42 us  [merge_heads(): array.reshape(tokens, heads * HD).astype(jnp.bfloat16)]
where the time goes in v13:
time: 101 us
  waiting for transfers between devices  37.4 us (37%)
  starting transfers between devices  24.7 us (24%)
  blocking collectives  15.7 us (16%)
  local copies, waits for them, and re-layouts  9.29 us (9%)
  matrix products  7.38 us (7%)
  other arithmetic  5.15 us (5%)
  between operations  1.39 us (1%)
    ppermute x7, waiting for transfers between devices, shifted(): lax.ppermute(value, axis, [(source, source + steps) for source in range(f...  37.4 us
    ppermute x7, starting transfers between devices, shifted(): lax.ppermute(value, axis, [(source, source + steps) for source in range(f...  24.7 us
    all_gather x2, blocking collectives, tp_sum(): value = jnp.sum(lax.all_gather(value, axis), axis=0)  15.7 us
    convert_element_type x5, local copies, waits for them, and re-layouts, merge_heads(): array.reshape(tokens, heads * HD).astype(jnp.bfloat16)  3.42 us
    unnamed x49, local copies, waits for them, and re-layouts  2.84 us
  transfers between devices with their start and end apart: 7, of which 6 were waited for; matrix products, arithmetic and copies ran while one was open for 5% of the time, Pallas kernels for 0%

profile of v13, /device:TPU:481, one launch (start us, length us, event | category | flops | bytes accessed | tf_op | source)
XLA Modules:
  0.0 100.9 jit_solution(6537975515229326993)
XLA Ops:
  0.7 0.7 multiply_exponential_fusion.2
  1.5 0.7 pad_add_fusion
  2.4 1.0 copy.201
  3.3 0.9 copy.210
  4.2 0.9 copy.209
  5.2 0.2 convolution_convert_fusion
  5.5 4.8 %collective-permute-start = (bf16[98304]{0:T(1024)(128)(2,1)S(1)}, bf16[98304]{0:T(1024)(128)(2,1)S(1)}, u32[]{:S(2)}, u32[]{:S(2)}) collective-permute-start(bf16[98304]{0:T(1024)(128)(2,1)S(1)} %pad_maximum_fusion.2), channel_id=1, source_target_pairs={{0,32},{16,48},{32,64},{48,80},{64,96},{80,112},{96,128},{112,144}... | collective-permute-start | bytes 589832 | tf_op jit(solution)/shard_map/ppermute | solution.py:22
  11.5 0.3 fusion.31
  11.8 0.2 fusion.21
  12.0 1.8 %collective-permute-done = bf16[98304]{0:T(1024)(128)(2,1)S(1)} collective-permute-done((bf16[98304]{0:T(1024)(128)(2,1)S(1)}, bf16[98304]{0:T(1024)(128)(2,1)S(1)}, u32[]{:S(2)}, u32[]{:S(2)}) %collective-permute-start) | collective-permute-done | bytes 196640 | tf_op jit(solution)/shard_map/ppermute | solution.py:22
  13.8 6.8 %collective-permute-start.1 = (bf16[196608]{0:T(1024)(128)(2,1)S(1)}, bf16[196608]{0:T(1024)(128)(2,1)S(1)}, u32[]{:S(2)}, u32[]{:S(2)}) collective-permute-start(bf16[196608]{0:T(1024)(128)(2,1)S(1)} %pad_maximum_fusion), channel_id=1, source_target_pairs={{0,16},{16,32},{32,48},{48,64},{64,80},{80,96},{96,112},{112,128},... | collective-permute-start | bytes 1179656 | tf_op jit(solution)/shard_map/ppermute | solution.py:22
  20.6 1.9 %collective-permute-start.3 = (bf16[98304]{0:T(1024)(128)(2,1)S(1)}, bf16[98304]{0:T(1024)(128)(2,1)S(1)}, u32[]{:S(2)}, u32[]{:S(2)}) collective-permute-start(bf16[98304]{0:T(1024)(128)(2,1)S(1)} %collective-permute-done), channel_id=1, source_target_pairs={{0,48},{16,64},{32,80},{48,96},{64,112},{80,128},{96,144},{112,160... | collective-permute-start | bytes 589832 | tf_op jit(solution)/shard_map/ppermute | solution.py:22
  22.5 1.9 %collective-permute-start.2 = (bf16[98304]{0:T(1024)(128)(2,1)S(1)}, bf16[98304]{0:T(1024)(128)(2,1)S(1)}, u32[]{:S(2)}, u32[]{:S(2)}) collective-permute-start(bf16[98304]{0:T(1024)(128)(2,1)S(1)} %collective-permute-done), channel_id=1, source_target_pairs={{0,32},{16,48},{32,64},{48,80},{64,96},{80,112},{96,128},{112,144}... | collective-permute-start | bytes 589832 | tf_op jit(solution)/shard_map/ppermute | solution.py:22
  24.4 9.3 %collective-permute-done.3 = bf16[98304]{0:T(1024)(128)(2,1)S(1)} collective-permute-done((bf16[98304]{0:T(1024)(128)(2,1)S(1)}, bf16[98304]{0:T(1024)(128)(2,1)S(1)}, u32[]{:S(2)}, u32[]{:S(2)}) %collective-permute-start.3) | collective-permute-done | bytes 196640 | tf_op jit(solution)/shard_map/ppermute | solution.py:22
  33.8 2.0 %collective-permute-done.2 = bf16[98304]{0:T(1024)(128)(2,1)S(1)} collective-permute-done((bf16[98304]{0:T(1024)(128)(2,1)S(1)}, bf16[98304]{0:T(1024)(128)(2,1)S(1)}, u32[]{:S(2)}, u32[]{:S(2)}) %collective-permute-start.2) | collective-permute-done | bytes 196640 | tf_op jit(solution)/shard_map/ppermute | solution.py:22
  36.1 0.3 fusion.14
  36.4 0.2 multiply_reduce_fusion.1
  36.9 8.0 %all-gather.2 = f32[4,2,128]{2,1,0:T(2,128)S(1)} all-gather(f32[1,2,128]{2,1,0:T(2,128)S(1)} %maximum_bitcast_fusion), channel_id=2, replica_groups=mesh['seq'=64,'tp_outer'=4,'tp_inner'=4] {'tp_inner'}, dimensions={0}, use_global_device_ids=true | all-gather | bytes 5120 | tf_op jit(solution)/shard_map/all_gather | solution.py:27
  44.8 7.7 %all-gather.3 = f32[4,2,128]{2,1,0:T(2,128)S(1)} all-gather(f32[1,2,128]{2,1,0:T(2,128)S(1)} %bitcast.299), channel_id=3, replica_groups=mesh['seq'=64,'tp_outer'=4,'tp_inner'=4] {'tp_outer'}, dimensions={0}, use_global_device_ids=true | all-gather | bytes 5120 | tf_op jit(solution)/shard_map/all_gather | solution.py:27
  52.8 1.3 %fusion.80 = (f32[2,128]{1,0:T(2,128)S(1)}, f32[2,128,768]{1,2,0:T(8,128)}) fusion(bf16[768,2,128]{2,0,1:T(8,128)(2,1)S(1)} %constant_dynamic-update-slice_fusion, bf16[128,2,128]{0,2,1:T(8,128)(2,1)S(1)} %bitcast.261, pred[128,768]{0,1:T(8,128)(4,1)S(1)} %fusion.31), kind=kOutput, calls=%fused_computation.175 | convolution fusion | flops 51118848 | bytes 1344512 | tf_op jit(solution)/shard_map/sub | solution.py:247
  54.1 0.6 fusion.82
  54.7 0.4 copy-done.11
  55.1 0.7 fusion.24
  56.4 1.5 %fusion.8 = bf16[2,128,768]{1,2,0:T(8,128)(2,1)S(1)} fusion(bf16[768,2,128]{2,0,1:T(8,128)(2,1)} %copy-done.10, bf16[128,2,128]{0,2,1:T(8,128)(2,1)S(1)} %bitcast.295, f32[2,128]{1,0:T(2,128)S(1)} %bitcast.302, f32[2,128,768]{1,2,0:T(8,128)} %get-tuple-element.56, f32[2,128]{1,0:T(2,128)S(1)} %get-tuple-element.55), kind=kOutput, calls=%fused_computation.12 | convolution fusion | flops 51118080 | bytes 1640448 | tf_op jit(solution)/shard_map/thd,uhd->htu/dot_general | solution.py:105
  58.0 0.3 fusion.81
  58.6 0.2 broadcast_multiply_fusion.1
  59.0 5.5 %collective-permute-start.4 = (bf16[294912]{0:T(1024)(128)(2,1)S(1)}, bf16[294912]{0:T(1024)(128)(2,1)S(1)}, u32[]{:S(2)}, u32[]{:S(2)}) collective-permute-start(bf16[294912]{0:T(1024)(128)(2,1)S(1)} %constant_dynamic-update-slice_fusion.3), channel_id=1, source_target_pairs={{16,0},{32,16},{48,32},{64,48},{80,64},{96,80},{112,96},{128,112},... | collective-permute-start | bytes 1769480 | tf_op jit(solution)/shard_map/ppermute | solution.py:22
  64.7 0.2 fusion.22
  64.9 0.3 fusion.12
  65.2 8.8 %collective-permute-done.4 = bf16[294912]{0:T(1024)(128)(2,1)S(1)} collective-permute-done((bf16[294912]{0:T(1024)(128)(2,1)S(1)}, bf16[294912]{0:T(1024)(128)(2,1)S(1)}, u32[]{:S(2)}, u32[]{:S(2)}) %collective-permute-start.4) | collective-permute-done | bytes 589856 | tf_op jit(solution)/shard_map/ppermute | solution.py:22
  74.2 0.8 pad_maximum_fusion.1
  75.0 1.9 %collective-permute-start.5 = (bf16[196608]{0:T(1024)(128)(2,1)}, bf16[196608]{0:T(1024)(128)(2,1)S(1)}, u32[]{:S(2)}, u32[]{:S(2)}) collective-permute-start(bf16[196608]{0:T(1024)(128)(2,1)} %pad_maximum_fusion.1), channel_id=1, source_target_pairs={{32,0},{48,16},{64,32},{80,48},{96,64},{112,80},{128,96},{144,112}... | collective-permute-start | bytes 1179656 | tf_op jit(solution)/shard_map/ppermute | solution.py:22
  76.9 0.2 fusion.23
  77.0 0.7 copy.198
  77.8 0.3 fusion.25
  78.1 0.6 copy.265
  78.8 0.2 convolution_bitcast_fusion.5
  79.0 8.5 %collective-permute-done.5 = bf16[196608]{0:T(1024)(128)(2,1)S(1)} collective-permute-done((bf16[196608]{0:T(1024)(128)(2,1)}, bf16[196608]{0:T(1024)(128)(2,1)S(1)}, u32[]{:S(2)}, u32[]{:S(2)}) %collective-permute-start.5) | collective-permute-done | bytes 393248 | tf_op jit(solution)/shard_map/ppermute | solution.py:22
  87.4 1.9 %collective-permute-start.6 = (bf16[98304]{0:T(1024)(128)(2,1)S(1)}, bf16[98304]{0:T(1024)(128)(2,1)S(1)}, u32[]{:S(2)}, u32[]{:S(2)}) collective-permute-start(bf16[98304]{0:T(1024)(128)(2,1)S(1)} %slice.451), channel_id=1, source_target_pairs={{32,0},{48,16},{64,32},{80,48},{96,64},{112,80},{128,96},{144,112}... | collective-permute-start | bytes 589832 | tf_op jit(solution)/shard_map/ppermute | solution.py:22
  89.4 0.2 convolution_bitcast_fusion.3
  89.6 7.0 %collective-permute-done.6 = bf16[98304]{0:T(1024)(128)(2,1)S(1)} collective-permute-done((bf16[98304]{0:T(1024)(128)(2,1)S(1)}, bf16[98304]{0:T(1024)(128)(2,1)S(1)}, u32[]{:S(2)}, u32[]{:S(2)}) %collective-permute-start.6) | collective-permute-done | bytes 196640 | tf_op jit(solution)/shard_map/ppermute | solution.py:22
  96.7 0.3 fusion.27
  96.9 0.3 fusion.26
  97.2 0.6 copy.267
  97.9 0.6 copy.266
  98.6 0.9 fusion.33
  99.5 0.7 copy.199
  100.3 0.6 copy_bitcast_fusion
  (109 shorter events, 3.8 us)
Async XLA Ops:
  0.6 4.6 %copy-start = (bf16[128,256]{1,0:T(8,128)(2,1)S(1)}, bf16[128,256]{1,0:T(8,128)(2,1)}, u32[]{:S(2)}) copy-start(bf16[128,256]{1,0:T(8,128)(2,1)} %param.13) | copy-start | bytes 196612
  0.6 10.0 %copy-start.2 = (bf16[128,256]{1,0:T(8,128)(2,1)S(1)}, bf16[128,256]{1,0:T(8,128)(2,1)}, u32[]{:S(2)}) copy-start(bf16[128,256]{1,0:T(8,128)(2,1)} %param.19) | copy-start | bytes 196612
  0.7 9.8 %copy-start.1 = (bf16[128,256]{1,0:T(8,128)(2,1)S(1)}, bf16[128,256]{1,0:T(8,128)(2,1)}, u32[]{:S(2)}) copy-start(bf16[128,256]{1,0:T(8,128)(2,1)} %param.18) | copy-start | bytes 196612
  0.7 10.2 %copy-start.7 = (bf16[128,256]{1,0:T(8,128)(2,1)S(1)}, bf16[128,256]{1,0:T(8,128)(2,1)}, u32[]{:S(2)}) copy-start(bf16[128,256]{1,0:T(8,128)(2,1)} %param.11) | copy-start | bytes 196612
  0.7 10.3 %copy-start.8 = (bf16[128,256]{1,0:T(8,128)(2,1)S(1)}, bf16[128,256]{1,0:T(8,128)(2,1)}, u32[]{:S(2)}) copy-start(bf16[128,256]{1,0:T(8,128)(2,1)} %param.17) | copy-start | bytes 196612
  0.7 10.4 %copy-start.9 = (bf16[128,256]{1,0:T(8,128)(2,1)S(1)}, bf16[128,256]{1,0:T(8,128)(2,1)}, u32[]{:S(2)}) copy-start(bf16[128,256]{1,0:T(8,128)(2,1)} %param.20) | copy-start | bytes 196612
  5.5 8.3 %collective-permute-start = (bf16[98304]{0:T(1024)(128)(2,1)S(1)}, bf16[98304]{0:T(1024)(128)(2,1)S(1)}, u32[]{:S(2)}, u32[]{:S(2)}) collective-permute-start(bf16[98304]{0:T(1024)(128)(2,1)S(1)} %pad_maximum_fusion.2), channel_id=1, source_target_pairs={{0,32},{16,48},{32,64},{48,80},{64,96},{80,112},{96,128},{112,144}... | collective-permute-start | bytes 589832 | tf_op jit(solution)/shard_map/ppermute | solution.py:22
  12.0 24.4 %copy-start.4 = (bf16[2,128,128]{2,1,0:T(8,128)(2,1)}, bf16[2,128,128]{2,1,0:T(8,128)(2,1)S(1)}, u32[]{:S(2)}) copy-start(bf16[2,128,128]{2,1,0:T(8,128)(2,1)S(1)} %fusion.21) | copy-start | bytes 196612
  13.8 22.1 %collective-permute-start.1 = (bf16[196608]{0:T(1024)(128)(2,1)S(1)}, bf16[196608]{0:T(1024)(128)(2,1)S(1)}, u32[]{:S(2)}, u32[]{:S(2)}) collective-permute-start(bf16[196608]{0:T(1024)(128)(2,1)S(1)} %pad_maximum_fusion), channel_id=1, source_target_pairs={{0,16},{16,32},{32,48},{48,64},{64,80},{80,96},{96,112},{112,128},... | collective-permute-start | bytes 1179656 | tf_op jit(solution)/shard_map/ppermute | solution.py:22
  20.6 13.1 %collective-permute-start.3 = (bf16[98304]{0:T(1024)(128)(2,1)S(1)}, bf16[98304]{0:T(1024)(128)(2,1)S(1)}, u32[]{:S(2)}, u32[]{:S(2)}) collective-permute-start(bf16[98304]{0:T(1024)(128)(2,1)S(1)} %collective-permute-done), channel_id=1, source_target_pairs={{0,48},{16,64},{32,80},{48,96},{64,112},{80,128},{96,144},{112,160... | collective-permute-start | bytes 589832 | tf_op jit(solution)/shard_map/ppermute | solution.py:22
  22.5 13.3 %collective-permute-start.2 = (bf16[98304]{0:T(1024)(128)(2,1)S(1)}, bf16[98304]{0:T(1024)(128)(2,1)S(1)}, u32[]{:S(2)}, u32[]{:S(2)}) collective-permute-start(bf16[98304]{0:T(1024)(128)(2,1)S(1)} %collective-permute-done), channel_id=1, source_target_pairs={{0,32},{16,48},{32,64},{48,80},{64,96},{80,112},{96,128},{112,144}... | collective-permute-start | bytes 589832 | tf_op jit(solution)/shard_map/ppermute | solution.py:22
  35.8 0.9 copy-start.3
  35.8 0.9 copy-start.12
  52.8 1.3 %copy-start.10 = (bf16[768,2,128]{2,0,1:T(8,128)(2,1)}, bf16[768,2,128]{2,0,1:T(8,128)(2,1)S(1)}, u32[]{:S(2)}) copy-start(bf16[768,2,128]{2,0,1:T(8,128)(2,1)S(1)} %constant_dynamic-update-slice_fusion.1) | copy-start | bytes 1179652
  54.1 1.0 copy-start.11
  55.1 1.1 %copy-start.6 = (f32[768,2,128]{0,2,1:T(8,128)}, f32[768,2,128]{0,2,1:T(8,128)S(1)}, u32[]{:S(2)}) copy-start(f32[768,2,128]{0,2,1:T(8,128)S(1)} %get-tuple-element.60) | copy-start | bytes 2359300
  59.0 15.1 %collective-permute-start.4 = (bf16[294912]{0:T(1024)(128)(2,1)S(1)}, bf16[294912]{0:T(1024)(128)(2,1)S(1)}, u32[]{:S(2)}, u32[]{:S(2)}) collective-permute-start(bf16[294912]{0:T(1024)(128)(2,1)S(1)} %constant_dynamic-update-slice_fusion.3), channel_id=1, source_target_pairs={{16,0},{32,16},{48,32},{64,48},{80,64},{96,80},{112,96},{128,112},... | collective-permute-start | bytes 1769480 | tf_op jit(solution)/shard_map/ppermute | solution.py:22
  75.0 12.5 %collective-permute-start.5 = (bf16[196608]{0:T(1024)(128)(2,1)}, bf16[196608]{0:T(1024)(128)(2,1)S(1)}, u32[]{:S(2)}, u32[]{:S(2)}) collective-permute-start(bf16[196608]{0:T(1024)(128)(2,1)} %pad_maximum_fusion.1), channel_id=1, source_target_pairs={{32,0},{48,16},{64,32},{80,48},{96,64},{112,80},{128,96},{144,112}... | collective-permute-start | bytes 1179656 | tf_op jit(solution)/shard_map/ppermute | solution.py:22
  77.8 11.6 %copy-start.5 = (bf16[2,128,128]{2,1,0:T(8,128)(2,1)S(1)}, bf16[2,128,128]{2,1,0:T(8,128)(2,1)}, u32[]{:S(2)}) copy-start(bf16[2,128,128]{2,1,0:T(8,128)(2,1)} %copy-done.4) | copy-start | bytes 196612
  87.4 9.1 %collective-permute-start.6 = (bf16[98304]{0:T(1024)(128)(2,1)S(1)}, bf16[98304]{0:T(1024)(128)(2,1)S(1)}, u32[]{:S(2)}, u32[]{:S(2)}) collective-permute-start(bf16[98304]{0:T(1024)(128)(2,1)S(1)} %slice.451), channel_id=1, source_target_pairs={{32,0},{48,16},{64,32},{80,48},{96,64},{112,80},{128,96},{144,112}... | collective-permute-start | bytes 589832 | tf_op jit(solution)/shard_map/ppermute | solution.py:22

commit v14 on v13

--- a/solution.py
+++ b/solution.py
@@ -266,30 +266,52 @@
     )
     soft_key_grad = key_terms[(REACH - 1) * tokens :]
     soft_value_grad = value_terms[(REACH - 1) * tokens :]
+    soft_part = {}
     items = {}
     for back in range(1, REACH):
         lower = (REACH - 1 - back) * tokens
         chain = jnp.prod(behind[REACH - back : REACH - 1], axis=0)
-        items[back] = packed(
-            key_terms[lower : lower + tokens],
-            value_terms[lower : lower + tokens],
-            chain[:, None, None] * back_summary,
-        )
+        soft_part[back] = packed(key_terms[lower : lower + tokens], value_terms[lower : lower + tokens])
+        items[back] = jnp.concatenate(
+            [soft_part[back], (chain[:, None, None] * back_summary).reshape(-1)]
+        )
+    soft_size = soft_part[1].shape[0]
     size = items[1].shape[0]
 
     def wire(value):
         return value.astype(jnp.bfloat16)
 
-    first = as_float(shifted(wire(jnp.concatenate([items[5], items[3], items[1]])), "seq", -1))
+    first = as_float(
+        shifted(
+            wire(
+                jnp.concatenate(
+                    [soft_part[5], soft_part[3], soft_part[1], back_summary.reshape(-1)]
+                )
+            ),
+            "seq",
+            -1,
+        )
+    )
+    raw = first[3 * soft_size :].reshape(state_shape)
+
+    def landed(slot, back):
+        chain = jnp.prod(behind[REACH - back + 1 : REACH], axis=0)
+        return jnp.concatenate(
+            [
+                first[slot * soft_size : (slot + 1) * soft_size],
+                (chain[:, None, None] * raw).reshape(-1),
+            ]
+        )
+
     second = as_float(
         shifted(
-            wire(jnp.concatenate([items[2] + first[size : 2 * size], items[4] + first[:size]])),
+            wire(jnp.concatenate([items[2] + landed(1, 3), items[4] + landed(0, 5)])),
             "seq",
             -2,
         )
     )
     third = as_float(shifted(wire(second[size:]), "seq", -2))
-    total = first[2 * size :] + second[:size] + third
+    total = landed(2, 1) + second[:size] + third
     got_key, got_value, reverse_in = unpacked(total, (kv_shape, kv_shape, state_shape))
     soft_key_grad = soft_key_grad + got_key
     soft_value_grad = soft_value_grad + got_value

time: 101 us -> 103 us (1.020)
  local copies, waits for them, and re-layouts: 9.29 us -> 15.7 us
  waiting for transfers between devices: 37.4 us -> 33.6 us
  other arithmetic: 5.15 us -> 3.15 us
  matrix products: 7.38 us -> 8.61 us
    unnamed x49 -> x43, local copies, waits for them, and re-layouts: 2.84 us -> 8.6 us
    ppermute x7, waiting for transfers between devices: 37.4 us -> 33.6 us  [shifted(): lax.ppermute(value, axis, [(source, source + steps) for source in range(f...]
    dot_general x1, matrix products: 0.67 us -> 1.95 us  [body(): jnp.einsum('htu,uhd->thd', probs_half, value_window, preferred_element_ty...]
  transfers between devices with their start and end apart: 7 -> 7, of which waited for: 6 -> 5; matrix products, arithmetic and copies ran while one was open for 5% -> 6% of each run, Pallas kernels for 0% -> 0%
where the time goes in v14:
time: 103 us; the launch traced here: 102 us
  waiting for transfers between devices  33.6 us (33%)
  starting transfers between devices  24.4 us (24%)
  local copies, waits for them, and re-layouts  15.7 us (15%)
  blocking collectives  15.7 us (15%)
  matrix products  8.61 us (8%)
  other arithmetic  3.15 us (3%)
  between operations  1.32 us (1%)
    ppermute x7, waiting for transfers between devices, shifted(): lax.ppermute(value, axis, [(source, source + steps) for source in range(f...  33.6 us
    ppermute x7, starting transfers between devices, shifted(): lax.ppermute(value, axis, [(source, source + steps) for source in range(f...  24.4 us
    all_gather x2, blocking collectives, tp_sum(): value = jnp.sum(lax.all_gather(value, axis), axis=0)  15.7 us
    unnamed x43, local copies, waits for them, and re-layouts  8.6 us
    convert_element_type x5, local copies, waits for them, and re-layouts, merge_heads(): array.reshape(tokens, heads * HD).astype(jnp.bfloat16)  3.42 us
  transfers between devices with their start and end apart: 7, of which 5 were waited for; matrix products, arithmetic and copies ran while one was open for 6% of the time, Pallas kernels for 0%

profile of v14, /device:TPU:481, one launch (start us, length us, event | category | flops | bytes accessed | tf_op | source)
XLA Modules:
  0.0 102.4 jit_solution(16806558675994746640)
XLA Ops:
  0.7 0.6 copy-done.10
  1.4 0.6 copy-done.9
  2.3 1.0 copy.201
  3.3 0.8 copy-done.1
  4.5 4.8 %collective-permute-start = (bf16[98304]{0:T(1024)(128)(2,1)S(1)}, bf16[98304]{0:T(1024)(128)(2,1)S(1)}, u32[]{:S(2)}, u32[]{:S(2)}) collective-permute-start(bf16[98304]{0:T(1024)(128)(2,1)S(1)} %pad_maximum_fusion.2), channel_id=1, source_target_pairs={{0,32},{16,48},{32,64},{48,80},{64,96},{80,112},{96,128},{112,144}... | collective-permute-start | bytes 589832 | tf_op jit(solution)/shard_map/ppermute | solution.py:22
  9.9 0.6 copy-done.5
  10.6 0.7 copy-done.6
  11.4 0.7 copy-done.7
  12.5 0.3 fusion.31
  12.8 0.2 fusion.21
  13.1 6.5 %collective-permute-start.1 = (bf16[196608]{0:T(1024)(128)(2,1)S(1)}, bf16[196608]{0:T(1024)(128)(2,1)S(1)}, u32[]{:S(2)}, u32[]{:S(2)}) collective-permute-start(bf16[196608]{0:T(1024)(128)(2,1)S(1)} %pad_maximum_fusion), channel_id=1, source_target_pairs={{0,16},{16,32},{32,48},{48,64},{64,80},{80,96},{96,112},{112,128},... | collective-permute-start | bytes 1179656 | tf_op jit(solution)/shard_map/ppermute | solution.py:22
  19.6 1.9 %collective-permute-start.3 = (bf16[98304]{0:T(1024)(128)(2,1)S(1)}, bf16[98304]{0:T(1024)(128)(2,1)S(1)}, u32[]{:S(2)}, u32[]{:S(2)}) collective-permute-start(bf16[98304]{0:T(1024)(128)(2,1)S(1)} %collective-permute-done), channel_id=1, source_target_pairs={{0,48},{16,64},{32,80},{48,96},{64,112},{80,128},{96,144},{112,160... | collective-permute-start | bytes 589832 | tf_op jit(solution)/shard_map/ppermute | solution.py:22
  21.5 1.9 %collective-permute-start.2 = (bf16[98304]{0:T(1024)(128)(2,1)S(1)}, bf16[98304]{0:T(1024)(128)(2,1)S(1)}, u32[]{:S(2)}, u32[]{:S(2)}) collective-permute-start(bf16[98304]{0:T(1024)(128)(2,1)S(1)} %collective-permute-done), channel_id=1, source_target_pairs={{0,32},{16,48},{32,64},{48,80},{64,96},{80,112},{96,128},{112,144}... | collective-permute-start | bytes 589832 | tf_op jit(solution)/shard_map/ppermute | solution.py:22
  23.5 9.3 %collective-permute-done.3 = bf16[98304]{0:T(1024)(128)(2,1)S(1)} collective-permute-done((bf16[98304]{0:T(1024)(128)(2,1)S(1)}, bf16[98304]{0:T(1024)(128)(2,1)S(1)}, u32[]{:S(2)}, u32[]{:S(2)}) %collective-permute-start.3) | collective-permute-done | bytes 196640 | tf_op jit(solution)/shard_map/ppermute | solution.py:22
  32.7 0.6 copy_dynamic-update-slice_fusion.4
  33.4 1.4 %collective-permute-done.2 = bf16[98304]{0:T(1024)(128)(2,1)S(1)} collective-permute-done((bf16[98304]{0:T(1024)(128)(2,1)S(1)}, bf16[98304]{0:T(1024)(128)(2,1)S(1)}, u32[]{:S(2)}, u32[]{:S(2)}) %collective-permute-start.2) | collective-permute-done | bytes 196640 | tf_op jit(solution)/shard_map/ppermute | solution.py:22
  34.8 0.6 copy_dynamic-update-slice_fusion.3
  35.7 0.3 fusion.14
  36.0 0.2 multiply_reduce_fusion.1
  36.3 0.7 copy-done.3
  37.2 8.0 %all-gather.2 = f32[4,2,128]{2,1,0:T(2,128)S(1)} all-gather(f32[1,2,128]{2,1,0:T(2,128)S(1)} %maximum_bitcast_fusion), channel_id=2, replica_groups=mesh['seq'=64,'tp_outer'=4,'tp_inner'=4] {'tp_inner'}, dimensions={0}, use_global_device_ids=true | all-gather | bytes 5120 | tf_op jit(solution)/shard_map/all_gather | solution.py:27
  45.1 7.7 %all-gather.3 = f32[4,2,128]{2,1,0:T(2,128)S(1)} all-gather(f32[1,2,128]{2,1,0:T(2,128)S(1)} %bitcast.301), channel_id=3, replica_groups=mesh['seq'=64,'tp_outer'=4,'tp_inner'=4] {'tp_outer'}, dimensions={0}, use_global_device_ids=true | all-gather | bytes 5120 | tf_op jit(solution)/shard_map/all_gather | solution.py:27
  52.9 0.6 copy_dynamic-update-slice_fusion.2
  53.6 0.6 copy_dynamic-update-slice_fusion.1
  54.2 0.6 copy_dynamic-update-slice_fusion
  54.9 0.6 constant_dynamic-update-slice_fusion.1
  55.5 1.2 %fusion.81 = (f32[2,128]{1,0:T(2,128)S(1)}, f32[2,128,768]{1,2,0:T(8,128)}) fusion(bf16[768,2,128]{2,0,1:T(8,128)(2,1)S(1)} %constant_dynamic-update-slice_fusion, bf16[128,2,128]{0,2,1:T(8,128)(2,1)S(1)} %bitcast.265, pred[128,768]{0,1:T(8,128)(4,1)S(1)} %fusion.31), kind=kOutput, calls=%fused_computation.174 | convolution fusion | flops 51118848 | bytes 1344512 | tf_op jit(solution)/shard_map/sub | solution.py:247
  56.7 0.6 fusion.83
  57.3 1.9 %fusion.24 = f32[128,2]{0,1:T(2,128)S(1)} fusion(bf16[768,2,128]{2,0,1:T(8,128)(2,1)} %constant_dynamic-update-slice_fusion.1, bf16[128,2,128]{0,2,1:T(8,128)(2,1)S(1)} %bitcast.296, f32[2,128]{1,0:T(2,128)S(1)} %get-tuple-element.55, bf16[768,2,128]{2,0,1:T(8,128)(2,1)S(1)} %constant_dynamic-update-slice_fusion, bf16[128,2,128]{0,2,1:T(8,128)(2,1)S(1)} %bitcast.267, ...), kind=kOutput, calls=%fused_computation.41 | convolution fusion | flops 101745408 | bytes 1017856 | tf_op jit(solution)/shard_map/htu,uhd->thd/dot_general | solution.py:251
  60.0 1.5 %fusion.8 = bf16[2,128,768]{1,2,0:T(8,128)(2,1)S(1)} fusion(bf16[768,2,128]{2,0,1:T(8,128)(2,1)} %constant_dynamic-update-slice_fusion.1, bf16[128,2,128]{0,2,1:T(8,128)(2,1)S(1)} %bitcast.297, f32[2,128]{1,0:T(2,128)S(1)} %bitcast.304, f32[2,128,768]{1,2,0:T(8,128)} %get-tuple-element.56, f32[2,128]{1,0:T(2,128)S(1)} %get-tuple-element.55), kind=kOutput, calls=%fused_computation.12 | convolution fusion | flops 51118080 | bytes 1640448 | tf_op jit(solution)/shard_map/thd,uhd->htu/dot_general | solution.py:105
  61.5 0.3 fusion.82
  62.7 5.5 %collective-permute-start.4 = (bf16[229376]{0:T(1024)(128)(2,1)S(1)}, bf16[229376]{0:T(1024)(128)(2,1)S(1)}, u32[]{:S(2)}, u32[]{:S(2)}) collective-permute-start(bf16[229376]{0:T(1024)(128)(2,1)S(1)} %constant_dynamic-update-slice_fusion.3), channel_id=1, source_target_pairs={{16,0},{32,16},{48,32},{64,48},{80,64},{96,80},{112,96},{128,112},... | collective-permute-start | bytes 1376264 | tf_op jit(solution)/shard_map/ppermute | solution.py:22
  68.4 0.3 fusion.12
  68.7 7.7 %collective-permute-done.4 = bf16[229376]{0:T(1024)(128)(2,1)S(1)} collective-permute-done((bf16[229376]{0:T(1024)(128)(2,1)S(1)}, bf16[229376]{0:T(1024)(128)(2,1)S(1)}, u32[]{:S(2)}, u32[]{:S(2)}) %collective-permute-start.4) | collective-permute-done | bytes 458784 | tf_op jit(solution)/shard_map/ppermute | solution.py:22
  76.7 1.9 %collective-permute-start.5 = (bf16[196608]{0:T(1024)(128)(2,1)S(1)}, bf16[196608]{0:T(1024)(128)(2,1)S(1)}, u32[]{:S(2)}, u32[]{:S(2)}) collective-permute-start(bf16[196608]{0:T(1024)(128)(2,1)S(1)} %pad_maximum_fusion.1), channel_id=1, source_target_pairs={{32,0},{48,16},{64,32},{80,48},{96,64},{112,80},{128,96},{144,112}... | collective-permute-start | bytes 1179656 | tf_op jit(solution)/shard_map/ppermute | solution.py:22
  78.8 0.7 copy.198
  79.5 0.3 fusion.25
  79.8 0.6 copy.265
  80.7 8.2 %collective-permute-done.5 = bf16[196608]{0:T(1024)(128)(2,1)S(1)} collective-permute-done((bf16[196608]{0:T(1024)(128)(2,1)S(1)}, bf16[196608]{0:T(1024)(128)(2,1)S(1)}, u32[]{:S(2)}, u32[]{:S(2)}) %collective-permute-start.5) | collective-permute-done | bytes 393248 | tf_op jit(solution)/shard_map/ppermute | solution.py:22
  88.9 1.9 %collective-permute-start.6 = (bf16[98304]{0:T(1024)(128)(2,1)S(1)}, bf16[98304]{0:T(1024)(128)(2,1)S(1)}, u32[]{:S(2)}, u32[]{:S(2)}) collective-permute-start(bf16[98304]{0:T(1024)(128)(2,1)S(1)} %slice.464), channel_id=1, source_target_pairs={{32,0},{48,16},{64,32},{80,48},{96,64},{112,80},{128,96},{144,112}... | collective-permute-start | bytes 589832 | tf_op jit(solution)/shard_map/ppermute | solution.py:22
  91.2 6.9 %collective-permute-done.6 = bf16[98304]{0:T(1024)(128)(2,1)S(1)} collective-permute-done((bf16[98304]{0:T(1024)(128)(2,1)S(1)}, bf16[98304]{0:T(1024)(128)(2,1)S(1)}, u32[]{:S(2)}, u32[]{:S(2)}) %collective-permute-start.6) | collective-permute-done | bytes 196640 | tf_op jit(solution)/shard_map/ppermute | solution.py:22
  98.2 0.3 fusion.27
  98.5 0.3 fusion.26
  98.7 0.6 copy.267
  99.4 0.6 copy.266
  100.1 0.9 fusion.33
  101.1 0.7 copy.199
  101.8 0.6 copy_bitcast_fusion
  (109 shorter events, 5.2 us)
Async XLA Ops:
  0.6 3.6 %copy-start = (bf16[128,256]{1,0:T(8,128)(2,1)S(1)}, bf16[128,256]{1,0:T(8,128)(2,1)}, u32[]{:S(2)}) copy-start(bf16[128,256]{1,0:T(8,128)(2,1)} %param.13) | copy-start | bytes 196612
  0.7 0.7 copy-start.10
  1.4 0.7 copy-start.9
  2.3 1.0 copy-start.2
  3.3 0.8 copy-start.1
  4.5 8.6 %collective-permute-start = (bf16[98304]{0:T(1024)(128)(2,1)S(1)}, bf16[98304]{0:T(1024)(128)(2,1)S(1)}, u32[]{:S(2)}, u32[]{:S(2)}) collective-permute-start(bf16[98304]{0:T(1024)(128)(2,1)S(1)} %pad_maximum_fusion.2), channel_id=1, source_target_pairs={{0,32},{16,48},{32,64},{48,80},{64,96},{80,112},{96,128},{112,144}... | collective-permute-start | bytes 589832 | tf_op jit(solution)/shard_map/ppermute | solution.py:22
  9.6 0.8 copy-start.5
  10.5 0.8 copy-start.6
  11.3 0.8 copy-start.7
  13.1 22.4 %collective-permute-start.1 = (bf16[196608]{0:T(1024)(128)(2,1)S(1)}, bf16[196608]{0:T(1024)(128)(2,1)S(1)}, u32[]{:S(2)}, u32[]{:S(2)}) collective-permute-start(bf16[196608]{0:T(1024)(128)(2,1)S(1)} %pad_maximum_fusion), channel_id=1, source_target_pairs={{0,16},{16,32},{32,48},{48,64},{64,80},{80,96},{96,112},{112,128},... | collective-permute-start | bytes 1179656 | tf_op jit(solution)/shard_map/ppermute | solution.py:22
  19.6 13.1 %collective-permute-start.3 = (bf16[98304]{0:T(1024)(128)(2,1)S(1)}, bf16[98304]{0:T(1024)(128)(2,1)S(1)}, u32[]{:S(2)}, u32[]{:S(2)}) collective-permute-start(bf16[98304]{0:T(1024)(128)(2,1)S(1)} %collective-permute-done), channel_id=1, source_target_pairs={{0,48},{16,64},{32,80},{48,96},{64,112},{80,128},{96,144},{112,160... | collective-permute-start | bytes 589832 | tf_op jit(solution)/shard_map/ppermute | solution.py:22
  21.5 13.3 %collective-permute-start.2 = (bf16[98304]{0:T(1024)(128)(2,1)S(1)}, bf16[98304]{0:T(1024)(128)(2,1)S(1)}, u32[]{:S(2)}, u32[]{:S(2)}) collective-permute-start(bf16[98304]{0:T(1024)(128)(2,1)S(1)} %collective-permute-done), channel_id=1, source_target_pairs={{0,32},{16,48},{32,64},{48,80},{64,96},{80,112},{96,128},{112,144}... | collective-permute-start | bytes 589832 | tf_op jit(solution)/shard_map/ppermute | solution.py:22
  36.2 0.8 copy-start.3
  36.2 0.8 copy-start.8
  57.3 2.4 %copy-start.4 = (f32[768,2,128]{0,2,1:T(8,128)}, f32[768,2,128]{0,2,1:T(8,128)S(1)}, u32[]{:S(2)}) copy-start(f32[768,2,128]{0,2,1:T(8,128)S(1)} %get-tuple-element.60) | copy-start | bytes 2359300
  62.7 13.7 %collective-permute-start.4 = (bf16[229376]{0:T(1024)(128)(2,1)S(1)}, bf16[229376]{0:T(1024)(128)(2,1)S(1)}, u32[]{:S(2)}, u32[]{:S(2)}) collective-permute-start(bf16[229376]{0:T(1024)(128)(2,1)S(1)} %constant_dynamic-update-slice_fusion.3), channel_id=1, source_target_pairs={{16,0},{32,16},{48,32},{64,48},{80,64},{96,80},{112,96},{128,112},... | collective-permute-start | bytes 1376264 | tf_op jit(solution)/shard_map/ppermute | solution.py:22
  76.7 12.3 %collective-permute-start.5 = (bf16[196608]{0:T(1024)(128)(2,1)S(1)}, bf16[196608]{0:T(1024)(128)(2,1)S(1)}, u32[]{:S(2)}, u32[]{:S(2)}) collective-permute-start(bf16[196608]{0:T(1024)(128)(2,1)S(1)} %pad_maximum_fusion.1), channel_id=1, source_target_pairs={{32,0},{48,16},{64,32},{80,48},{96,64},{112,80},{128,96},{144,112}... | collective-permute-start | bytes 1179656 | tf_op jit(solution)/shard_map/ppermute | solution.py:22
  88.9 9.1 %collective-permute-start.6 = (bf16[98304]{0:T(1024)(128)(2,1)S(1)}, bf16[98304]{0:T(1024)(128)(2,1)S(1)}, u32[]{:S(2)}, u32[]{:S(2)}) collective-permute-start(bf16[98304]{0:T(1024)(128)(2,1)S(1)} %slice.464), channel_id=1, source_target_pairs={{32,0},{48,16},{64,32},{80,48},{96,64},{112,80},{128,96},{144,112}... | collective-permute-start | bytes 589832 | tf_op jit(solution)/shard_map/ppermute | solution.py:22
